TPU v7x, 512 devices: a whole 4x8x8 slice. The times are simulated.
512 devices in a mesh: expert: 64 (over y, z_hi, core), narrow: 8 (over z_lo, x).
Axes of the slice: x: 4, y: 8, z: 8 (z_hi: 4, z_lo: 2; z = z_hi * 2 + z_lo), core: 2. Of those that a mesh axis runs over, the one named last changes fastest.
Arguments:
- tokens: bfloat16 [3072, 4096], P('expert', 'narrow'), may hold values from -6 to 6
- route_ids: int32 [3072, 8], P('expert'), may hold values from 0 to 63, all different within a row; in each aligned block of 48 rows (0 to 47, 48 to 95, ...) at most 12 rows name the same one
- route_weight: bfloat16 [3072, 8], P('expert'), may hold values from 0.049804688 to 0.5
- partner: int32 [64], replicated, may hold values from 0 to 63, as said below
- old_place: int32 [64], replicated, may hold values from 0 to 63, each once
- gate_weight: bfloat16 [64, 768, 4096], P('expert', 'narrow'), may hold values from -0.09375 to 0.09375
- up_weight: bfloat16 [64, 768, 4096], P('expert', 'narrow'), may hold values from -0.09375 to 0.09375
- down_weight: bfloat16 [64, 768, 4096], P('expert', None, 'narrow'), may hold values from -0.21875 to 0.21875
Outputs:
- layer_out: bfloat16 [3072, 4096], P('expert', 'narrow')
- new_gate: bfloat16 [64, 768, 4096], P('expert', 'narrow')
- new_up: bfloat16 [64, 768, 4096], P('expert', 'narrow')
- new_down: bfloat16 [64, 768, 4096], P('expert', None, 'narrow')
Inputs may be any that keep to these rules, and one draw needn't show every extreme that they name: partner[partner[s]] == s for every slot; slots with partner[s] == s keep their weights; the number of pairs varies between draws from 1 to 32. `old_place`: a permutation of the experts. `route_ids`: each row names 8 different experts; among the 48 tokens of one index of expert, no expert is named by more than 12 tokens.
All inputs are finite; a program needn't handle non-finite values.
Results may differ from a plain program's by a relative error of at most 0.0058.
Values may be sent and summed in bfloat16 or wider, within the bound.
No kernel may reach another device: no remote copies, remote signals or barrier semaphores. Data moves between devices by JAX's collectives and lax.ppermute only.
A program may use at most 128 MiB of HBM per device.

v0:
```python
import jax
import jax.numpy as jnp
from jax import lax
from jax.sharding import PartitionSpec as P


def slot_layout(route_ids, route_weight, holder, groups):
    tokens_here, top_count = route_ids.shape
    capacity = 2 * tokens_here * top_count // groups
    slot_ids = jnp.arange(groups, dtype=jnp.int32)
    matches = (holder[None, None, :] == route_ids[:, :, None]).astype(jnp.int32)
    target = jnp.sum(matches * slot_ids[None, None, :], axis=2)
    onehot = matches.reshape(tokens_here * top_count, groups)
    running = jnp.cumsum(onehot, axis=0) - 1
    position = jnp.sum(onehot * running, axis=1).reshape(tokens_here, top_count)
    row_index = target * capacity + position
    buffer_rows = jnp.arange(groups * capacity, dtype=jnp.int32)
    row_hits = buffer_rows[:, None, None] == row_index[None, :, :]
    dispatch = jnp.sum(row_hits.astype(jnp.float32), axis=2).astype(jnp.bfloat16)
    token_hits = row_index[:, :, None] == buffer_rows[None, None, :]
    combine = jnp.sum(
        jnp.where(token_hits, route_weight[:, :, None], jnp.zeros((), jnp.bfloat16)), axis=1
    )
    return (dispatch, combine, capacity)


def contract_last(left, right):
    return lax.dot_general(
        left, right, (((1,), (1,)), ((), ())), preferred_element_type=jnp.float32
    )


def body(tokens, route_ids, route_weight, partner, old_place, gate_weight, up_weight, down_weight):
    groups = lax.axis_size("expert")
    gate_flat = gate_weight.reshape(groups, -1)
    up_flat = up_weight.reshape(groups, -1)
    down_flat = down_weight.reshape(groups, -1)
    spread = (
        lax.all_to_all(gate_flat, "expert", split_axis=0, concat_axis=0, tiled=True),
        lax.all_to_all(up_flat, "expert", split_axis=0, concat_axis=0, tiled=True),
        lax.all_to_all(down_flat, "expert", split_axis=0, concat_axis=0, tiled=True),
    )
    gate_order = jnp.take(spread[0], partner, axis=0)
    up_order = jnp.take(spread[1], partner, axis=0)
    down_order = jnp.take(spread[2], partner, axis=0)
    arrived = (
        lax.all_to_all(gate_order, "expert", split_axis=0, concat_axis=0, tiled=True),
        lax.all_to_all(up_order, "expert", split_axis=0, concat_axis=0, tiled=True),
        lax.all_to_all(down_order, "expert", split_axis=0, concat_axis=0, tiled=True),
    )
    new_gate = arrived[0].reshape(gate_weight.shape)
    new_up = arrived[1].reshape(up_weight.shape)
    new_down = arrived[2].reshape(down_weight.shape)
    holder = jnp.take(old_place, partner)
    gate_block = new_gate[0]
    up_block = new_up[0]
    down_block = new_down[0]
    dispatch, combine, capacity = slot_layout(route_ids, route_weight, holder, groups)
    full_tokens = lax.all_gather(tokens, "narrow", axis=1, tiled=True)
    outgoing = jnp.dot(dispatch, full_tokens, preferred_element_type=jnp.float32).astype(
        jnp.bfloat16
    )
    arrived_rows = lax.all_to_all(
        outgoing.reshape(groups, capacity, -1), "expert", split_axis=0, concat_axis=0, tiled=True
    )
    flat_rows = arrived_rows.reshape(-1, arrived_rows.shape[2])
    gate_sum = contract_last(flat_rows, gate_block)
    up_sum = contract_last(flat_rows, up_block)
    hidden = (jax.nn.silu(gate_sum) * up_sum).astype(jnp.bfloat16)
    produced = (
        jnp.dot(
            lax.all_gather(hidden, "narrow", axis=1, tiled=True),
            down_block,
            preferred_element_type=jnp.float32,
        )
        .astype(jnp.bfloat16)
        .reshape(arrived_rows.shape[0], arrived_rows.shape[1], -1)
    )
    returned = lax.all_to_all(produced, "expert", split_axis=0, concat_axis=0, tiled=True)
    layer_out = jnp.dot(
        combine, returned.reshape(-1, returned.shape[2]), preferred_element_type=jnp.float32
    ).astype(jnp.bfloat16)
    return (layer_out, new_gate, new_up, new_down)


def solution(mesh):
    return jax.shard_map(
        body,
        mesh=mesh,
        in_specs=(
            P("expert", "narrow"),
            P("expert", None),
            P("expert", None),
            P(),
            P(),
            P("expert", "narrow", None),
            P("expert", "narrow", None),
            P("expert", None, "narrow"),
        ),
        out_specs=(
            P("expert", "narrow"),
            P("expert", "narrow", None),
            P("expert", "narrow", None),
            P("expert", None, "narrow"),
        ),
        check_vma=False,
    )
```

profile of v0, /device:TPU:80, one launch (start us, length us, event | category | flops | bytes accessed | tf_op | source)
XLA Modules:
  0.0 634.3 jit_solution(16042910142443403601)
XLA Ops:
  7.2 4.7 all_to_all.67
  12.4 5.5 reduce.9
  19.4 16.0 %all-to-all-start.5 = ((bf16[64,2,3072]{2,1,0:T(2,128)(2,1)}), bf16[64,2,3072]{2,1,0:T(2,128)(2,1)S(1)}, u32[]{:S(2)}, u32[]{:S(2)}) async-start(bf16[64,2,3072]{2,1,0:T(2,128)(2,1)} %reshape.175), calls=%async_computation.5 | async-start | bytes 1572864 | tf_op jit(solution)/shard_map/all_to_all | solution.py:41
  36.7 5.5 reduce.10
  43.6 17.1 %all-to-all-done.5 = bf16[64,2,3072]{2,1,0:T(2,128)(2,1)S(1)} async-done(((bf16[64,2,3072]{2,1,0:T(2,128)(2,1)}), bf16[64,2,3072]{2,1,0:T(2,128)(2,1)S(1)}, u32[]{:S(2)}, u32[]{:S(2)}) %all-to-all-start.5) | async-done | bytes 786464 | tf_op jit(solution)/shard_map/all_to_all | solution.py:41
  60.7 6.1 all-to-all-start.1
  68.1 5.5 reduce.11
  75.1 16.9 %all-to-all-done.1 = bf16[64,2,3072]{2,1,0:T(2,128)(2,1)} async-done(((bf16[64,2,3072]{2,1,0:T(2,128)(2,1)}), bf16[64,2,3072]{2,1,0:T(2,128)(2,1)}, u32[]{:S(2)}, u32[]{:S(2)}) %all-to-all-start.1) | async-done | bytes 786464 | tf_op jit(solution)/shard_map/all_to_all | solution.py:39
  92.0 6.3 all-to-all-start.3
  101.3 4.9 reshape.172
  108.6 15.0 %all-to-all-done.3 = bf16[64,2,3072]{2,1,0:T(2,128)(2,1)} async-done(((bf16[64,2,3072]{2,1,0:T(2,128)(2,1)}), bf16[64,2,3072]{2,1,0:T(2,128)(2,1)}, u32[]{:S(2)}, u32[]{:S(2)}) %all-to-all-start.3) | async-done | bytes 786464 | tf_op jit(solution)/shard_map/all_to_all | solution.py:40
  123.6 4.9 reshape.168
  131.5 2.3 reduce.12
  135.2 5.5 all-to-all-start.4
  143.4 22.8 %all-to-all-done.4 = bf16[64,2,3072]{2,1,0:T(2,128)(2,1)S(1)} async-done(((bf16[64,2,3072]{2,1,0:T(2,128)(2,1)}), bf16[64,2,3072]{2,1,0:T(2,128)(2,1)S(1)}, u32[]{:S(2)}, u32[]{:S(2)}) %all-to-all-start.4) | async-done | bytes 786464 | tf_op jit(solution)/shard_map/all_to_all | solution.py:48
  166.3 5.5 all-to-all-start.2
  175.0 37.4 %all_gather.6 = bf16[48,4096]{1,0:T(8,128)(2,1)S(1)} all-gather(bf16[48,512]{1,0:T(8,128)(2,1)S(1)} %copy-done.10), channel_id=1, replica_groups=mesh['expert'=64,'narrow'=8] {'narrow'}, dimensions={1}, use_global_device_ids=true | all-gather | bytes 442368 | tf_op jit(solution)/shard_map/all_gather | solution.py:59
  212.3 4.5 convolution_convert_fusion
  216.8 9.7 %reshape.111 = bf16[64,12,4096]{2,1,0:T(8,128)(2,1)} reshape(bf16[768,4096]{1,0:T(8,128)(2,1)} %convolution_convert_fusion) | data formatting | bytes 12582912 | tf_op jit(solution)/shard_map/reshape | solution.py:64
  227.4 15.7 %all-to-all-start = ((bf16[64,12,4096]{2,1,0:T(8,128)(2,1)}), bf16[64,12,4096]{2,1,0:T(8,128)(2,1)}, u32[]{:S(2)}, u32[]{:S(2)}) async-start(bf16[64,12,4096]{2,1,0:T(8,128)(2,1)} %reshape.111), calls=%async_computation | async-start | bytes 16777216 | tf_op jit(solution)/shard_map/all_to_all | solution.py:63
  243.8 4.9 reduce.3
  250.8 4.9 reduce.2
  256.3 206.2 %all-to-all-done = bf16[64,12,4096]{2,1,0:T(8,128)(2,1)} async-done(((bf16[64,12,4096]{2,1,0:T(8,128)(2,1)}), bf16[64,12,4096]{2,1,0:T(8,128)(2,1)}, u32[]{:S(2)}, u32[]{:S(2)}) %all-to-all-start) | async-done | bytes 6291488 | tf_op jit(solution)/shard_map/all_to_all | solution.py:63
  462.5 10.0 %reshape.112 = bf16[768,4096]{1,0:T(8,128)(2,1)} reshape(bf16[64,12,4096]{2,1,0:T(8,128)(2,1)} %all-to-all-done) | data formatting | bytes 12582912 | tf_op jit(solution)/shard_map/reshape | solution.py:66
  472.5 5.0 fusion.6
  477.6 2.7 fusion.1
  482.1 54.6 %all_to_all.76 = bf16[64,2,3072]{2,1,0:T(2,128)(2,1)S(1)} all-to-all(bf16[64,2,3072]{2,1,0:T(2,128)(2,1)S(1)} %reshape.177), channel_id=1, replica_groups=mesh['expert'=64,'narrow'=8] {'expert'}, dimensions={0} | all-to-all | bytes 1572864 | tf_op jit(solution)/shard_map/all_to_all | solution.py:49
  538.7 5.8 reduce.4
  546.4 29.8 %all-gather.2.cloned.1.call-done = bf16[768,768]{0,1:T(8,128)(2,1)} async-done(((bf16[768,96]{0,1:T(8,128)(2,1)}), bf16[768,768]{0,1:T(8,128)(2,1)}) %all-gather.2.cloned.1.call-update) | async-done | bytes 1179664 | tf_op jit(solution)/shard_map/all_gather | solution.py:72
  576.2 2.3 convolution_convert_fusion.1
  579.7 15.6 %all-to-all-start.7 = ((bf16[64,12,512]{2,1,0:T(8,128)(2,1)}), bf16[64,12,512]{2,1,0:T(8,128)(2,1)S(1)}, u32[]{:S(2)}, u32[]{:S(2)}) async-start(bf16[64,12,512]{2,1,0:T(8,128)(2,1)} %reshape.113), calls=%async_computation.7 | async-start | bytes 2097152 | tf_op jit(solution)/shard_map/all_to_all | solution.py:79
  600.6 25.5 %all-to-all-done.7 = bf16[64,12,512]{2,1,0:T(8,128)(2,1)S(1)} async-done(((bf16[64,12,512]{2,1,0:T(8,128)(2,1)}), bf16[64,12,512]{2,1,0:T(8,128)(2,1)S(1)}, u32[]{:S(2)}, u32[]{:S(2)}) %all-to-all-start.7) | async-done | bytes 786464 | tf_op jit(solution)/shard_map/all_to_all | solution.py:79
  (80 shorter events, 40.3 us)
Async XLA Ops:
  7.2 91.2 %copy-start = (s32[64]{0:T(128)S(1)}, s32[64]{0:T(128)}, u32[]{:S(2)}) copy-start(s32[64]{0:T(128)} %param.14) | copy-start | bytes 772
  19.4 16.0 %copy-start.8 = (bf16[1,96,4096]{2,1,0:T(8,128)(2,1)S(1)}, bf16[1,96,4096]{2,1,0:T(8,128)(2,1)}, u32[]{:S(2)}) copy-start(bf16[1,96,4096]{2,1,0:T(8,128)(2,1)} %param.15) | copy-start | bytes 2359300
  19.4 41.3 %all-to-all-start.5 = ((bf16[64,2,3072]{2,1,0:T(2,128)(2,1)}), bf16[64,2,3072]{2,1,0:T(2,128)(2,1)S(1)}, u32[]{:S(2)}, u32[]{:S(2)}) async-start(bf16[64,2,3072]{2,1,0:T(2,128)(2,1)} %reshape.175), calls=%async_computation.5 | async-start | bytes 1572864 | tf_op jit(solution)/shard_map/all_to_all | solution.py:41
  43.6 23.2 %copy-start.9 = (bf16[1,96,4096]{2,1,0:T(8,128)(2,1)S(1)}, bf16[1,96,4096]{2,1,0:T(8,128)(2,1)}, u32[]{:S(2)}) copy-start(bf16[1,96,4096]{2,1,0:T(8,128)(2,1)} %param.16) | copy-start | bytes 2359300
  60.7 31.3 %all-to-all-start.1 = ((bf16[64,2,3072]{2,1,0:T(2,128)(2,1)}), bf16[64,2,3072]{2,1,0:T(2,128)(2,1)}, u32[]{:S(2)}, u32[]{:S(2)}) async-start(bf16[64,2,3072]{2,1,0:T(2,128)(2,1)} %reshape.171), calls=%async_computation.1 | async-start | bytes 1572864 | tf_op jit(solution)/shard_map/all_to_all | solution.py:39
  73.6 24.7 %copy-start.13 = (s32[64]{0:T(128)S(1)}, s32[64]{0:T(128)}, u32[]{:S(2)}) copy-start(s32[64]{0:T(128)} %param.13) | copy-start | bytes 772
  92.0 31.5 %all-to-all-start.3 = ((bf16[64,2,3072]{2,1,0:T(2,128)(2,1)}), bf16[64,2,3072]{2,1,0:T(2,128)(2,1)}, u32[]{:S(2)}, u32[]{:S(2)}) async-start(bf16[64,2,3072]{2,1,0:T(2,128)(2,1)} %reshape.167), calls=%async_computation.3 | async-start | bytes 1572864 | tf_op jit(solution)/shard_map/all_to_all | solution.py:40
  128.9 1.1 copy-start.3
  135.2 31.0 %all-to-all-start.4 = ((bf16[64,2,3072]{2,1,0:T(2,128)(2,1)}), bf16[64,2,3072]{2,1,0:T(2,128)(2,1)S(1)}, u32[]{:S(2)}, u32[]{:S(2)}) async-start(bf16[64,2,3072]{2,1,0:T(2,128)(2,1)} %reshape.169), calls=%async_computation.4 | async-start | bytes 1572864 | tf_op jit(solution)/shard_map/all_to_all | solution.py:48
  142.0 29.8 %copy-start.11 = (s32[48,8]{0,1:T(8,128)S(1)}, s32[48,8]{0,1:T(8,128)}, u32[]{:S(2)}) copy-start(s32[48,8]{0,1:T(8,128)} %param.11) | copy-start | bytes 4612
  143.4 31.5 %copy-start.10 = (bf16[48,512]{1,0:T(8,128)(2,1)S(1)}, bf16[48,512]{1,0:T(8,128)(2,1)}, u32[]{:S(2)}) copy-start(bf16[48,512]{1,0:T(8,128)(2,1)} %param.10) | copy-start | bytes 147460
  166.3 60.3 %all-to-all-start.2 = ((bf16[64,2,3072]{2,1,0:T(2,128)(2,1)}), bf16[64,2,3072]{2,1,0:T(2,128)(2,1)S(1)}, u32[]{:S(2)}, u32[]{:S(2)}) async-start(bf16[64,2,3072]{2,1,0:T(2,128)(2,1)} %reshape.173), calls=%async_computation.2 | async-start | bytes 1572864 | tf_op jit(solution)/shard_map/all_to_all | solution.py:47
  226.6 0.9 copy-start.5
  227.4 235.0 %all-to-all-start = ((bf16[64,12,4096]{2,1,0:T(8,128)(2,1)}), bf16[64,12,4096]{2,1,0:T(8,128)(2,1)}, u32[]{:S(2)}, u32[]{:S(2)}) async-start(bf16[64,12,4096]{2,1,0:T(8,128)(2,1)} %reshape.111), calls=%async_computation | async-start | bytes 16777216 | tf_op jit(solution)/shard_map/all_to_all | solution.py:63
  243.1 333.1 %all-gather.2.cloned.1.call-start = ((), (), s32[]{:S(2)}) async-start(), calls=%async_computation.8 | async-start | bytes 1327104 | tf_op jit(solution)/shard_map/all_gather | solution.py:72
  248.7 1.5 copy-start.6
  472.5 5.0 copy-start.2
  472.5 5.0 copy-start.7
  477.6 2.8 copy-start.4
  578.5 16.8 %copy-start.12 = (bf16[48,8]{0,1:T(8,128)(2,1)S(1)}, bf16[48,8]{0,1:T(8,128)(2,1)}, u32[]{:S(2)}) copy-start(bf16[48,8]{0,1:T(8,128)(2,1)} %param.12) | copy-start | bytes 2308
  579.7 46.5 %all-to-all-start.7 = ((bf16[64,12,512]{2,1,0:T(8,128)(2,1)}), bf16[64,12,512]{2,1,0:T(8,128)(2,1)S(1)}, u32[]{:S(2)}, u32[]{:S(2)}) async-start(bf16[64,12,512]{2,1,0:T(8,128)(2,1)} %reshape.113), calls=%async_computation.7 | async-start | bytes 2097152 | tf_op jit(solution)/shard_map/all_to_all | solution.py:79
  598.8 28.4 %copy-start.1 = (s32[64]{0:T(128)S(1)}, s32[64]{0:T(128)}, u32[]{:S(2)}) copy-start(s32[64]{0:T(128)} %param.14) | copy-start | bytes 772
Sparse Core Ops, SparseCore 0:
  480.5 95.6 all-gather.1
where the time goes:
time: 641 us; the launch traced here: 634 us
  waiting for transfers between devices  333 us (52%)
  blocking collectives  92 us (14%)
  starting transfers between devices  70.7 us (11%)
  local copies, waits for them, and re-layouts  66.9 us (10%)
  other arithmetic  41.2 us (6%)
  matrix products  15.4 us (2%)
  between operations  14.8 us (2%)
    all_to_all x1, waiting for transfers between devices, body(): lax.all_to_all(outgoing.reshape(groups, capacity, -1), 'expert', split_ax...  206 us
    all_to_all x1, blocking collectives, body(): lax.all_to_all(down_order, 'expert', split_axis=0, concat_axis=0, tiled=T...  54.6 us
    all_gather x1, blocking collectives, body(): full_tokens = lax.all_gather(tokens, 'narrow', axis=1, tiled=True)  37.4 us
    all_gather x1, waiting for transfers between devices, body(): lax.all_gather(hidden, 'narrow', axis=1, tiled=True)  29.8 us
    all_to_all x1, waiting for transfers between devices, body(): lax.all_to_all(produced, 'expert', split_axis=0, concat_axis=0, tiled=True)  25.5 us
    unnamed x45, local copies, waits for them, and re-layouts  24.1 us
    all_to_all x1, waiting for transfers between devices, body(): lax.all_to_all(up_order, 'expert', split_axis=0, concat_axis=0, tiled=True)  22.8 us
    all_to_all x1, waiting for transfers between devices, body(): lax.all_to_all(down_flat, 'expert', split_axis=0, concat_axis=0, tiled=True)  17.1 us
  transfers between devices with their start and end apart: 8, of which 7 were waited for; matrix products, arithmetic and copies ran while one was open for 12% of the time, Pallas kernels for 0%

commit v1 on v0

--- a/solution.py
+++ b/solution.py
@@ -2,6 +2,8 @@
 import jax.numpy as jnp
 from jax import lax
 from jax.sharding import PartitionSpec as P
+
+LANES = 128
 
 
 def slot_layout(route_ids, route_weight, holder, groups):
@@ -30,40 +32,59 @@
     )
 
 
+def pack_weights(gate, up, down, groups):
+    rows, width = gate.shape
+    depth, narrow_width = down.shape
+    gate_c = gate.reshape(rows, width // LANES, LANES).transpose(1, 0, 2)
+    up_c = up.reshape(rows, width // LANES, LANES).transpose(1, 0, 2)
+    down_c = (
+        down.reshape(depth // rows, rows, narrow_width // LANES, LANES)
+        .transpose(0, 2, 1, 3)
+        .reshape(-1, rows, LANES)
+    )
+    stacked = jnp.concatenate([gate_c, up_c, down_c], axis=0)
+    return stacked.reshape(groups, -1, LANES)
+
+
+def unpack_weights(packed, gate_shape, down_shape):
+    rows, width = gate_shape
+    depth, narrow_width = down_shape
+    chunks = packed.reshape(-1, rows, LANES)
+    n_gate = width // LANES
+    gate = chunks[:n_gate].transpose(1, 0, 2).reshape(rows, width)
+    up = chunks[n_gate : 2 * n_gate].transpose(1, 0, 2).reshape(rows, width)
+    down = (
+        chunks[2 * n_gate :]
+        .reshape(depth // rows, narrow_width // LANES, rows, LANES)
+        .transpose(0, 2, 1, 3)
+        .reshape(depth, narrow_width)
+    )
+    return gate, up, down
+
+
+def exchange(gate, up, down, partner, groups):
+    packed = pack_weights(gate, up, down, groups)
+    spread = lax.all_to_all(packed, "expert", split_axis=0, concat_axis=0, tiled=True)
+    ordered = jnp.take(spread, partner, axis=0)
+    arrived = lax.all_to_all(ordered, "expert", split_axis=0, concat_axis=0, tiled=True)
+    return unpack_weights(arrived, gate.shape, down.shape)
+
+
 def body(tokens, route_ids, route_weight, partner, old_place, gate_weight, up_weight, down_weight):
     groups = lax.axis_size("expert")
-    gate_flat = gate_weight.reshape(groups, -1)
-    up_flat = up_weight.reshape(groups, -1)
-    down_flat = down_weight.reshape(groups, -1)
-    spread = (
-        lax.all_to_all(gate_flat, "expert", split_axis=0, concat_axis=0, tiled=True),
-        lax.all_to_all(up_flat, "expert", split_axis=0, concat_axis=0, tiled=True),
-        lax.all_to_all(down_flat, "expert", split_axis=0, concat_axis=0, tiled=True),
-    )
-    gate_order = jnp.take(spread[0], partner, axis=0)
-    up_order = jnp.take(spread[1], partner, axis=0)
-    down_order = jnp.take(spread[2], partner, axis=0)
-    arrived = (
-        lax.all_to_all(gate_order, "expert", split_axis=0, concat_axis=0, tiled=True),
-        lax.all_to_all(up_order, "expert", split_axis=0, concat_axis=0, tiled=True),
-        lax.all_to_all(down_order, "expert", split_axis=0, concat_axis=0, tiled=True),
-    )
-    new_gate = arrived[0].reshape(gate_weight.shape)
-    new_up = arrived[1].reshape(up_weight.shape)
-    new_down = arrived[2].reshape(down_weight.shape)
-    holder = jnp.take(old_place, partner)
-    gate_block = new_gate[0]
-    up_block = new_up[0]
-    down_block = new_down[0]
-    dispatch, combine, capacity = slot_layout(route_ids, route_weight, holder, groups)
-    full_tokens = lax.all_gather(tokens, "narrow", axis=1, tiled=True)
-    outgoing = jnp.dot(dispatch, full_tokens, preferred_element_type=jnp.float32).astype(
-        jnp.bfloat16
-    )
+    gate_block = gate_weight[0]
+    up_block = up_weight[0]
+    down_block = down_weight[0]
+
+    new_gate, new_up, new_down = exchange(gate_block, up_block, down_block, partner, groups)
+
+    dispatch, combine, capacity = slot_layout(route_ids, route_weight, old_place, groups)
+    outgoing = jnp.dot(dispatch, tokens, preferred_element_type=jnp.float32).astype(jnp.bfloat16)
     arrived_rows = lax.all_to_all(
         outgoing.reshape(groups, capacity, -1), "expert", split_axis=0, concat_axis=0, tiled=True
     )
-    flat_rows = arrived_rows.reshape(-1, arrived_rows.shape[2])
+    slice_rows = arrived_rows.reshape(-1, arrived_rows.shape[2])
+    flat_rows = lax.all_gather(slice_rows, "narrow", axis=1, tiled=True)
     gate_sum = contract_last(flat_rows, gate_block)
     up_sum = contract_last(flat_rows, up_block)
     hidden = (jax.nn.silu(gate_sum) * up_sum).astype(jnp.bfloat16)
@@ -74,13 +95,18 @@
             preferred_element_type=jnp.float32,
         )
         .astype(jnp.bfloat16)
-        .reshape(arrived_rows.shape[0], arrived_rows.shape[1], -1)
+        .reshape(groups, capacity, -1)
     )
     returned = lax.all_to_all(produced, "expert", split_axis=0, concat_axis=0, tiled=True)
     layer_out = jnp.dot(
         combine, returned.reshape(-1, returned.shape[2]), preferred_element_type=jnp.float32
     ).astype(jnp.bfloat16)
-    return (layer_out, new_gate, new_up, new_down)
+    return (
+        layer_out,
+        new_gate.reshape(gate_weight.shape),
+        new_up.reshape(up_weight.shape),
+        new_down.reshape(down_weight.shape),
+    )
 
 
 def solution(mesh):

time: 641 us -> 347 us (0.54)
  the two profiles are of different devices: /device:TPU:80 before, /device:TPU:16 now
where the time goes in v1:
time: 347 us
  waiting for transfers between devices  216 us (62%)
  blocking collectives  47.1 us (14%)
  starting transfers between devices  30.2 us (9%)
  local copies, waits for them, and re-layouts  18.2 us (5%)
  between operations  14.3 us (4%)
  matrix products  11.3 us (3%)
  other arithmetic  9.22 us (3%)
    all_gather x1, waiting for transfers between devices, body(): flat_rows = lax.all_gather(slice_rows, 'narrow', axis=1, tiled=True)  86.6 us
    all_to_all x1, waiting for transfers between devices, exchange(): lax.all_to_all(packed, 'expert', split_axis=0, concat_axis=0, tiled=True)  58.9 us
    all_gather x1, waiting for transfers between devices, body(): lax.all_gather(hidden, 'narrow', axis=1, tiled=True)  47.9 us
    all_to_all x1, blocking collectives, body(): lax.all_to_all(outgoing.reshape(groups, capacity, -1), 'expert', split_ax...  47.1 us
    all_to_all x1, waiting for transfers between devices, body(): lax.all_to_all(produced, 'expert', split_axis=0, concat_axis=0, tiled=True)  23 us
    all_to_all x1, starting transfers between devices, body(): lax.all_to_all(produced, 'expert', split_axis=0, concat_axis=0, tiled=True)  12.5 us
    all_to_all x1, starting transfers between devices, exchange(): lax.all_to_all(ordered, 'expert', split_axis=0, concat_axis=0, tiled=True)  11.6 us
    dot_general x2, matrix products, contract_last(): lax.dot_general(left, right, (((1,), (1,)), ((), ())), preferred_element_...  7.73 us
  transfers between devices with their start and end apart: 5, of which 4 were waited for; matrix products, arithmetic and copies ran while one was open for 9% of the time, Pallas kernels for 0%

profile of v1, /device:TPU:16, one launch (start us, length us, event | category | flops | bytes accessed | tf_op | source)
XLA Modules:
  0.0 346.8 jit_solution(9973418779246863607)
XLA Ops:
  7.2 0.8 copy.30
  8.2 1.6 select_reduce_fusion
  9.8 0.7 compare_convert_fusion
  10.5 0.9 reduce-window.6
  11.7 0.8 fusion.8
  12.6 0.4 convert_reduce_fusion
  13.6 47.1 %all_to_all.20 = bf16[64,12,512]{2,1,0:T(8,128)(2,1)S(1)} all-to-all(bf16[64,12,512]{2,1,0:T(8,128)(2,1)S(1)} %reshape.82), channel_id=1, replica_groups=mesh['expert'=64,'narrow'=8] {'expert'}, dimensions={0} | all-to-all | bytes 1572864 | tf_op jit(solution)/shard_map/all_to_all | solution.py:83
  60.7 1.1 reshape.83
  61.8 1.8 reshape_squeeze.11
  64.3 0.5 copy-done.5
  65.1 2.3 copy.37
  67.4 5.9 %all-to-all-start.2 = ((bf16[64,144,128]{2,1,0:T(8,128)(2,1)}), bf16[64,144,128]{2,1,0:T(8,128)(2,1)S(1)}, u32[]{:S(2)}, u32[]{:S(2)}) async-start(bf16[64,144,128]{2,1,0:T(8,128)(2,1)} %bitcast.54), calls=%async_computation.2 | async-start | bytes 4718592 | tf_op jit(solution)/shard_map/all_to_all | solution.py:67
  73.4 58.9 %all-to-all-done.2 = bf16[64,144,128]{2,1,0:T(8,128)(2,1)S(1)} async-done(((bf16[64,144,128]{2,1,0:T(8,128)(2,1)}), bf16[64,144,128]{2,1,0:T(8,128)(2,1)S(1)}, u32[]{:S(2)}, u32[]{:S(2)}) %all-to-all-start.2) | async-done | bytes 2359328 | tf_op jit(solution)/shard_map/all_to_all | solution.py:67
  132.3 2.3 gather_fusion
  134.6 3.4 broadcast_select_fusion
  138.0 11.6 %all-to-all-start.3 = ((bf16[64,144,128]{2,1,0:T(8,128)(2,1)}), bf16[64,144,128]{2,1,0:T(8,128)(2,1)S(1)}, u32[]{:S(2)}, u32[]{:S(2)}) async-start(bf16[64,144,128]{2,1,0:T(8,128)(2,1)} %broadcast_select_fusion), calls=%async_computation.3 | async-start | bytes 4718592 | tf_op jit(solution)/shard_map/all_to_all | solution.py:69
  149.8 86.6 %all-gather.3.cloned.1.call-done = bf16[768,4096]{1,0:T(8,128)(2,1)} async-done(((bf16[768,512]{1,0:T(8,128)(2,1)}), bf16[768,4096]{1,0:T(8,128)(2,1)}) %all-gather.3.cloned.1.call-update) | async-done | bytes 6291472 | tf_op jit(solution)/shard_map/all_gather | solution.py:87
  236.4 5.0 %fusion.4 = f32[768,96]{0,1:T(8,128)S(1)} fusion(bf16[768,4096]{1,0:T(8,128)(2,1)} %all-gather.3.cloned.1.call-done, bf16[1,96,4096]{2,1,0:T(8,128)(2,1)S(1)} %copy-done.2), kind=kOutput, calls=%fused_computation.16 | convolution fusion | flops 603979776 | bytes 7372800 | tf_op jit(solution)/shard_map/dot_general | solution.py:30
  241.4 2.7 fusion.1
  244.2 47.9 %all-gather.5.cloned.1.call-done = bf16[768,768]{0,1:T(8,128)(2,1)} async-done(((bf16[768,96]{0,1:T(8,128)(2,1)}), bf16[768,768]{0,1:T(8,128)(2,1)}) %all-gather.5.cloned.1.call-update) | async-done | bytes 1179664 | tf_op jit(solution)/shard_map/all_gather | solution.py:93
  292.1 2.3 convolution_convert_fusion
  294.4 1.1 reshape.84
  295.5 12.5 %all-to-all-start.1 = ((bf16[64,12,512]{2,1,0:T(8,128)(2,1)}), bf16[64,12,512]{2,1,0:T(8,128)(2,1)S(1)}, u32[]{:S(2)}, u32[]{:S(2)}) async-start(bf16[64,12,512]{2,1,0:T(8,128)(2,1)} %reshape.84), calls=%async_computation.1 | async-start | bytes 2097152 | tf_op jit(solution)/shard_map/all_to_all | solution.py:100
  308.0 0.7 copy.34
  308.7 1.2 fusion.6
  309.9 1.3 fusion.10
  311.5 1.2 reshape_reshape.10
  312.8 0.4 copy.40
  313.2 1.2 reshape_reshape.11
  314.7 1.2 reshape_reshape.9
  315.9 23.0 %all-to-all-done.1 = bf16[64,12,512]{2,1,0:T(8,128)(2,1)S(1)} async-done(((bf16[64,12,512]{2,1,0:T(8,128)(2,1)}), bf16[64,12,512]{2,1,0:T(8,128)(2,1)S(1)}, u32[]{:S(2)}, u32[]{:S(2)}) %all-to-all-start.1) | async-done | bytes 786464 | tf_op jit(solution)/shard_map/all_to_all | solution.py:100
  339.1 0.9 convolution_convert_fusion.2
  (41 shorter events, 3.1 us)
Async XLA Ops:
  7.2 5.8 %copy-start = (bf16[48,512]{1,0:T(8,128)(2,1)S(1)}, bf16[48,512]{1,0:T(8,128)(2,1)}, u32[]{:S(2)}) copy-start(bf16[48,512]{1,0:T(8,128)(2,1)} %param.8) | copy-start | bytes 147460
  7.2 229.2 %all-gather.3.cloned.1.call-start = ((), (), s32[]{:S(2)}) async-start(), calls=%async_computation.4 | async-start | bytes 7077888 | tf_op jit(solution)/shard_map/all_gather | solution.py:87
  61.8 2.3 copy-start.2
  63.6 1.1 copy-start.5
  67.4 5.9 %copy-start.8 = (s32[64]{0:T(128)S(1)}, s32[64]{0:T(128)}, u32[]{:S(2)}) copy-start(s32[64]{0:T(128)} %param.11) | copy-start | bytes 772
  67.4 64.9 %all-to-all-start.2 = ((bf16[64,144,128]{2,1,0:T(8,128)(2,1)}), bf16[64,144,128]{2,1,0:T(8,128)(2,1)S(1)}, u32[]{:S(2)}, u32[]{:S(2)}) async-start(bf16[64,144,128]{2,1,0:T(8,128)(2,1)} %bitcast.54), calls=%async_computation.2 | async-start | bytes 4718592 | tf_op jit(solution)/shard_map/all_to_all | solution.py:67
  138.0 157.5 %all-to-all-start.3 = ((bf16[64,144,128]{2,1,0:T(8,128)(2,1)}), bf16[64,144,128]{2,1,0:T(8,128)(2,1)S(1)}, u32[]{:S(2)}, u32[]{:S(2)}) async-start(bf16[64,144,128]{2,1,0:T(8,128)(2,1)} %broadcast_select_fusion), calls=%async_computation.3 | async-start | bytes 4718592 | tf_op jit(solution)/shard_map/all_to_all | solution.py:69
  149.6 142.5 %all-gather.5.cloned.1.call-start = ((), (), s32[]{:S(2)}) async-start(), calls=%async_computation.5 | async-start | bytes 1327104 | tf_op jit(solution)/shard_map/all_gather | solution.py:93
  236.4 5.0 %copy-start.1 = (bf16[768,4096]{1,0:T(8,128)(2,1)S(1)}, bf16[768,4096]{1,0:T(8,128)(2,1)}, u32[]{:S(2)}) copy-start(bf16[768,4096]{1,0:T(8,128)(2,1)} %all-gather.3.cloned.1.call-done) | copy-start | bytes 18874372
  236.4 5.0 %copy-start.6 = (bf16[1,96,4096]{2,1,0:T(8,128)(2,1)S(1)}, bf16[1,96,4096]{2,1,0:T(8,128)(2,1)}, u32[]{:S(2)}) copy-start(bf16[1,96,4096]{2,1,0:T(8,128)(2,1)} %param.14) | copy-start | bytes 2359300
  294.4 13.6 %copy-start.7 = (bf16[48,8]{0,1:T(8,128)(2,1)S(1)}, bf16[48,8]{0,1:T(8,128)(2,1)}, u32[]{:S(2)}) copy-start(bf16[48,8]{0,1:T(8,128)(2,1)} %param.10) | copy-start | bytes 2308
  295.5 43.3 %all-to-all-start.1 = ((bf16[64,12,512]{2,1,0:T(8,128)(2,1)}), bf16[64,12,512]{2,1,0:T(8,128)(2,1)S(1)}, u32[]{:S(2)}, u32[]{:S(2)}) async-start(bf16[64,12,512]{2,1,0:T(8,128)(2,1)} %reshape.84), calls=%async_computation.1 | async-start | bytes 2097152 | tf_op jit(solution)/shard_map/all_to_all | solution.py:100
  311.2 1.5 copy-start.4
  311.5 2.8 copy-start.3
Sparse Core Ops, SparseCore 0:
  61.9 174.4 all-gather.2
  244.3 47.7 all-gather.4

commit v2 on v1

--- a/solution.py
+++ b/solution.py
@@ -1,7 +1,7 @@
 import jax
 import jax.numpy as jnp
 from jax import lax
-from jax.sharding import PartitionSpec as P
+from jax.sharding import Mesh, PartitionSpec as P
 
 LANES = 128
 
@@ -72,11 +72,24 @@
 
 def body(tokens, route_ids, route_weight, partner, old_place, gate_weight, up_weight, down_weight):
     groups = lax.axis_size("expert")
+    half = lax.axis_index("zlo")
     gate_block = gate_weight[0]
     up_block = up_weight[0]
     down_block = down_weight[0]
 
     new_gate, new_up, new_down = exchange(gate_block, up_block, down_block, partner, groups)
+
+    rows, width = gate_block.shape
+    pair = [(0, 1), (1, 0)]
+    gate_halves = gate_block.reshape(rows, 2, width // 2)
+    up_halves = up_block.reshape(rows, 2, width // 2)
+    keep = jnp.concatenate(
+        [jnp.take(gate_halves, half, axis=1), jnp.take(up_halves, half, axis=1)], axis=0
+    )
+    give = jnp.concatenate(
+        [jnp.take(gate_halves, 1 - half, axis=1), jnp.take(up_halves, 1 - half, axis=1)], axis=0
+    )
+    taken = lax.ppermute(give, "zlo", pair)
 
     dispatch, combine, capacity = slot_layout(route_ids, route_weight, old_place, groups)
     outgoing = jnp.dot(dispatch, tokens, preferred_element_type=jnp.float32).astype(jnp.bfloat16)
@@ -84,13 +97,17 @@
         outgoing.reshape(groups, capacity, -1), "expert", split_axis=0, concat_axis=0, tiled=True
     )
     slice_rows = arrived_rows.reshape(-1, arrived_rows.shape[2])
-    flat_rows = lax.all_gather(slice_rows, "narrow", axis=1, tiled=True)
-    gate_sum = contract_last(flat_rows, gate_block)
-    up_sum = contract_last(flat_rows, up_block)
+    half_rows = lax.all_gather(slice_rows, "x", axis=1, tiled=True)
+    own_part = contract_last(half_rows, keep)
+    other_part = contract_last(half_rows, taken)
+    back = lax.ppermute(other_part, "zlo", pair)
+    sums = own_part + back
+    gate_sum = sums[:, :rows]
+    up_sum = sums[:, rows:]
     hidden = (jax.nn.silu(gate_sum) * up_sum).astype(jnp.bfloat16)
     produced = (
         jnp.dot(
-            lax.all_gather(hidden, "narrow", axis=1, tiled=True),
+            lax.all_gather(hidden, ("zlo", "x"), axis=1, tiled=True),
             down_block,
             preferred_element_type=jnp.float32,
         )
@@ -110,24 +127,29 @@
 
 
 def solution(mesh):
+    expert_size, narrow_size = mesh.devices.shape
+    split_mesh = Mesh(
+        mesh.devices.reshape(expert_size, 2, narrow_size // 2), ("expert", "zlo", "x")
+    )
+    narrow = ("zlo", "x")
     return jax.shard_map(
         body,
-        mesh=mesh,
+        mesh=split_mesh,
         in_specs=(
-            P("expert", "narrow"),
+            P("expert", narrow),
             P("expert", None),
             P("expert", None),
             P(),
             P(),
-            P("expert", "narrow", None),
-            P("expert", "narrow", None),
-            P("expert", None, "narrow"),
+            P("expert", narrow, None),
+            P("expert", narrow, None),
+            P("expert", None, narrow),
         ),
         out_specs=(
-            P("expert", "narrow"),
-            P("expert", "narrow", None),
-            P("expert", "narrow", None),
-            P("expert", None, "narrow"),
+            P("expert", narrow),
+            P("expert", narrow, None),
+            P("expert", narrow, None),
+            P("expert", None, narrow),
         ),
         check_vma=False,
     )

time: 347 us -> 339 us (0.977)
  blocking collectives: 47.1 us -> 0 us
  starting transfers between devices: 30.2 us -> 54.5 us
  local copies, waits for them, and re-layouts: 18.2 us -> 26 us
  other arithmetic: 9.22 us -> 16.4 us
    all_gather x2, waiting for transfers between devices: 134 us -> 47.8 us  [the longest x1 47.8 us: body(): lax.all_gather(hidden, ('zlo', 'x'), axis=1, tiled=True)]
    ppermute x0 -> x2, waiting for transfers between devices: none -> 72.4 us  [the longest x1 60.6 us: body(): taken = lax.ppermute(give, 'zlo', pair)]
    all_to_all x1 -> x0, blocking collectives: 47.1 us -> none  [body(): lax.all_to_all(outgoing.reshape(groups, capacity, -1), 'expert', split_ax...]
    all_to_all x0 -> x1, waiting for transfers between devices: none -> 25.2 us  [body(): lax.all_to_all(outgoing.reshape(groups, capacity, -1), 'expert', split_ax...]
    all_to_all x0 -> x1, starting transfers between devices: none -> 16.5 us  [body(): lax.all_to_all(outgoing.reshape(groups, capacity, -1), 'expert', split_ax...]
    all_to_all x1, waiting for transfers between devices: 58.9 us -> 50.8 us  [exchange(): lax.all_to_all(packed, 'expert', split_axis=0, concat_axis=0, tiled=True)]
    ppermute x0 -> x2, starting transfers between devices: none -> 6.56 us  [the longest x1 4.5 us: body(): back = lax.ppermute(other_part, 'zlo', pair)]
    select_n x0 -> x1, other arithmetic: none -> 6.24 us  [body(): jnp.take(up_halves, 1 - half, axis=1)]
  transfers between devices with their start and end apart: 5 -> 8, of which waited for: 4 -> 6; matrix products, arithmetic and copies ran while one was open for 9% -> 12% of each run, Pallas kernels for 0% -> 0%
where the time goes in v2:
time: 339 us
  waiting for transfers between devices  219 us (65%)
  starting transfers between devices  54.5 us (16%)
  local copies, waits for them, and re-layouts  26 us (8%)
  other arithmetic  16.4 us (5%)
  between operations  14.4 us (4%)
  matrix products  8.13 us (2%)
    ppermute x1, waiting for transfers between devices, body(): taken = lax.ppermute(give, 'zlo', pair)  60.6 us
    all_to_all x1, waiting for transfers between devices, exchange(): lax.all_to_all(packed, 'expert', split_axis=0, concat_axis=0, tiled=True)  50.8 us
    all_gather x1, waiting for transfers between devices, body(): lax.all_gather(hidden, ('zlo', 'x'), axis=1, tiled=True)  47.8 us
    all_to_all x1, waiting for transfers between devices, body(): lax.all_to_all(outgoing.reshape(groups, capacity, -1), 'expert', split_ax...  25.2 us
    all_to_all x1, waiting for transfers between devices, body(): lax.all_to_all(produced, 'expert', split_axis=0, concat_axis=0, tiled=True)  23 us
    all_to_all x1, starting transfers between devices, body(): lax.all_to_all(outgoing.reshape(groups, capacity, -1), 'expert', split_ax...  16.5 us
    all_to_all x1, starting transfers between devices, exchange(): lax.all_to_all(ordered, 'expert', split_axis=0, concat_axis=0, tiled=True)  13 us
    all_to_all x1, starting transfers between devices, body(): lax.all_to_all(produced, 'expert', split_axis=0, concat_axis=0, tiled=True)  12.5 us
  transfers between devices with their start and end apart: 8, of which 6 were waited for; matrix products, arithmetic and copies ran while one was open for 12% of the time, Pallas kernels for 0%

profile of v2, /device:TPU:16, one launch (start us, length us, event | category | flops | bytes accessed | tf_op | source)
XLA Modules:
  0.0 338.7 jit_solution(8235907400037643468)
XLA Ops:
  8.1 1.6 select_reduce_fusion
  13.4 1.1 reshape.83
  14.5 16.5 %all-to-all-start = ((bf16[64,12,512]{2,1,0:T(8,128)(2,1)}), bf16[64,12,512]{2,1,0:T(8,128)(2,1)S(1)}, u32[]{:S(2)}, u32[]{:S(2)}) async-start(bf16[64,12,512]{2,1,0:T(8,128)(2,1)} %reshape.83), calls=%async_computation | async-start | bytes 2097152 | tf_op jit(solution)/shard_map/all_to_all | solution.py:96
  31.0 1.1 reshape_squeeze.19
  32.1 1.3 copy.48
  34.3 2.4 copy.50
  36.7 25.2 %all-to-all-done = bf16[64,12,512]{2,1,0:T(8,128)(2,1)S(1)} async-done(((bf16[64,12,512]{2,1,0:T(8,128)(2,1)}), bf16[64,12,512]{2,1,0:T(8,128)(2,1)S(1)}, u32[]{:S(2)}, u32[]{:S(2)}) %all-to-all-start) | async-done | bytes 786464 | tf_op jit(solution)/shard_map/all_to_all | solution.py:96
  61.9 5.8 %all-to-all-start.2 = ((bf16[64,144,128]{2,1,0:T(8,128)(2,1)}), bf16[64,144,128]{2,1,0:T(8,128)(2,1)S(1)}, u32[]{:S(2)}, u32[]{:S(2)}) async-start(bf16[64,144,128]{2,1,0:T(8,128)(2,1)} %bitcast.6), calls=%async_computation.2 | async-start | bytes 4718592 | tf_op jit(solution)/shard_map/all_to_all | solution.py:67
  67.7 1.1 reshape.84
  68.8 2.6 reshape_squeeze.15
  71.3 3.3 reshape_squeeze.16
  74.6 50.8 %all-to-all-done.2 = bf16[64,144,128]{2,1,0:T(8,128)(2,1)S(1)} async-done(((bf16[64,144,128]{2,1,0:T(8,128)(2,1)}), bf16[64,144,128]{2,1,0:T(8,128)(2,1)S(1)}, u32[]{:S(2)}, u32[]{:S(2)}) %all-to-all-start.2) | async-done | bytes 2359328 | tf_op jit(solution)/shard_map/all_to_all | solution.py:67
  125.5 2.3 gather_fusion
  127.8 3.4 %broadcast_select_fusion = bf16[64,144,128]{2,1,0:T(8,128)(2,1)} fusion(bf16[64,144,128]{2,1,0:T(8,128)(2,1)} %gather_fusion, pred[64]{0:T(512)(128)(4,1)S(1)} %compare_and_fusion), kind=kLoop, calls=%fused_computation.2 | loop fusion | flops 1179648 | bytes 4718656 | tf_op jit(solution)/shard_map/jit(_take)/select_n | solution.py:68
  131.3 13.0 %all-to-all-start.3 = ((bf16[64,144,128]{2,1,0:T(8,128)(2,1)}), bf16[64,144,128]{2,1,0:T(8,128)(2,1)S(1)}, u32[]{:S(2)}, u32[]{:S(2)}) async-start(bf16[64,144,128]{2,1,0:T(8,128)(2,1)} %broadcast_select_fusion), calls=%async_computation.3 | async-start | bytes 4718592 | tf_op jit(solution)/shard_map/all_to_all | solution.py:69
  144.5 6.2 %broadcast_select_fusion.1 = (bf16[96,1,2048]{2,1,0:T(2,128)(2,1)S(1)}, bf16[96,1,2048]{2,1,0:T(2,128)(2,1)}, bf16[96,1,2048]{2,1,0:T(2,128)(2,1)}, bf16[96,1,2048]{2,1,0:T(2,128)(2,1)S(1)}) fusion(pred[]{:T(512)S(6)} %and.19, bf16[96,2,2048]{2,1,0:T(2,128)(2,1)} %reshape_squeeze.16, s32[]{:T(128)S(6)} %select_n.41, s32[]{:T(128)S(6)} %select_n.37, ...), kind=kLoop, calls=%fused_computation.3 | loop fusion | flops 786432 | bytes 3145738 | tf_op jit(solution)/shard_map/jit(_take)/select_n | solution.py:90
  151.3 2.1 collective-permute-start
  153.4 60.6 %collective-permute-done = bf16[192,2048]{1,0:T(8,128)(2,1)} collective-permute-done((bf16[192,2048]{1,0:T(8,128)(2,1)S(1)}, bf16[192,2048]{1,0:T(8,128)(2,1)}, u32[]{:S(2)}, u32[]{:S(2)}) %collective-permute-start) | collective-permute-done | bytes 786464 | tf_op jit(solution)/shard_map/ppermute | solution.py:92
  214.0 3.4 %fusion.13 = f32[768,192]{0,1:T(8,128)S(1)} fusion(bf16[768,2048]{1,0:T(8,128)(2,1)} %all-gather.3.cloned.1.call-done, bf16[192,2048]{1,0:T(8,128)(2,1)} %collective-permute-done), kind=kOutput, calls=%fused_computation.43 | convolution fusion | flops 603979776 | bytes 4521984 | tf_op jit(solution)/shard_map/dot_general | solution.py:30
  217.4 4.5 %collective-permute-start.1 = (f32[768,192]{0,1:T(8,128)S(1)}, f32[768,192]{0,1:T(8,128)S(1)}, u32[]{:S(2)}, u32[]{:S(2)}) collective-permute-start(f32[768,192]{0,1:T(8,128)S(1)} %fusion.13), channel_id=1, source_target_pairs={{0,4},{4,0},{1,5},{5,1},{2,6},{6,2},{3,7},{7,3},{8,12},{12,8},{9,1... | collective-permute-start | bytes 1769480 | tf_op jit(solution)/shard_map/ppermute | solution.py:103
  222.4 1.2 fusion.1
  223.6 11.7 %collective-permute-done.1 = f32[768,192]{0,1:T(8,128)S(1)} collective-permute-done((f32[768,192]{0,1:T(8,128)S(1)}, f32[768,192]{0,1:T(8,128)S(1)}, u32[]{:S(2)}, u32[]{:S(2)}) %collective-permute-start.1) | collective-permute-done | bytes 589856 | tf_op jit(solution)/shard_map/ppermute | solution.py:103
  236.2 47.8 %all-gather.5.cloned.1.call-done = bf16[768,768]{0,1:T(8,128)(2,1)} async-done(((bf16[768,96]{0,1:T(8,128)(2,1)}), bf16[768,768]{0,1:T(8,128)(2,1)}) %all-gather.5.cloned.1.call-update) | async-done | bytes 1179664 | tf_op jit(solution)/shard_map/all_gather | solution.py:110
  284.0 2.3 convolution_convert_fusion
  286.3 1.1 reshape.85
  287.4 12.5 %all-to-all-start.1 = ((bf16[64,12,512]{2,1,0:T(8,128)(2,1)}), bf16[64,12,512]{2,1,0:T(8,128)(2,1)S(1)}, u32[]{:S(2)}, u32[]{:S(2)}) async-start(bf16[64,12,512]{2,1,0:T(8,128)(2,1)} %reshape.85), calls=%async_computation.1 | async-start | bytes 2097152 | tf_op jit(solution)/shard_map/all_to_all | solution.py:117
  300.6 1.2 fusion.6
  301.8 1.3 fusion.12
  303.4 1.2 reshape_reshape.10
  305.1 1.2 reshape_reshape.11
  306.6 1.2 reshape_reshape.9
  307.8 23.0 %all-to-all-done.1 = bf16[64,12,512]{2,1,0:T(8,128)(2,1)S(1)} async-done(((bf16[64,12,512]{2,1,0:T(8,128)(2,1)}), bf16[64,12,512]{2,1,0:T(8,128)(2,1)S(1)}, u32[]{:S(2)}, u32[]{:S(2)}) %all-to-all-start.1) | async-done | bytes 786464 | tf_op jit(solution)/shard_map/all_to_all | solution.py:117
  (60 shorter events, 10.2 us)
Async XLA Ops:
  7.2 5.8 %copy-start = (bf16[48,512]{1,0:T(8,128)(2,1)S(1)}, bf16[48,512]{1,0:T(8,128)(2,1)}, u32[]{:S(2)}) copy-start(bf16[48,512]{1,0:T(8,128)(2,1)} %param.10) | copy-start | bytes 147460
  13.0 18.0 %copy-start.7 = (bf16[1,768,512]{2,1,0:T(8,128)(2,1)S(1)}, bf16[1,768,512]{2,1,0:T(8,128)(2,1)}, u32[]{:S(2)}) copy-start(bf16[1,768,512]{2,1,0:T(8,128)(2,1)} %param.17) | copy-start | bytes 2359300
  14.5 47.3 %all-to-all-start = ((bf16[64,12,512]{2,1,0:T(8,128)(2,1)}), bf16[64,12,512]{2,1,0:T(8,128)(2,1)S(1)}, u32[]{:S(2)}, u32[]{:S(2)}) async-start(bf16[64,12,512]{2,1,0:T(8,128)(2,1)} %reshape.83), calls=%async_computation | async-start | bytes 2097152 | tf_op jit(solution)/shard_map/all_to_all | solution.py:96
  31.0 2.7 copy-start.3
  32.1 1.8 copy-start.4
  61.9 63.6 %all-to-all-start.2 = ((bf16[64,144,128]{2,1,0:T(8,128)(2,1)}), bf16[64,144,128]{2,1,0:T(8,128)(2,1)S(1)}, u32[]{:S(2)}, u32[]{:S(2)}) async-start(bf16[64,144,128]{2,1,0:T(8,128)(2,1)} %bitcast.6), calls=%async_computation.2 | async-start | bytes 4718592 | tf_op jit(solution)/shard_map/all_to_all | solution.py:67
  67.6 146.3 %all-gather.3.cloned.1.call-start = ((), (), s32[]{:S(2)}) async-start(), calls=%async_computation.4 | async-start | bytes 3932160 | tf_op jit(solution)/shard_map/all_gather | solution.py:100
  68.7 5.9 %copy-start.10 = (s32[64]{0:T(128)S(1)}, s32[64]{0:T(128)}, u32[]{:S(2)}) copy-start(s32[64]{0:T(128)} %param.13) | copy-start | bytes 772
  131.3 156.2 %all-to-all-start.3 = ((bf16[64,144,128]{2,1,0:T(8,128)(2,1)}), bf16[64,144,128]{2,1,0:T(8,128)(2,1)S(1)}, u32[]{:S(2)}, u32[]{:S(2)}) async-start(bf16[64,144,128]{2,1,0:T(8,128)(2,1)} %broadcast_select_fusion), calls=%async_computation.3 | async-start | bytes 4718592 | tf_op jit(solution)/shard_map/all_to_all | solution.py:69
  144.3 139.7 %all-gather.5.cloned.1.call-start = ((), (), s32[]{:S(2)}) async-start(), calls=%async_computation.5 | async-start | bytes 1327104 | tf_op jit(solution)/shard_map/all_gather | solution.py:110
  151.3 70.9 %copy-start.5 = (bf16[96,1,2048]{2,1,0:T(2,128)(2,1)S(1)}, bf16[96,1,2048]{2,1,0:T(2,128)(2,1)}, u32[]{:S(2)}) copy-start(bf16[96,1,2048]{2,1,0:T(2,128)(2,1)} %get-tuple-element.23) | copy-start | bytes 1179652
  151.3 62.7 %collective-permute-start = (bf16[192,2048]{1,0:T(8,128)(2,1)S(1)}, bf16[192,2048]{1,0:T(8,128)(2,1)}, u32[]{:S(2)}, u32[]{:S(2)}) collective-permute-start(bf16[192,2048]{1,0:T(8,128)(2,1)S(1)} %pad_maximum_fusion.1), channel_id=1, source_target_pairs={{0,4},{4,0},{1,5},{5,1},{2,6},{6,2},{3,7},{7,3},{8,12},{12,8},{9,1... | collective-permute-start | bytes 2359304 | tf_op jit(solution)/shard_map/ppermute | solution.py:92
  214.0 7.9 %copy-start.6 = (bf16[96,1,2048]{2,1,0:T(2,128)(2,1)S(1)}, bf16[96,1,2048]{2,1,0:T(2,128)(2,1)}, u32[]{:S(2)}) copy-start(bf16[96,1,2048]{2,1,0:T(2,128)(2,1)} %get-tuple-element.22) | copy-start | bytes 1179652
  214.0 8.4 %copy-start.9 = (bf16[768,2048]{1,0:T(8,128)(2,1)S(1)}, bf16[768,2048]{1,0:T(8,128)(2,1)}, u32[]{:S(2)}) copy-start(bf16[768,2048]{1,0:T(8,128)(2,1)} %all-gather.3.cloned.1.call-done) | copy-start | bytes 9437188
  217.4 17.9 %collective-permute-start.1 = (f32[768,192]{0,1:T(8,128)S(1)}, f32[768,192]{0,1:T(8,128)S(1)}, u32[]{:S(2)}, u32[]{:S(2)}) collective-permute-start(f32[768,192]{0,1:T(8,128)S(1)} %fusion.13), channel_id=1, source_target_pairs={{0,4},{4,0},{1,5},{5,1},{2,6},{6,2},{3,7},{7,3},{8,12},{12,8},{9,1... | collective-permute-start | bytes 1769480 | tf_op jit(solution)/shard_map/ppermute | solution.py:103
  286.3 13.6 %copy-start.8 = (bf16[48,8]{0,1:T(8,128)(2,1)S(1)}, bf16[48,8]{0,1:T(8,128)(2,1)}, u32[]{:S(2)}) copy-start(bf16[48,8]{0,1:T(8,128)(2,1)} %param.12) | copy-start | bytes 2308
  287.4 43.3 %all-to-all-start.1 = ((bf16[64,12,512]{2,1,0:T(8,128)(2,1)}), bf16[64,12,512]{2,1,0:T(8,128)(2,1)S(1)}, u32[]{:S(2)}, u32[]{:S(2)}) async-start(bf16[64,12,512]{2,1,0:T(8,128)(2,1)} %reshape.85), calls=%async_computation.1 | async-start | bytes 2097152 | tf_op jit(solution)/shard_map/all_to_all | solution.py:117
  303.1 1.5 copy-start.2
  303.4 2.8 copy-start.1
Sparse Core Ops, SparseCore 0:
  71.2 45.5 all-gather.2
  236.3 47.6 all-gather.4

commit v3 on v2

--- a/solution.py
+++ b/solution.py
@@ -62,12 +62,15 @@
     return gate, up, down
 
 
-def exchange(gate, up, down, partner, groups):
+def spread_weights(gate, up, down, groups):
     packed = pack_weights(gate, up, down, groups)
-    spread = lax.all_to_all(packed, "expert", split_axis=0, concat_axis=0, tiled=True)
-    ordered = jnp.take(spread, partner, axis=0)
+    return lax.all_to_all(packed, "expert", split_axis=0, concat_axis=0, tiled=True)
+
+
+def finish_exchange(spread, partner, gate_shape, down_shape):
+    ordered = jnp.take(spread, partner, axis=0, mode="clip")
     arrived = lax.all_to_all(ordered, "expert", split_axis=0, concat_axis=0, tiled=True)
-    return unpack_weights(arrived, gate.shape, down.shape)
+    return unpack_weights(arrived, gate_shape, down_shape)
 
 
 def body(tokens, route_ids, route_weight, partner, old_place, gate_weight, up_weight, down_weight):
@@ -77,17 +80,25 @@
     up_block = up_weight[0]
     down_block = down_weight[0]
 
-    new_gate, new_up, new_down = exchange(gate_block, up_block, down_block, partner, groups)
+    spread = spread_weights(gate_block, up_block, down_block, groups)
 
     rows, width = gate_block.shape
     pair = [(0, 1), (1, 0)]
     gate_halves = gate_block.reshape(rows, 2, width // 2)
     up_halves = up_block.reshape(rows, 2, width // 2)
     keep = jnp.concatenate(
-        [jnp.take(gate_halves, half, axis=1), jnp.take(up_halves, half, axis=1)], axis=0
+        [
+            lax.dynamic_index_in_dim(gate_halves, half, axis=1, keepdims=False),
+            lax.dynamic_index_in_dim(up_halves, half, axis=1, keepdims=False),
+        ],
+        axis=0,
     )
     give = jnp.concatenate(
-        [jnp.take(gate_halves, 1 - half, axis=1), jnp.take(up_halves, 1 - half, axis=1)], axis=0
+        [
+            lax.dynamic_index_in_dim(gate_halves, 1 - half, axis=1, keepdims=False),
+            lax.dynamic_index_in_dim(up_halves, 1 - half, axis=1, keepdims=False),
+        ],
+        axis=0,
     )
     taken = lax.ppermute(give, "zlo", pair)
 
@@ -96,10 +107,13 @@
     arrived_rows = lax.all_to_all(
         outgoing.reshape(groups, capacity, -1), "expert", split_axis=0, concat_axis=0, tiled=True
     )
+    taken, arrived_rows = lax.optimization_barrier((taken, arrived_rows))
     slice_rows = arrived_rows.reshape(-1, arrived_rows.shape[2])
     half_rows = lax.all_gather(slice_rows, "x", axis=1, tiled=True)
     own_part = contract_last(half_rows, keep)
     other_part = contract_last(half_rows, taken)
+    spread, own_part, other_part = lax.optimization_barrier((spread, own_part, other_part))
+    new_gate, new_up, new_down = finish_exchange(spread, partner, gate_block.shape, down_block.shape)
     back = lax.ppermute(other_part, "zlo", pair)
     sums = own_part + back
     gate_sum = sums[:, :rows]

time: 339 us -> 339 us (level)
  the two profiles are of different devices: /device:TPU:16 before, /device:TPU:4 now
where the time goes in v3:
time: 339 us; the launch traced here: 338 us
  waiting for transfers between devices  224 us (66%)
  starting transfers between devices  53.2 us (16%)
  local copies, waits for them, and re-layouts  29.2 us (9%)
  between operations  14.4 us (4%)
  matrix products  10.1 us (3%)
  other arithmetic  6.69 us (2%)
    all_to_all x1, waiting for transfers between devices, finish_exchange(): lax.all_to_all(ordered, 'expert', split_axis=0, concat_axis=0, tiled=True)  58.1 us
    all_gather x1, waiting for transfers between devices, body(): lax.all_gather(hidden, ('zlo', 'x'), axis=1, tiled=True)  44.2 us
    ppermute x1, waiting for transfers between devices, body(): taken = lax.ppermute(give, 'zlo', pair)  30.8 us
    all_to_all x1, waiting for transfers between devices, body(): lax.all_to_all(produced, 'expert', split_axis=0, concat_axis=0, tiled=True)  27.7 us
    all_to_all x1, waiting for transfers between devices, spread_weights(): lax.all_to_all(packed, 'expert', split_axis=0, concat_axis=0, tiled=True)  26.3 us
    all_gather x1, waiting for transfers between devices, body(): half_rows = lax.all_gather(slice_rows, 'x', axis=1, tiled=True)  24.4 us
    all_to_all x1, starting transfers between devices, body(): lax.all_to_all(outgoing.reshape(groups, capacity, -1), 'expert', split_ax...  16.6 us
    all_to_all x1, starting transfers between devices, body(): lax.all_to_all(produced, 'expert', split_axis=0, concat_axis=0, tiled=True)  13.1 us
  transfers between devices with their start and end apart: 8, of which 7 were waited for; matrix products, arithmetic and copies ran while one was open for 8% of the time, Pallas kernels for 0%

profile of v3, /device:TPU:4, one launch (start us, length us, event | category | flops | bytes accessed | tf_op | source)
XLA Modules:
  0.0 337.9 jit_solution(6109345556324568363)
XLA Ops:
  8.1 1.6 select_reduce_fusion
  13.4 1.1 reshape.79
  14.5 16.6 %all-to-all-start.1 = ((bf16[64,12,512]{2,1,0:T(8,128)(2,1)}), bf16[64,12,512]{2,1,0:T(8,128)(2,1)S(1)}, u32[]{:S(2)}, u32[]{:S(2)}) async-start(bf16[64,12,512]{2,1,0:T(8,128)(2,1)} %reshape.79), calls=%async_computation.1 | async-start | bytes 2097152 | tf_op jit(solution)/shard_map/all_to_all | solution.py:107
  31.8 2.6 reshape_squeeze.19
  34.3 4.2 %constant_dynamic-slice_fusion = (bf16[96,1,2048]{2,1,0:T(2,128)(2,1)}, bf16[96,1,2048]{2,1,0:T(2,128)(2,1)S(1)}, bf16[96,1,2048]{2,1,0:T(2,128)(2,1)S(1)}, bf16[96,1,2048]{2,1,0:T(2,128)(2,1)}) fusion(bf16[96,2,2048]{2,1,0:T(2,128)(2,1)S(1)} %reshape_squeeze.18, s32[]{:T(128)S(6)} %select_n.15, s32[]{:T(128)S(6)} %select_n.14, ...), kind=kLoop, calls=%fused_computation.34 | loop fusion | bytes 3145736 | tf_op jit(solution)/shard_map/jit(dynamic_index_in_dim)/dynamic_slice | solution.py:91
  39.0 3.5 %collective-permute-start = (bf16[192,2048]{1,0:T(8,128)(2,1)S(1)}, bf16[192,2048]{1,0:T(8,128)(2,1)S(1)}, u32[]{:S(2)}, u32[]{:S(2)}) collective-permute-start(bf16[192,2048]{1,0:T(8,128)(2,1)S(1)} %pad_maximum_fusion.1), channel_id=1, source_target_pairs={{0,4},{4,0},{1,5},{5,1},{2,6},{6,2},{3,7},{7,3},{8,12},{12,8},{9,1... | collective-permute-start | bytes 2359304 | tf_op jit(solution)/shard_map/ppermute | solution.py:103
  42.6 30.8 %collective-permute-done = bf16[192,2048]{1,0:T(8,128)(2,1)S(1)} collective-permute-done((bf16[192,2048]{1,0:T(8,128)(2,1)S(1)}, bf16[192,2048]{1,0:T(8,128)(2,1)S(1)}, u32[]{:S(2)}, u32[]{:S(2)}) %collective-permute-start) | collective-permute-done | bytes 786464 | tf_op jit(solution)/shard_map/ppermute | solution.py:103
  73.4 1.1 reshape.80
  76.2 2.4 copy.37
  78.6 11.2 %all-to-all-start = ((bf16[64,144,128]{2,1,0:T(8,128)(2,1)}), bf16[64,144,128]{2,1,0:T(8,128)(2,1)S(1)}, u32[]{:S(2)}, u32[]{:S(2)}) async-start(bf16[64,144,128]{2,1,0:T(8,128)(2,1)} %bitcast.60), calls=%async_computation | async-start | bytes 4718592 | tf_op jit(solution)/shard_map/all_to_all | solution.py:67
  90.1 2.2 copy.53
  93.3 24.4 %all-gather.3.cloned.1.call-done = bf16[768,2048]{1,0:T(8,128)(2,1)} async-done(((bf16[768,512]{1,0:T(8,128)(2,1)}), bf16[768,2048]{1,0:T(8,128)(2,1)}) %all-gather.3.cloned.1.call-update) | async-done | bytes 3145744 | tf_op jit(solution)/shard_map/all_gather | solution.py:112
  117.7 3.4 %fusion.1 = f32[768,192]{0,1:T(8,128)S(1)} fusion(bf16[768,2048]{1,0:T(8,128)(2,1)} %all-gather.3.cloned.1.call-done, bf16[96,2048]{1,0:T(8,128)(2,1)} %bitcast.71, bf16[96,2048]{1,0:T(8,128)(2,1)} %bitcast.72), kind=kOutput, calls=%fused_computation.12 | convolution fusion | flops 605552640 | bytes 4521984 | tf_op jit(solution)/shard_map/dot_general | solution.py:30
  121.1 2.0 fusion.13
  123.1 26.3 %all-to-all-done = bf16[64,144,128]{2,1,0:T(8,128)(2,1)S(1)} async-done(((bf16[64,144,128]{2,1,0:T(8,128)(2,1)}), bf16[64,144,128]{2,1,0:T(8,128)(2,1)S(1)}, u32[]{:S(2)}, u32[]{:S(2)}) %all-to-all-start) | async-done | bytes 2359328 | tf_op jit(solution)/shard_map/all_to_all | solution.py:67
  149.5 1.9 collective-permute-start.1
  151.4 12.8 %collective-permute-done.1 = f32[768,192]{0,1:T(8,128)S(1)} collective-permute-done((f32[768,192]{0,1:T(8,128)}, f32[768,192]{0,1:T(8,128)S(1)}, u32[]{:S(2)}, u32[]{:S(2)}) %collective-permute-start.1) | collective-permute-done | bytes 589856 | tf_op jit(solution)/shard_map/ppermute | solution.py:117
  165.0 44.2 %all-gather.5.cloned.1.call-done = bf16[768,768]{0,1:T(8,128)(2,1)} async-done(((bf16[768,96]{0,1:T(8,128)(2,1)}), bf16[768,768]{0,1:T(8,128)(2,1)}) %all-gather.5.cloned.1.call-update) | async-done | bytes 1179664 | tf_op jit(solution)/shard_map/all_gather | solution.py:124
  209.2 2.3 convolution_convert_fusion
  211.5 1.2 reshape.81
  212.6 13.1 %all-to-all-start.2 = ((bf16[64,12,512]{2,1,0:T(8,128)(2,1)}), bf16[64,12,512]{2,1,0:T(8,128)(2,1)S(1)}, u32[]{:S(2)}, u32[]{:S(2)}) async-start(bf16[64,12,512]{2,1,0:T(8,128)(2,1)} %reshape.81), calls=%async_computation.2 | async-start | bytes 2097152 | tf_op jit(solution)/shard_map/all_to_all | solution.py:131
  225.7 2.3 gather_fusion
  228.0 27.7 %all-to-all-done.2 = bf16[64,12,512]{2,1,0:T(8,128)(2,1)S(1)} async-done(((bf16[64,12,512]{2,1,0:T(8,128)(2,1)}), bf16[64,12,512]{2,1,0:T(8,128)(2,1)S(1)}, u32[]{:S(2)}, u32[]{:S(2)}) %all-to-all-start.2) | async-done | bytes 786464 | tf_op jit(solution)/shard_map/all_to_all | solution.py:131
  255.7 6.6 %all-to-all-start.3 = ((bf16[64,144,128]{2,1,0:T(8,128)(2,1)}), bf16[64,144,128]{2,1,0:T(8,128)(2,1)S(1)}, u32[]{:S(2)}, u32[]{:S(2)}) async-start(bf16[64,144,128]{2,1,0:T(8,128)(2,1)} %gather_fusion), calls=%async_computation.3 | async-start | bytes 4718592 | tf_op jit(solution)/shard_map/all_to_all | solution.py:72
  263.0 1.2 fusion.6
  264.2 1.1 reshape.82
  265.2 2.0 convolution_convert_fusion.2
  267.2 58.1 %all-to-all-done.3 = bf16[64,144,128]{2,1,0:T(8,128)(2,1)S(1)} async-done(((bf16[64,144,128]{2,1,0:T(8,128)(2,1)}), bf16[64,144,128]{2,1,0:T(8,128)(2,1)S(1)}, u32[]{:S(2)}, u32[]{:S(2)}) %all-to-all-start.3) | async-done | bytes 2359328 | tf_op jit(solution)/shard_map/all_to_all | solution.py:72
  325.3 1.1 fusion.12
  326.7 1.2 reshape_reshape.10
  328.3 1.2 reshape_reshape.11
  329.8 1.2 reshape_reshape.9
  (57 shorter events, 11.1 us)
Async XLA Ops:
  7.2 5.8 %copy-start = (bf16[48,512]{1,0:T(8,128)(2,1)S(1)}, bf16[48,512]{1,0:T(8,128)(2,1)}, u32[]{:S(2)}) copy-start(bf16[48,512]{1,0:T(8,128)(2,1)} %param.8) | copy-start | bytes 147460
  13.0 18.2 %copy-start.2 = (bf16[1,96,4096]{2,1,0:T(8,128)(2,1)S(1)}, bf16[1,96,4096]{2,1,0:T(8,128)(2,1)}, u32[]{:S(2)}) copy-start(bf16[1,96,4096]{2,1,0:T(8,128)(2,1)} %param.13) | copy-start | bytes 2359300
  14.5 58.9 %all-to-all-start.1 = ((bf16[64,12,512]{2,1,0:T(8,128)(2,1)}), bf16[64,12,512]{2,1,0:T(8,128)(2,1)S(1)}, u32[]{:S(2)}, u32[]{:S(2)}) async-start(bf16[64,12,512]{2,1,0:T(8,128)(2,1)} %reshape.79), calls=%async_computation.1 | async-start | bytes 2097152 | tf_op jit(solution)/shard_map/all_to_all | solution.py:107
  31.1 86.6 %all-gather.3.cloned.1.call-start = ((), (), s32[]{:S(2)}) async-start(), calls=%async_computation.4 | async-start | bytes 3932160 | tf_op jit(solution)/shard_map/all_gather | solution.py:112
  39.0 35.6 %copy-start.5 = (bf16[1,768,512]{2,1,0:T(8,128)(2,1)S(1)}, bf16[1,768,512]{2,1,0:T(8,128)(2,1)}, u32[]{:S(2)}) copy-start(bf16[1,768,512]{2,1,0:T(8,128)(2,1)} %param.15) | copy-start | bytes 2359300
  39.0 34.4 %collective-permute-start = (bf16[192,2048]{1,0:T(8,128)(2,1)S(1)}, bf16[192,2048]{1,0:T(8,128)(2,1)S(1)}, u32[]{:S(2)}, u32[]{:S(2)}) collective-permute-start(bf16[192,2048]{1,0:T(8,128)(2,1)S(1)} %pad_maximum_fusion.1), channel_id=1, source_target_pairs={{0,4},{4,0},{1,5},{5,1},{2,6},{6,2},{3,7},{7,3},{8,12},{12,8},{9,1... | collective-permute-start | bytes 2359304 | tf_op jit(solution)/shard_map/ppermute | solution.py:103
  73.4 1.5 copy-start.9
  74.8 1.1 copy-start.3
  78.6 13.7 %copy-start.4 = (bf16[96,1,2048]{2,1,0:T(2,128)(2,1)S(1)}, bf16[96,1,2048]{2,1,0:T(2,128)(2,1)}, u32[]{:S(2)}) copy-start(bf16[96,1,2048]{2,1,0:T(2,128)(2,1)} %get-tuple-element.17) | copy-start | bytes 1179652
  78.6 70.8 %all-to-all-start = ((bf16[64,144,128]{2,1,0:T(8,128)(2,1)}), bf16[64,144,128]{2,1,0:T(8,128)(2,1)S(1)}, u32[]{:S(2)}, u32[]{:S(2)}) async-start(bf16[64,144,128]{2,1,0:T(8,128)(2,1)} %bitcast.60), calls=%async_computation | async-start | bytes 4718592 | tf_op jit(solution)/shard_map/all_to_all | solution.py:67
  89.9 119.3 %all-gather.5.cloned.1.call-start = ((), (), s32[]{:S(2)}) async-start(), calls=%async_computation.5 | async-start | bytes 1327104 | tf_op jit(solution)/shard_map/all_gather | solution.py:124
  117.7 3.4 %copy-start.8 = (bf16[768,2048]{1,0:T(8,128)(2,1)S(1)}, bf16[768,2048]{1,0:T(8,128)(2,1)}, u32[]{:S(2)}) copy-start(bf16[768,2048]{1,0:T(8,128)(2,1)} %all-gather.3.cloned.1.call-done) | copy-start | bytes 9437188
  117.7 3.4 %copy-start.10 = (bf16[192,2048]{1,0:T(8,128)(2,1)S(1)}, bf16[192,2048]{1,0:T(8,128)(2,1)}, u32[]{:S(2)}) copy-start(bf16[192,2048]{1,0:T(8,128)(2,1)} %copy-done.9) | copy-start | bytes 2359300
  149.5 14.7 %collective-permute-start.1 = (f32[768,192]{0,1:T(8,128)}, f32[768,192]{0,1:T(8,128)S(1)}, u32[]{:S(2)}, u32[]{:S(2)}) collective-permute-start(f32[768,192]{0,1:T(8,128)} %fusion.13), channel_id=1, source_target_pairs={{0,4},{4,0},{1,5},{5,1},{2,6},{6,2},{3,7},{7,3},{8,12},{12,8},{9,1... | collective-permute-start | bytes 1769480 | tf_op jit(solution)/shard_map/ppermute | solution.py:117
  211.5 14.2 %copy-start.7 = (s32[64]{0:T(128)S(1)}, s32[64]{0:T(128)}, u32[]{:S(2)}) copy-start(s32[64]{0:T(128)} %param.11) | copy-start | bytes 772
  212.6 43.1 %all-to-all-start.2 = ((bf16[64,12,512]{2,1,0:T(8,128)(2,1)}), bf16[64,12,512]{2,1,0:T(8,128)(2,1)S(1)}, u32[]{:S(2)}, u32[]{:S(2)}) async-start(bf16[64,12,512]{2,1,0:T(8,128)(2,1)} %reshape.81), calls=%async_computation.2 | async-start | bytes 2097152 | tf_op jit(solution)/shard_map/all_to_all | solution.py:131
  228.0 34.3 %copy-start.6 = (bf16[48,8]{0,1:T(8,128)(2,1)S(1)}, bf16[48,8]{0,1:T(8,128)(2,1)}, u32[]{:S(2)}) copy-start(bf16[48,8]{0,1:T(8,128)(2,1)} %param.10) | copy-start | bytes 2308
  255.7 69.6 %all-to-all-start.3 = ((bf16[64,144,128]{2,1,0:T(8,128)(2,1)}), bf16[64,144,128]{2,1,0:T(8,128)(2,1)S(1)}, u32[]{:S(2)}, u32[]{:S(2)}) async-start(bf16[64,144,128]{2,1,0:T(8,128)(2,1)} %gather_fusion), calls=%async_computation.3 | async-start | bytes 4718592 | tf_op jit(solution)/shard_map/all_to_all | solution.py:72
  326.4 1.5 copy-start.1
Sparse Core Ops, SparseCore 0:
  74.7 42.9 all-gather.2
  165.1 44.0 all-gather.4

commit v4 on v3

--- a/solution.py
+++ b/solution.py
@@ -62,15 +62,8 @@
     return gate, up, down
 
 
-def spread_weights(gate, up, down, groups):
-    packed = pack_weights(gate, up, down, groups)
-    return lax.all_to_all(packed, "expert", split_axis=0, concat_axis=0, tiled=True)
-
-
-def finish_exchange(spread, partner, gate_shape, down_shape):
-    ordered = jnp.take(spread, partner, axis=0, mode="clip")
-    arrived = lax.all_to_all(ordered, "expert", split_axis=0, concat_axis=0, tiled=True)
-    return unpack_weights(arrived, gate_shape, down_shape)
+def to_lanes(block, groups):
+    return block.reshape(groups, -1, LANES)
 
 
 def body(tokens, route_ids, route_weight, partner, old_place, gate_weight, up_weight, down_weight):
@@ -79,11 +72,10 @@
     gate_block = gate_weight[0]
     up_block = up_weight[0]
     down_block = down_weight[0]
+    rows, width = gate_block.shape
+    depth, narrow_width = down_block.shape
+    pair = [(0, 1), (1, 0)]
 
-    spread = spread_weights(gate_block, up_block, down_block, groups)
-
-    rows, width = gate_block.shape
-    pair = [(0, 1), (1, 0)]
     gate_halves = gate_block.reshape(rows, 2, width // 2)
     up_halves = up_block.reshape(rows, 2, width // 2)
     keep = jnp.concatenate(
@@ -104,34 +96,50 @@
 
     dispatch, combine, capacity = slot_layout(route_ids, route_weight, old_place, groups)
     outgoing = jnp.dot(dispatch, tokens, preferred_element_type=jnp.float32).astype(jnp.bfloat16)
-    arrived_rows = lax.all_to_all(
-        outgoing.reshape(groups, capacity, -1), "expert", split_axis=0, concat_axis=0, tiled=True
+    packed = pack_weights(gate_block, up_block, down_block, groups)
+    token_lanes = to_lanes(outgoing, groups)
+    split_at = token_lanes.shape[1]
+    first = lax.all_to_all(
+        jnp.concatenate([token_lanes, packed], axis=1),
+        "expert",
+        split_axis=0,
+        concat_axis=0,
+        tiled=True,
     )
-    taken, arrived_rows = lax.optimization_barrier((taken, arrived_rows))
-    slice_rows = arrived_rows.reshape(-1, arrived_rows.shape[2])
-    half_rows = lax.all_gather(slice_rows, "x", axis=1, tiled=True)
-    own_part = contract_last(half_rows, keep)
-    other_part = contract_last(half_rows, taken)
-    spread, own_part, other_part = lax.optimization_barrier((spread, own_part, other_part))
-    new_gate, new_up, new_down = finish_exchange(spread, partner, gate_block.shape, down_block.shape)
+    slice_rows = first[:, :split_at].reshape(groups * capacity, narrow_width)
+    spread = first[:, split_at:]
+
+    pieces = lax.all_gather(slice_rows, "x", axis=0, tiled=False)
+    keep3 = keep.reshape(keep.shape[0], pieces.shape[0], narrow_width)
+    taken3 = taken.reshape(taken.shape[0], pieces.shape[0], narrow_width)
+    own_part = lax.dot_general(
+        pieces, keep3, (((0, 2), (1, 2)), ((), ())), preferred_element_type=jnp.float32
+    )
+    other_part = lax.dot_general(
+        pieces, taken3, (((0, 2), (1, 2)), ((), ())), preferred_element_type=jnp.float32
+    )
     back = lax.ppermute(other_part, "zlo", pair)
     sums = own_part + back
     gate_sum = sums[:, :rows]
     up_sum = sums[:, rows:]
     hidden = (jax.nn.silu(gate_sum) * up_sum).astype(jnp.bfloat16)
-    produced = (
-        jnp.dot(
-            lax.all_gather(hidden, ("zlo", "x"), axis=1, tiled=True),
-            down_block,
-            preferred_element_type=jnp.float32,
-        )
-        .astype(jnp.bfloat16)
-        .reshape(groups, capacity, -1)
+    hidden_all = lax.all_gather(hidden, ("zlo", "x"), axis=0, tiled=False)
+    down3 = down_block.reshape(hidden_all.shape[0], rows, narrow_width)
+    produced = lax.dot_general(
+        hidden_all, down3, (((0, 2), (0, 1)), ((), ())), preferred_element_type=jnp.float32
+    ).astype(jnp.bfloat16)
+
+    ordered = jnp.take(spread, partner, axis=0, mode="clip")
+    second = lax.all_to_all(
+        jnp.concatenate([to_lanes(produced, groups), ordered], axis=1),
+        "expert",
+        split_axis=0,
+        concat_axis=0,
+        tiled=True,
     )
-    returned = lax.all_to_all(produced, "expert", split_axis=0, concat_axis=0, tiled=True)
-    layer_out = jnp.dot(
-        combine, returned.reshape(-1, returned.shape[2]), preferred_element_type=jnp.float32
-    ).astype(jnp.bfloat16)
+    returned = second[:, :split_at].reshape(groups * capacity, narrow_width)
+    new_gate, new_up, new_down = unpack_weights(second[:, split_at:], gate_block.shape, down_block.shape)
+    layer_out = jnp.dot(combine, returned, preferred_element_type=jnp.float32).astype(jnp.bfloat16)
     return (
         layer_out,
         new_gate.reshape(gate_weight.shape),

time: 339 us -> 347 us (1.024)
  the two profiles are of different devices: /device:TPU:4 before, /device:TPU:40 now
where the time goes in v4:
time: 347 us
  waiting for transfers between devices  165 us (48%)
  blocking collectives  90.2 us (26%)
  local copies, waits for them, and re-layouts  40.2 us (12%)
  starting transfers between devices  20.3 us (6%)
  between operations  14.4 us (4%)
  other arithmetic  8.55 us (2%)
  matrix products  7.61 us (2%)
    all_to_all x1, blocking collectives, body(): lax.all_to_all(jnp.concatenate([token_lanes, packed], axis=1), 'expert',...  90.2 us
    all_to_all x1, waiting for transfers between devices, body(): lax.all_to_all(jnp.concatenate([to_lanes(produced, groups), ordered], axi...  88.6 us
    all_gather x1, waiting for transfers between devices, body(): hidden_all = lax.all_gather(hidden, ('zlo', 'x'), axis=0, tiled=False)  40.8 us
    ppermute x1, waiting for transfers between devices, body(): taken = lax.ppermute(give, 'zlo', pair)  18.5 us
    all_to_all x1, starting transfers between devices, body(): lax.all_to_all(jnp.concatenate([to_lanes(produced, groups), ordered], axi...  12.7 us
    ppermute x1, waiting for transfers between devices, body(): back = lax.ppermute(other_part, 'zlo', pair)  12.1 us
    dynamic_slice x1, local copies, waits for them, and re-layouts, body(): lax.dynamic_index_in_dim(gate_halves, 1 - half, axis=1, keepdims=False)  9.15 us
  transfers between devices with their start and end apart: 5, of which 5 were waited for; matrix products, arithmetic and copies ran while one was open for 6% of the time, Pallas kernels for 0%

profile of v4, /device:TPU:40, one launch (start us, length us, event | category | flops | bytes accessed | tf_op | source)
XLA Modules:
  0.0 346.6 jit_solution(16128838432431993070)
XLA Ops:
  8.3 1.6 select_reduce_fusion
  10.7 0.9 reduce-window.6
  14.4 1.8 reshape_squeeze.20
  16.8 0.9 copy.78
  18.1 90.2 %all_to_all.10 = bf16[64,192,128]{2,1,0:T(8,128)(2,1)S(1)} all-to-all(bf16[64,192,128]{2,1,0:T(8,128)(2,1)S(1)} %pad_maximum_fusion), channel_id=1, replica_groups=mesh['expert'=64,'zlo'=2,'x'=4] {'expert'}, dimensions={0} | all-to-all | bytes 6291456 | tf_op jit(solution)/shard_map/all_to_all | solution.py:102
  108.3 0.9 slice.47
  109.3 2.3 all_gather_reshape.3
  111.8 3.3 reshape_squeeze.21
  115.1 3.2 reshape_squeeze.22
  118.3 9.2 %constant_dynamic-slice_fusion = (bf16[96,1,2048]{2,1,0:T(2,128)(2,1)S(1)}, bf16[96,2048]{1,0:T(8,128)(2,1)}, bf16[96,2048]{1,0:T(8,128)(2,1)}, bf16[96,1,2048]{2,1,0:T(2,128)(2,1)S(1)}) fusion(bf16[96,2,2048]{2,1,0:T(2,128)(2,1)} %reshape_squeeze.21, s32[]{:T(128)S(6)} %select_n.15, s32[]{:T(128)S(6)} %select_n.14, bf16[96,2,2048]{2,1,0:T(2,128)(2,1)} %reshape_squeeze.22), kind=kLoop, calls=%fused_computation.41 | loop fusion | bytes 3145736 | tf_op jit(solution)/shard_map/jit(dynamic_index_in_dim)/dynamic_slice | solution.py:90
  128.0 3.8 %collective-permute-start = (bf16[192,2048]{1,0:T(8,128)(2,1)S(1)}, bf16[192,2048]{1,0:T(8,128)(2,1)}, u32[]{:S(2)}, u32[]{:S(2)}) collective-permute-start(bf16[192,2048]{1,0:T(8,128)(2,1)S(1)} %pad_maximum_fusion.3), channel_id=1, source_target_pairs={{0,4},{4,0},{1,5},{5,1},{2,6},{6,2},{3,7},{7,3},{8,12},{12,8},{9,1... | collective-permute-start | bytes 2359304 | tf_op jit(solution)/shard_map/ppermute | solution.py:95
  131.8 18.5 %collective-permute-done = bf16[192,2048]{1,0:T(8,128)(2,1)} collective-permute-done((bf16[192,2048]{1,0:T(8,128)(2,1)S(1)}, bf16[192,2048]{1,0:T(8,128)(2,1)}, u32[]{:S(2)}, u32[]{:S(2)}) %collective-permute-start) | collective-permute-done | bytes 786464 | tf_op jit(solution)/shard_map/ppermute | solution.py:95
  150.3 5.3 %all-gather.4.cloned.1.call-done = bf16[4,768,512]{2,1,0:T(8,128)(2,1)} async-done(((bf16[1,768,512]{2,1,0:T(8,128)(2,1)}), bf16[4,768,512]{2,1,0:T(8,128)(2,1)}) %all-gather.4.cloned.1.call-update) | async-done | bytes 3145744 | tf_op jit(solution)/shard_map/all_gather | solution.py:112
  155.6 3.4 convolution_bitcast_fusion
  159.0 3.6 %collective-permute-start.1 = (f32[768,192]{0,1:T(8,128)S(1)}, f32[768,192]{0,1:T(8,128)S(1)}, u32[]{:S(2)}, u32[]{:S(2)}) collective-permute-start(f32[768,192]{0,1:T(8,128)S(1)} %convolution_bitcast_fusion), channel_id=1, source_target_pairs={{0,4},{4,0},{1,5},{5,1},{2,6},{6,2},{3,7},{7,3},{8,12},{12,8},{9,1... | collective-permute-start | bytes 1769480 | tf_op jit(solution)/shard_map/ppermute | solution.py:121
  162.7 1.2 convolution_bitcast_fusion.1
  163.9 12.1 %collective-permute-done.1 = f32[768,192]{0,1:T(8,128)S(1)} collective-permute-done((f32[768,192]{0,1:T(8,128)S(1)}, f32[768,192]{0,1:T(8,128)S(1)}, u32[]{:S(2)}, u32[]{:S(2)}) %collective-permute-start.1) | collective-permute-done | bytes 589856 | tf_op jit(solution)/shard_map/ppermute | solution.py:121
  176.8 1.6 slice.50
  178.4 2.7 gather_fusion
  181.1 40.8 %all-gather.6.cloned.1.call-done = bf16[6144,96]{0,1:T(8,128)(2,1)} async-done(((bf16[768,96]{0,1:T(8,128)(2,1)}), bf16[6144,96]{0,1:T(8,128)(2,1)}) %all-gather.6.cloned.1.call-update) | async-done | bytes 1179664 | tf_op jit(solution)/shard_map/all_gather | solution.py:126
  221.9 1.5 copy.94
  223.4 1.8 bitcast_convert_fusion
  225.2 1.6 reshape.86
  226.8 2.1 pad_maximum_fusion.1
  228.9 12.7 %all-to-all-start.1 = ((bf16[64,192,128]{2,1,0:T(8,128)(2,1)}), bf16[64,192,128]{2,1,0:T(8,128)(2,1)S(1)}, u32[]{:S(2)}, u32[]{:S(2)}) async-start(bf16[64,192,128]{2,1,0:T(8,128)(2,1)} %pad_maximum_fusion.1), calls=%async_computation.1 | async-start | bytes 6291456 | tf_op jit(solution)/shard_map/all_to_all | solution.py:133
  242.1 88.6 %all-to-all-done.1 = bf16[64,192,128]{2,1,0:T(8,128)(2,1)S(1)} async-done(((bf16[64,192,128]{2,1,0:T(8,128)(2,1)}), bf16[64,192,128]{2,1,0:T(8,128)(2,1)S(1)}, u32[]{:S(2)}, u32[]{:S(2)}) %all-to-all-start.1) | async-done | bytes 3145760 | tf_op jit(solution)/shard_map/all_to_all | solution.py:133
  330.7 0.9 slice.51
  331.6 2.3 reshape.87
  334.6 1.2 reshape_reshape.11
  336.1 1.2 reshape_reshape.10
  337.6 1.2 reshape_reshape.9
  338.8 0.9 convolution_convert_fusion.1
  (57 shorter events, 9.2 us)
Async XLA Ops:
  7.2 6.0 %copy-start = (bf16[48,512]{1,0:T(8,128)(2,1)S(1)}, bf16[48,512]{1,0:T(8,128)(2,1)}, u32[]{:S(2)}) copy-start(bf16[48,512]{1,0:T(8,128)(2,1)} %param.8) | copy-start | bytes 147460
  7.2 6.9 %copy-start.2 = (bf16[1,96,4096]{2,1,0:T(8,128)(2,1)S(1)}, bf16[1,96,4096]{2,1,0:T(8,128)(2,1)}, u32[]{:S(2)}) copy-start(bf16[1,96,4096]{2,1,0:T(8,128)(2,1)} %param.14) | copy-start | bytes 2359300
  7.2 148.4 %all-gather.4.cloned.1.call-start = ((), (), s32[]{:S(2)}) async-start(), calls=%async_computation.2 | async-start | bytes 3932160 | tf_op jit(solution)/shard_map/all_gather | solution.py:112
  9.9 4.4 %copy-start.1 = (bf16[1,96,4096]{2,1,0:T(8,128)(2,1)S(1)}, bf16[1,96,4096]{2,1,0:T(8,128)(2,1)}, u32[]{:S(2)}) copy-start(bf16[1,96,4096]{2,1,0:T(8,128)(2,1)} %param.13) | copy-start | bytes 2359300
  111.6 110.3 %all-gather.6.cloned.1.call-start = ((), (), s32[]{:S(2)}) async-start(), calls=%async_computation.3 | async-start | bytes 1327104 | tf_op jit(solution)/shard_map/all_gather | solution.py:126
  128.0 22.3 %collective-permute-start = (bf16[192,2048]{1,0:T(8,128)(2,1)S(1)}, bf16[192,2048]{1,0:T(8,128)(2,1)}, u32[]{:S(2)}, u32[]{:S(2)}) collective-permute-start(bf16[192,2048]{1,0:T(8,128)(2,1)S(1)} %pad_maximum_fusion.3), channel_id=1, source_target_pairs={{0,4},{4,0},{1,5},{5,1},{2,6},{6,2},{3,7},{7,3},{8,12},{12,8},{9,1... | collective-permute-start | bytes 2359304 | tf_op jit(solution)/shard_map/ppermute | solution.py:95
  155.6 7.0 %copy-start.5 = (bf16[96,2048]{1,0:T(8,128)(2,1)S(1)}, bf16[96,2048]{1,0:T(8,128)(2,1)}, u32[]{:S(2)}) copy-start(bf16[96,2048]{1,0:T(8,128)(2,1)} %get-tuple-element.8) | copy-start | bytes 1179652
  155.6 7.0 %copy-start.4 = (bf16[96,2048]{1,0:T(8,128)(2,1)S(1)}, bf16[96,2048]{1,0:T(8,128)(2,1)}, u32[]{:S(2)}) copy-start(bf16[96,2048]{1,0:T(8,128)(2,1)} %get-tuple-element.11) | copy-start | bytes 1179652
  155.6 7.1 %copy-start.9 = (bf16[4,768,512]{2,1,0:T(8,128)(2,1)S(1)}, bf16[4,768,512]{2,1,0:T(8,128)(2,1)}, u32[]{:S(2)}) copy-start(bf16[4,768,512]{2,1,0:T(8,128)(2,1)} %all-gather.4.cloned.1.call-done) | copy-start | bytes 9437188
  159.0 17.0 %collective-permute-start.1 = (f32[768,192]{0,1:T(8,128)S(1)}, f32[768,192]{0,1:T(8,128)S(1)}, u32[]{:S(2)}, u32[]{:S(2)}) collective-permute-start(f32[768,192]{0,1:T(8,128)S(1)} %convolution_bitcast_fusion), channel_id=1, source_target_pairs={{0,4},{4,0},{1,5},{5,1},{2,6},{6,2},{3,7},{7,3},{8,12},{12,8},{9,1... | collective-permute-start | bytes 1769480 | tf_op jit(solution)/shard_map/ppermute | solution.py:121
  163.8 13.0 %copy-start.8 = (s32[64]{0:T(128)S(1)}, s32[64]{0:T(128)}, u32[]{:S(2)}) copy-start(s32[64]{0:T(128)} %param.11) | copy-start | bytes 772
  181.1 42.3 %copy-start.6 = (bf16[1,768,512]{2,1,0:T(8,128)(2,1)S(1)}, bf16[1,768,512]{2,1,0:T(8,128)(2,1)}, u32[]{:S(2)}) copy-start(bf16[1,768,512]{2,1,0:T(8,128)(2,1)} %param.15) | copy-start | bytes 2359300
  228.9 12.7 %copy-start.7 = (bf16[48,8]{0,1:T(8,128)(2,1)S(1)}, bf16[48,8]{0,1:T(8,128)(2,1)}, u32[]{:S(2)}) copy-start(bf16[48,8]{0,1:T(8,128)(2,1)} %param.10) | copy-start | bytes 2308
  228.9 101.8 %all-to-all-start.1 = ((bf16[64,192,128]{2,1,0:T(8,128)(2,1)}), bf16[64,192,128]{2,1,0:T(8,128)(2,1)S(1)}, u32[]{:S(2)}, u32[]{:S(2)}) async-start(bf16[64,192,128]{2,1,0:T(8,128)(2,1)} %pad_maximum_fusion.1), calls=%async_computation.1 | async-start | bytes 6291456 | tf_op jit(solution)/shard_map/all_to_all | solution.py:133
  336.1 2.7 copy-start.3
Sparse Core Ops, SparseCore 0:
  111.7 43.8 all-gather.3
  176.9 44.9 all-gather.5

commit v5 on v4

--- a/solution.py
+++ b/solution.py
@@ -66,9 +66,21 @@
     return block.reshape(groups, -1, LANES)
 
 
+def ring_gather(value, axis, size, index):
+    pieces = [value]
+    for shift in range(1, size):
+        pieces.append(lax.ppermute(value, axis, [(i, (i + shift) % size) for i in range(size)]))
+    sources = (index - jnp.arange(size, dtype=jnp.int32)) % size
+    return jnp.stack(pieces, axis=0), sources
+
+
 def body(tokens, route_ids, route_weight, partner, old_place, gate_weight, up_weight, down_weight):
     groups = lax.axis_size("expert")
     half = lax.axis_index("zlo")
+    column = lax.axis_index("x")
+    columns = lax.axis_size("x")
+    narrow_count = lax.axis_size("zlo") * columns
+    narrow_index = half * columns + column
     gate_block = gate_weight[0]
     up_block = up_weight[0]
     down_block = down_weight[0]
@@ -92,7 +104,8 @@
         ],
         axis=0,
     )
-    taken = lax.ppermute(give, "zlo", pair)
+    both = lax.all_gather(give, "zlo", axis=0, tiled=False)
+    taken = lax.dynamic_index_in_dim(both, 1 - half, axis=0, keepdims=False)
 
     dispatch, combine, capacity = slot_layout(route_ids, route_weight, old_place, groups)
     outgoing = jnp.dot(dispatch, tokens, preferred_element_type=jnp.float32).astype(jnp.bfloat16)
@@ -108,10 +121,14 @@
     )
     slice_rows = first[:, :split_at].reshape(groups * capacity, narrow_width)
     spread = first[:, split_at:]
+    ordered = jnp.take(spread, partner, axis=0, mode="clip")
+    arrived = lax.all_to_all(ordered, "expert", split_axis=0, concat_axis=0, tiled=True)
 
-    pieces = lax.all_gather(slice_rows, "x", axis=0, tiled=False)
-    keep3 = keep.reshape(keep.shape[0], pieces.shape[0], narrow_width)
-    taken3 = taken.reshape(taken.shape[0], pieces.shape[0], narrow_width)
+    pieces, sources = ring_gather(slice_rows, "x", columns, column)
+    keep3 = jnp.take(keep.reshape(keep.shape[0], columns, narrow_width), sources, axis=1, mode="clip")
+    taken3 = jnp.take(
+        taken.reshape(taken.shape[0], columns, narrow_width), sources, axis=1, mode="clip"
+    )
     own_part = lax.dot_general(
         pieces, keep3, (((0, 2), (1, 2)), ((), ())), preferred_element_type=jnp.float32
     )
@@ -123,22 +140,17 @@
     gate_sum = sums[:, :rows]
     up_sum = sums[:, rows:]
     hidden = (jax.nn.silu(gate_sum) * up_sum).astype(jnp.bfloat16)
-    hidden_all = lax.all_gather(hidden, ("zlo", "x"), axis=0, tiled=False)
-    down3 = down_block.reshape(hidden_all.shape[0], rows, narrow_width)
+    hidden_all, owners = ring_gather(hidden, ("zlo", "x"), narrow_count, narrow_index)
+    down3 = jnp.take(down_block.reshape(narrow_count, rows, narrow_width), owners, axis=0, mode="clip")
     produced = lax.dot_general(
         hidden_all, down3, (((0, 2), (0, 1)), ((), ())), preferred_element_type=jnp.float32
     ).astype(jnp.bfloat16)
 
-    ordered = jnp.take(spread, partner, axis=0, mode="clip")
-    second = lax.all_to_all(
-        jnp.concatenate([to_lanes(produced, groups), ordered], axis=1),
-        "expert",
-        split_axis=0,
-        concat_axis=0,
-        tiled=True,
-    )
-    returned = second[:, :split_at].reshape(groups * capacity, narrow_width)
-    new_gate, new_up, new_down = unpack_weights(second[:, split_at:], gate_block.shape, down_block.shape)
+    produced, arrived = lax.optimization_barrier((produced, arrived))
+    returned = lax.all_to_all(
+        produced.reshape(groups, capacity, -1), "expert", split_axis=0, concat_axis=0, tiled=True
+    ).reshape(groups * capacity, narrow_width)
+    new_gate, new_up, new_down = unpack_weights(arrived, gate_block.shape, down_block.shape)
     layer_out = jnp.dot(combine, returned, preferred_element_type=jnp.float32).astype(jnp.bfloat16)
     return (
         layer_out,

time: 347 us -> 311 us (0.90)
  the two profiles are of different devices: /device:TPU:40 before, /device:TPU:16 now
where the time goes in v5:
time: 311 us; the launch traced here: 310 us
  waiting for transfers between devices  126 us (41%)
  starting transfers between devices  91.4 us (29%)
  local copies, waits for them, and re-layouts  57.1 us (18%)
  between operations  14.5 us (5%)
  matrix products  11.1 us (4%)
  other arithmetic  9.64 us (3%)
    all_to_all x1, waiting for transfers between devices, body(): lax.all_to_all(jnp.concatenate([token_lanes, packed], axis=1), 'expert',...  57 us
    ppermute x1, waiting for transfers between devices, body(): back = lax.ppermute(other_part, 'zlo', pair)  46 us
    ppermute x10, starting transfers between devices, ring_gather(): lax.ppermute(value, axis, [(i, (i + shift) % size) for i in range(size)])  37.6 us
    all_to_all x1, waiting for transfers between devices, body(): lax.all_to_all(produced.reshape(groups, capacity, -1), 'expert', split_ax...  23 us
    all_to_all x1, starting transfers between devices, body(): lax.all_to_all(ordered, 'expert', split_axis=0, concat_axis=0, tiled=True)  21.2 us
    all_to_all x1, starting transfers between devices, body(): lax.all_to_all(jnp.concatenate([token_lanes, packed], axis=1), 'expert',...  16.5 us
    all_to_all x1, starting transfers between devices, body(): lax.all_to_all(produced.reshape(groups, capacity, -1), 'expert', split_ax...  14 us
    dynamic_slice x1, local copies, waits for them, and re-layouts, body(): lax.dynamic_index_in_dim(up_halves, half, axis=1, keepdims=False)  9.22 us
  transfers between devices with their start and end apart: 15, of which 3 were waited for; matrix products, arithmetic and copies ran while one was open for 21% of the time, Pallas kernels for 0%

profile of v5, /device:TPU:16, one launch (start us, length us, event | category | flops | bytes accessed | tf_op | source)
XLA Modules:
  0.0 309.8 jit_solution(14723159662280270794)
XLA Ops:
  8.2 1.6 select_reduce_fusion
  16.6 2.1 pad_maximum_fusion
  18.7 16.5 %all-to-all-start = ((bf16[64,192,128]{2,1,0:T(8,128)(2,1)}), bf16[64,192,128]{2,1,0:T(8,128)(2,1)S(1)}, u32[]{:S(2)}, u32[]{:S(2)}) async-start(bf16[64,192,128]{2,1,0:T(8,128)(2,1)} %pad_maximum_fusion), calls=%async_computation | async-start | bytes 6291456 | tf_op jit(solution)/shard_map/all_to_all | solution.py:115
  35.4 3.3 %reshape_squeeze.21 = bf16[96,2,2048]{2,1,0:T(2,128)(2,1)} reshape(bf16[1,96,4096]{2,1,0:T(8,128)(2,1)} %param.13) | data formatting | bytes 1572864 | tf_op jit(solution)/shard_map/reshape;squeeze | solution.py:91
  38.6 3.2 %reshape_squeeze.22 = bf16[96,2,2048]{2,1,0:T(2,128)(2,1)} reshape(bf16[1,96,4096]{2,1,0:T(8,128)(2,1)} %param.14) | data formatting | bytes 1572864 | tf_op jit(solution)/shard_map/reshape;squeeze | solution.py:92
  41.9 9.2 %dynamic-slice_reduce_fusion = (bf16[96,2048]{1,0:T(8,128)(2,1)}, bf16[96,1,2048]{2,1,0:T(2,128)(2,1)S(1)}, bf16[96,1,2048]{2,1,0:T(2,128)(2,1)S(1)}, bf16[96,2048]{1,0:T(8,128)(2,1)}) fusion(bf16[96,2,2048]{2,1,0:T(2,128)(2,1)} %reshape_squeeze.22, s32[]{:T(128)S(6)} %select_n.43, s32[]{:T(128)S(6)} %select_n.45, bf16[96,2,2048]{2,1,0:T(2,128)(2,1)} %reshape_squeeze.21), kind=kLoop, calls=%fused_computation.23 | loop fusion | bytes 3145736 | tf_op jit(solution)/shard_map/jit(dynamic_index_in_dim)/dynamic_slice | solution.py:96
  52.5 57.0 %all-to-all-done = bf16[64,192,128]{2,1,0:T(8,128)(2,1)S(1)} async-done(((bf16[64,192,128]{2,1,0:T(8,128)(2,1)}), bf16[64,192,128]{2,1,0:T(8,128)(2,1)S(1)}, u32[]{:S(2)}, u32[]{:S(2)}) %all-to-all-start) | async-done | bytes 3145760 | tf_op jit(solution)/shard_map/all_to_all | solution.py:115
  110.4 2.3 reshape.169
  112.8 3.5 %collective-permute-start = (bf16[768,512]{1,0:T(8,128)(2,1)}, bf16[768,512]{1,0:T(8,128)(2,1)}, u32[]{:S(2)}, u32[]{:S(2)}) collective-permute-start(bf16[768,512]{1,0:T(8,128)(2,1)} %reshape.169), channel_id=1, source_target_pairs={{0,1},{1,2},{2,3},{3,0},{4,5},{5,6},{6,7},{7,4},{8,9},{9,10},{10,1... | collective-permute-start | bytes 2359304 | tf_op jit(solution)/shard_map/ppermute | solution.py:72
  116.3 4.9 %collective-permute-start.1 = (bf16[768,512]{1,0:T(8,128)(2,1)}, bf16[768,512]{1,0:T(8,128)(2,1)}, u32[]{:S(2)}, u32[]{:S(2)}) collective-permute-start(bf16[768,512]{1,0:T(8,128)(2,1)} %reshape.169), channel_id=1, source_target_pairs={{0,2},{1,3},{2,0},{3,1},{4,6},{5,7},{6,4},{7,5},{8,10},{9,11},{10,... | collective-permute-start | bytes 2359304 | tf_op jit(solution)/shard_map/ppermute | solution.py:72
  121.2 2.8 collective-permute-start.2
  124.1 1.6 slice.48
  125.6 3.9 %gather_fusion.3 = bf16[64,144,128]{2,1,0:T(8,128)(2,1)} fusion(bf16[64,144,128]{2,1,0:T(8,128)(2,1)} %slice.48, s32[1024]{0:T(1024)S(1)} %pad_clamp_fusion), kind=kCustom, calls=%fused_computation.3 | custom fusion | bytes 4718848 | tf_op jit(solution)/shard_map/jit(_take)/gather | solution.py:124
  129.6 21.2 %all-to-all-start.1 = ((bf16[64,144,128]{2,1,0:T(8,128)(2,1)}), bf16[64,144,128]{2,1,0:T(8,128)(2,1)S(1)}, u32[]{:S(2)}, u32[]{:S(2)}) async-start(bf16[64,144,128]{2,1,0:T(8,128)(2,1)} %gather_fusion.3), calls=%async_computation.1 | async-start | bytes 4718592 | tf_op jit(solution)/shard_map/all_to_all | solution.py:125
  150.8 2.1 constant_dynamic-slice_fusion
  152.9 3.1 reshape.170
  156.0 2.2 copy.61
  158.1 2.6 gather_fusion.1
  162.1 4.2 %convolution_bitcast_fusion = f32[768,192]{0,1:T(8,128)} fusion(bf16[4,192,512]{2,1,0:T(8,128)(2,1)} %gather_fusion.1, bf16[1,768,512]{2,1,0:T(8,128)(2,1)} %bitcast.8, bf16[1,768,512]{2,1,0:T(8,128)(2,1)} %bitcast.7, bf16[1,768,512]{2,1,0:T(8,128)(2,1)} %bitcast.6, bf16[1,768,512]{2,1,0:T(8,128)(2,1)} %stack_reshape.3), kind=kOutput, calls=%fused_computation.9 | convolution fusion | flops 608698368 | bytes 4521984 | tf_op jit(solution)/shard_map/dot_general | solution.py:135
  166.3 1.9 collective-permute-start.3
  169.8 46.0 %collective-permute-done.3 = f32[768,192]{0,1:T(8,128)} collective-permute-done((f32[768,192]{0,1:T(8,128)}, f32[768,192]{0,1:T(8,128)}, u32[]{:S(2)}, u32[]{:S(2)}) %collective-permute-start.3) | collective-permute-done | bytes 589856 | tf_op jit(solution)/shard_map/ppermute | solution.py:138
  215.8 3.4 %fusion = f32[768,192]{0,1:T(8,128)S(1)} fusion(f32[768,192]{0,1:T(8,128)} %collective-permute-done.3, bf16[4,192,512]{2,1,0:T(8,128)(2,1)} %gather_fusion, bf16[1,768,512]{2,1,0:T(8,128)(2,1)} %bitcast.8, bf16[1,768,512]{2,1,0:T(8,128)(2,1)} %bitcast.7, bf16[1,768,512]{2,1,0:T(8,128)(2,1)} %bitcast.6, bf16[1,768,512]{2,1,0:T(8,128)(2,1)} %stack_reshape.3), kind=kOutput, calls=%fused_computation.11 | convolution fusion | flops 608845824 | bytes 5111808 | tf_op jit(solution)/shard_map/dot_general | solution.py:132
  220.0 2.9 collective-permute-start.4
  224.4 2.7 collective-permute-start.5
  227.0 5.8 %collective-permute-start.6 = (bf16[768,96]{0,1:T(8,128)(2,1)S(1)}, bf16[768,96]{0,1:T(8,128)(2,1)S(1)}, u32[]{:S(2)}, u32[]{:S(2)}) collective-permute-start(bf16[768,96]{0,1:T(8,128)(2,1)S(1)} %get-tuple-element.9), channel_id=1, source_target_pairs={{0,3},{1,4},{2,5},{3,6},{4,7},{5,0},{6,1},{7,2},{8,11},{9,12},{10,... | collective-permute-start | bytes 442376 | tf_op jit(solution)/shard_map/ppermute | solution.py:72
  232.8 1.9 collective-permute-start.7
  234.8 3.8 %collective-permute-start.8 = (bf16[768,96]{0,1:T(8,128)(2,1)S(1)}, bf16[768,96]{0,1:T(8,128)(2,1)S(1)}, u32[]{:S(2)}, u32[]{:S(2)}) collective-permute-start(bf16[768,96]{0,1:T(8,128)(2,1)S(1)} %get-tuple-element.9), channel_id=1, source_target_pairs={{0,5},{1,6},{2,7},{3,0},{4,1},{5,2},{6,3},{7,4},{8,13},{9,14},{10,... | collective-permute-start | bytes 442376 | tf_op jit(solution)/shard_map/ppermute | solution.py:72
  238.6 5.2 %collective-permute-start.9 = (bf16[768,96]{0,1:T(8,128)(2,1)S(1)}, bf16[768,96]{0,1:T(8,128)(2,1)S(1)}, u32[]{:S(2)}, u32[]{:S(2)}) collective-permute-start(bf16[768,96]{0,1:T(8,128)(2,1)S(1)} %get-tuple-element.9), channel_id=1, source_target_pairs={{0,6},{1,7},{2,0},{3,1},{4,2},{5,3},{6,4},{7,5},{8,14},{9,15},{10,... | collective-permute-start | bytes 442376 | tf_op jit(solution)/shard_map/ppermute | solution.py:72
  245.4 4.2 %collective-permute-start.10 = (bf16[768,96]{0,1:T(8,128)(2,1)S(1)}, bf16[768,96]{0,1:T(8,128)(2,1)S(1)}, u32[]{:S(2)}, u32[]{:S(2)}) collective-permute-start(bf16[768,96]{0,1:T(8,128)(2,1)S(1)} %get-tuple-element.9), channel_id=1, source_target_pairs={{0,7},{1,0},{2,1},{3,2},{4,3},{5,4},{6,5},{7,6},{8,15},{9,8},{10,9... | collective-permute-start | bytes 442376 | tf_op jit(solution)/shard_map/ppermute | solution.py:72
  253.6 2.3 bitcast_convert_fusion
  257.0 14.0 %all-to-all-start.2 = ((bf16[64,12,512]{2,1,0:T(8,128)(2,1)}), bf16[64,12,512]{2,1,0:T(8,128)(2,1)S(1)}, u32[]{:S(2)}, u32[]{:S(2)}) async-start(bf16[64,12,512]{2,1,0:T(8,128)(2,1)} %reshape.171), calls=%async_computation.2 | async-start | bytes 2097152 | tf_op jit(solution)/shard_map/all_to_all | solution.py:150
  278.9 23.0 %all-to-all-done.2 = bf16[64,12,512]{2,1,0:T(8,128)(2,1)S(1)} async-done(((bf16[64,12,512]{2,1,0:T(8,128)(2,1)}), bf16[64,12,512]{2,1,0:T(8,128)(2,1)S(1)}, u32[]{:S(2)}, u32[]{:S(2)}) %all-to-all-start.2) | async-done | bytes 786464 | tf_op jit(solution)/shard_map/all_to_all | solution.py:150
  (93 shorter events, 31.1 us)
Async XLA Ops:
  7.2 5.9 %copy-start = (bf16[48,512]{1,0:T(8,128)(2,1)S(1)}, bf16[48,512]{1,0:T(8,128)(2,1)}, u32[]{:S(2)}) copy-start(bf16[48,512]{1,0:T(8,128)(2,1)} %param.8) | copy-start | bytes 147460
  7.2 6.8 %copy-start.6 = (bf16[1,768,512]{2,1,0:T(8,128)(2,1)S(1)}, bf16[1,768,512]{2,1,0:T(8,128)(2,1)}, u32[]{:S(2)}) copy-start(bf16[1,768,512]{2,1,0:T(8,128)(2,1)} %param.15) | copy-start | bytes 2359300
  13.9 1.1 copy-start.4
  14.1 1.2 copy-start.5
  18.7 90.8 %all-to-all-start = ((bf16[64,192,128]{2,1,0:T(8,128)(2,1)}), bf16[64,192,128]{2,1,0:T(8,128)(2,1)S(1)}, u32[]{:S(2)}, u32[]{:S(2)}) async-start(bf16[64,192,128]{2,1,0:T(8,128)(2,1)} %pad_maximum_fusion), calls=%async_computation | async-start | bytes 6291456 | tf_op jit(solution)/shard_map/all_to_all | solution.py:115
  35.1 115.7 %all-gather.3.cloned.1.call-start = ((), (), s32[]{:S(2)}) async-start(), calls=%async_computation.3 | async-start | bytes 2359296 | tf_op jit(solution)/shard_map/all_gather | solution.py:107
  52.5 71.5 %copy-start.11 = (s32[64]{0:T(128)S(1)}, s32[64]{0:T(128)}, u32[]{:S(2)}) copy-start(s32[64]{0:T(128)} %param.11) | copy-start | bytes 772
  112.8 49.3 %collective-permute-start = (bf16[768,512]{1,0:T(8,128)(2,1)}, bf16[768,512]{1,0:T(8,128)(2,1)}, u32[]{:S(2)}, u32[]{:S(2)}) collective-permute-start(bf16[768,512]{1,0:T(8,128)(2,1)} %reshape.169), channel_id=1, source_target_pairs={{0,1},{1,2},{2,3},{3,0},{4,5},{5,6},{6,7},{7,4},{8,9},{9,10},{10,1... | collective-permute-start | bytes 2359304 | tf_op jit(solution)/shard_map/ppermute | solution.py:72
  116.3 45.8 %collective-permute-start.1 = (bf16[768,512]{1,0:T(8,128)(2,1)}, bf16[768,512]{1,0:T(8,128)(2,1)}, u32[]{:S(2)}, u32[]{:S(2)}) collective-permute-start(bf16[768,512]{1,0:T(8,128)(2,1)} %reshape.169), channel_id=1, source_target_pairs={{0,2},{1,3},{2,0},{3,1},{4,6},{5,7},{6,4},{7,5},{8,10},{9,11},{10,... | collective-permute-start | bytes 2359304 | tf_op jit(solution)/shard_map/ppermute | solution.py:72
  121.2 40.9 %collective-permute-start.2 = (bf16[768,512]{1,0:T(8,128)(2,1)}, bf16[768,512]{1,0:T(8,128)(2,1)}, u32[]{:S(2)}, u32[]{:S(2)}) collective-permute-start(bf16[768,512]{1,0:T(8,128)(2,1)} %reshape.169), channel_id=1, source_target_pairs={{0,3},{1,0},{2,1},{3,2},{4,7},{5,4},{6,5},{7,6},{8,11},{9,8},{10,9... | collective-permute-start | bytes 2359304 | tf_op jit(solution)/shard_map/ppermute | solution.py:72
  129.6 126.3 %all-to-all-start.1 = ((bf16[64,144,128]{2,1,0:T(8,128)(2,1)}), bf16[64,144,128]{2,1,0:T(8,128)(2,1)S(1)}, u32[]{:S(2)}, u32[]{:S(2)}) async-start(bf16[64,144,128]{2,1,0:T(8,128)(2,1)} %gather_fusion.3), calls=%async_computation.1 | async-start | bytes 4718592 | tf_op jit(solution)/shard_map/all_to_all | solution.py:125
  152.9 7.8 %copy-start.1 = (bf16[64,48,128]{2,1,0:T(8,128)(2,1)S(1)}, bf16[64,48,128]{2,1,0:T(8,128)(2,1)}, u32[]{:S(2)}) copy-start(bf16[64,48,128]{2,1,0:T(8,128)(2,1)} %slice.45) | copy-start | bytes 2359300
  162.1 6.1 %copy-start.9 = (bf16[96,2048]{1,0:T(8,128)(2,1)S(1)}, bf16[96,2048]{1,0:T(8,128)(2,1)}, u32[]{:S(2)}) copy-start(bf16[96,2048]{1,0:T(8,128)(2,1)} %get-tuple-element.15) | copy-start | bytes 1179652
  162.1 6.1 %copy-start.8 = (bf16[96,2048]{1,0:T(8,128)(2,1)S(1)}, bf16[96,2048]{1,0:T(8,128)(2,1)}, u32[]{:S(2)}) copy-start(bf16[96,2048]{1,0:T(8,128)(2,1)} %get-tuple-element.18) | copy-start | bytes 1179652
  166.3 49.5 %collective-permute-start.3 = (f32[768,192]{0,1:T(8,128)}, f32[768,192]{0,1:T(8,128)}, u32[]{:S(2)}, u32[]{:S(2)}) collective-permute-start(f32[768,192]{0,1:T(8,128)} %convolution_bitcast_fusion), channel_id=1, source_target_pairs={{0,4},{4,0},{1,5},{5,1},{2,6},{6,2},{3,7},{7,3},{8,12},{12,8},{9,1... | collective-permute-start | bytes 1769480 | tf_op jit(solution)/shard_map/ppermute | solution.py:138
  169.8 53.1 %copy-start.7 = (bf16[1,768,512]{2,1,0:T(8,128)(2,1)S(1)}, bf16[1,768,512]{2,1,0:T(8,128)(2,1)}, u32[]{:S(2)}) copy-start(bf16[1,768,512]{2,1,0:T(8,128)(2,1)} %param.15) | copy-start | bytes 2359300
  220.0 18.6 %collective-permute-start.4 = (bf16[768,96]{0,1:T(8,128)(2,1)S(1)}, bf16[768,96]{0,1:T(8,128)(2,1)}, u32[]{:S(2)}, u32[]{:S(2)}) collective-permute-start(bf16[768,96]{0,1:T(8,128)(2,1)S(1)} %get-tuple-element.9), channel_id=1, source_target_pairs={{0,1},{1,2},{2,3},{3,4},{4,5},{5,6},{6,7},{7,0},{8,9},{9,10},{10,1... | collective-permute-start | bytes 442376 | tf_op jit(solution)/shard_map/ppermute | solution.py:72
  224.4 21.0 %collective-permute-start.5 = (bf16[768,96]{0,1:T(8,128)(2,1)S(1)}, bf16[768,96]{0,1:T(8,128)(2,1)S(1)}, u32[]{:S(2)}, u32[]{:S(2)}) collective-permute-start(bf16[768,96]{0,1:T(8,128)(2,1)S(1)} %get-tuple-element.9), channel_id=1, source_target_pairs={{0,2},{1,3},{2,4},{3,5},{4,6},{5,7},{6,0},{7,1},{8,10},{9,11},{10,... | collective-permute-start | bytes 442376 | tf_op jit(solution)/shard_map/ppermute | solution.py:72
  227.0 23.2 %collective-permute-start.6 = (bf16[768,96]{0,1:T(8,128)(2,1)S(1)}, bf16[768,96]{0,1:T(8,128)(2,1)S(1)}, u32[]{:S(2)}, u32[]{:S(2)}) collective-permute-start(bf16[768,96]{0,1:T(8,128)(2,1)S(1)} %get-tuple-element.9), channel_id=1, source_target_pairs={{0,3},{1,4},{2,5},{3,6},{4,7},{5,0},{6,1},{7,2},{8,11},{9,12},{10,... | collective-permute-start | bytes 442376 | tf_op jit(solution)/shard_map/ppermute | solution.py:72
  232.8 18.1 %collective-permute-start.7 = (bf16[768,96]{0,1:T(8,128)(2,1)S(1)}, bf16[768,96]{0,1:T(8,128)(2,1)S(1)}, u32[]{:S(2)}, u32[]{:S(2)}) collective-permute-start(bf16[768,96]{0,1:T(8,128)(2,1)S(1)} %get-tuple-element.9), channel_id=1, source_target_pairs={{0,4},{1,5},{2,6},{3,7},{4,0},{5,1},{6,2},{7,3},{8,12},{9,13},{10,... | collective-permute-start | bytes 442376 | tf_op jit(solution)/shard_map/ppermute | solution.py:72
  234.8 16.8 %collective-permute-start.8 = (bf16[768,96]{0,1:T(8,128)(2,1)S(1)}, bf16[768,96]{0,1:T(8,128)(2,1)S(1)}, u32[]{:S(2)}, u32[]{:S(2)}) collective-permute-start(bf16[768,96]{0,1:T(8,128)(2,1)S(1)} %get-tuple-element.9), channel_id=1, source_target_pairs={{0,5},{1,6},{2,7},{3,0},{4,1},{5,2},{6,3},{7,4},{8,13},{9,14},{10,... | collective-permute-start | bytes 442376 | tf_op jit(solution)/shard_map/ppermute | solution.py:72
  238.6 13.7 %collective-permute-start.9 = (bf16[768,96]{0,1:T(8,128)(2,1)S(1)}, bf16[768,96]{0,1:T(8,128)(2,1)S(1)}, u32[]{:S(2)}, u32[]{:S(2)}) collective-permute-start(bf16[768,96]{0,1:T(8,128)(2,1)S(1)} %get-tuple-element.9), channel_id=1, source_target_pairs={{0,6},{1,7},{2,0},{3,1},{4,2},{5,3},{6,4},{7,5},{8,14},{9,15},{10,... | collective-permute-start | bytes 442376 | tf_op jit(solution)/shard_map/ppermute | solution.py:72
  245.4 7.5 %collective-permute-start.10 = (bf16[768,96]{0,1:T(8,128)(2,1)S(1)}, bf16[768,96]{0,1:T(8,128)(2,1)S(1)}, u32[]{:S(2)}, u32[]{:S(2)}) collective-permute-start(bf16[768,96]{0,1:T(8,128)(2,1)S(1)} %get-tuple-element.9), channel_id=1, source_target_pairs={{0,7},{1,0},{2,1},{3,2},{4,3},{5,4},{6,5},{7,6},{8,15},{9,8},{10,9... | collective-permute-start | bytes 442376 | tf_op jit(solution)/shard_map/ppermute | solution.py:72
  255.9 15.2 %copy-start.10 = (bf16[48,8]{0,1:T(8,128)(2,1)S(1)}, bf16[48,8]{0,1:T(8,128)(2,1)}, u32[]{:S(2)}) copy-start(bf16[48,8]{0,1:T(8,128)(2,1)} %param.10) | copy-start | bytes 2308
  257.0 44.8 %all-to-all-start.2 = ((bf16[64,12,512]{2,1,0:T(8,128)(2,1)}), bf16[64,12,512]{2,1,0:T(8,128)(2,1)S(1)}, u32[]{:S(2)}, u32[]{:S(2)}) async-start(bf16[64,12,512]{2,1,0:T(8,128)(2,1)} %reshape.171), calls=%async_computation.2 | async-start | bytes 2097152 | tf_op jit(solution)/shard_map/all_to_all | solution.py:150
  274.2 1.5 copy-start.3
  274.5 2.8 copy-start.2
Sparse Core Ops, SparseCore 0:
  52.6 71.8 all-gather.2

commit v6 on v5

--- a/solution.py
+++ b/solution.py
@@ -121,8 +121,6 @@
     )
     slice_rows = first[:, :split_at].reshape(groups * capacity, narrow_width)
     spread = first[:, split_at:]
-    ordered = jnp.take(spread, partner, axis=0, mode="clip")
-    arrived = lax.all_to_all(ordered, "expert", split_axis=0, concat_axis=0, tiled=True)
 
     pieces, sources = ring_gather(slice_rows, "x", columns, column)
     keep3 = jnp.take(keep.reshape(keep.shape[0], columns, narrow_width), sources, axis=1, mode="clip")
@@ -146,11 +144,16 @@
         hidden_all, down3, (((0, 2), (0, 1)), ((), ())), preferred_element_type=jnp.float32
     ).astype(jnp.bfloat16)
 
-    produced, arrived = lax.optimization_barrier((produced, arrived))
-    returned = lax.all_to_all(
-        produced.reshape(groups, capacity, -1), "expert", split_axis=0, concat_axis=0, tiled=True
-    ).reshape(groups * capacity, narrow_width)
-    new_gate, new_up, new_down = unpack_weights(arrived, gate_block.shape, down_block.shape)
+    ordered = jnp.take(spread, partner, axis=0, mode="clip")
+    second = lax.all_to_all(
+        jnp.concatenate([to_lanes(produced, groups), ordered], axis=1),
+        "expert",
+        split_axis=0,
+        concat_axis=0,
+        tiled=True,
+    )
+    returned = second[:, :split_at].reshape(groups * capacity, narrow_width)
+    new_gate, new_up, new_down = unpack_weights(second[:, split_at:], gate_block.shape, down_block.shape)
     layer_out = jnp.dot(combine, returned, preferred_element_type=jnp.float32).astype(jnp.bfloat16)
     return (
         layer_out,

time: 311 us -> 362 us (1.16)
  the two profiles are of different devices: /device:TPU:16 before, /device:TPU:40 now
where the time goes in v6:
time: 362 us; the launch traced here: 361 us
  waiting for transfers between devices  187 us (52%)
  local copies, waits for them, and re-layouts  69.1 us (19%)
  starting transfers between devices  67.2 us (19%)
  between operations  14.5 us (4%)
  other arithmetic  11.9 us (3%)
  matrix products  11.8 us (3%)
    all_to_all x1, waiting for transfers between devices, body(): lax.all_to_all(jnp.concatenate([to_lanes(produced, groups), ordered], axi...  89.5 us
    all_to_all x1, waiting for transfers between devices, body(): lax.all_to_all(jnp.concatenate([token_lanes, packed], axis=1), 'expert',...  69.1 us
    ppermute x10, starting transfers between devices, ring_gather(): lax.ppermute(value, axis, [(i, (i + shift) % size) for i in range(size)])  34.6 us
    ppermute x10, waiting for transfers between devices, ring_gather(): lax.ppermute(value, axis, [(i, (i + shift) % size) for i in range(size)])  17.4 us
    all_to_all x1, starting transfers between devices, body(): lax.all_to_all(jnp.concatenate([token_lanes, packed], axis=1), 'expert',...  16.3 us
    all_to_all x1, starting transfers between devices, body(): lax.all_to_all(jnp.concatenate([to_lanes(produced, groups), ordered], axi...  14 us
    ppermute x1, waiting for transfers between devices, body(): back = lax.ppermute(other_part, 'zlo', pair)  10.6 us
    dynamic_slice x1, local copies, waits for them, and re-layouts, body(): lax.dynamic_index_in_dim(up_halves, half, axis=1, keepdims=False)  9.12 us
  transfers between devices with their start and end apart: 14, of which 7 were waited for; matrix products, arithmetic and copies ran while one was open for 13% of the time, Pallas kernels for 0%

profile of v6, /device:TPU:40, one launch (start us, length us, event | category | flops | bytes accessed | tf_op | source)
XLA Modules:
  0.0 361.0 jit_solution(27998851605444815)
XLA Ops:
  18.7 16.3 %all-to-all-start = ((bf16[64,192,128]{2,1,0:T(8,128)(2,1)}), bf16[64,192,128]{2,1,0:T(8,128)(2,1)S(1)}, u32[]{:S(2)}, u32[]{:S(2)}) async-start(bf16[64,192,128]{2,1,0:T(8,128)(2,1)} %pad_maximum_fusion), calls=%async_computation | async-start | bytes 6291456 | tf_op jit(solution)/shard_map/all_to_all | solution.py:115
  35.2 3.3 reshape_squeeze.21
  38.4 3.2 reshape_squeeze.22
  41.7 9.1 %dynamic-slice_reduce_fusion = (bf16[96,2048]{1,0:T(8,128)(2,1)}, bf16[96,1,2048]{2,1,0:T(2,128)(2,1)S(1)}, bf16[96,1,2048]{2,1,0:T(2,128)(2,1)S(1)}, bf16[96,2048]{1,0:T(8,128)(2,1)}) fusion(bf16[96,2,2048]{2,1,0:T(2,128)(2,1)} %reshape_squeeze.22, s32[]{:T(128)S(6)} %select_n.43, s32[]{:T(128)S(6)} %select_n.45, bf16[96,2,2048]{2,1,0:T(2,128)(2,1)} %reshape_squeeze.21), kind=kLoop, calls=%fused_computation.24 | loop fusion | bytes 3145736 | tf_op jit(solution)/shard_map/jit(dynamic_index_in_dim)/dynamic_slice | solution.py:96
  52.2 69.1 %all-to-all-done = bf16[64,192,128]{2,1,0:T(8,128)(2,1)S(1)} async-done(((bf16[64,192,128]{2,1,0:T(8,128)(2,1)}), bf16[64,192,128]{2,1,0:T(8,128)(2,1)S(1)}, u32[]{:S(2)}, u32[]{:S(2)}) %all-to-all-start) | async-done | bytes 3145760 | tf_op jit(solution)/shard_map/all_to_all | solution.py:115
  122.3 2.3 reshape.169
  126.5 5.8 %collective-permute-start.1 = (bf16[768,512]{1,0:T(8,128)(2,1)}, bf16[768,512]{1,0:T(8,128)(2,1)}, u32[]{:S(2)}, u32[]{:S(2)}) collective-permute-start(bf16[768,512]{1,0:T(8,128)(2,1)} %reshape.169), channel_id=1, source_target_pairs={{0,2},{1,3},{2,0},{3,1},{4,6},{5,7},{6,4},{7,5},{8,10},{9,11},{10,... | collective-permute-start | bytes 2359304 | tf_op jit(solution)/shard_map/ppermute | solution.py:72
  136.4 3.0 reshape.170
  139.3 2.2 copy.61
  141.5 2.6 gather_fusion.1
  144.1 2.3 stack_reshape.3
  146.3 2.7 collective-permute-done
  149.0 11.7 %collective-permute-done.1 = bf16[768,512]{1,0:T(8,128)(2,1)} collective-permute-done((bf16[768,512]{1,0:T(8,128)(2,1)}, bf16[768,512]{1,0:T(8,128)(2,1)}, u32[]{:S(2)}, u32[]{:S(2)}) %collective-permute-start.1) | collective-permute-done | bytes 786464 | tf_op jit(solution)/shard_map/ppermute | solution.py:72
  160.7 2.5 collective-permute-done.2
  163.2 4.2 %convolution_bitcast_fusion = f32[768,192]{0,1:T(8,128)} fusion(bf16[4,192,512]{2,1,0:T(8,128)(2,1)} %gather_fusion.1, bf16[1,768,512]{2,1,0:T(8,128)(2,1)} %bitcast.8, bf16[1,768,512]{2,1,0:T(8,128)(2,1)} %bitcast.7, bf16[1,768,512]{2,1,0:T(8,128)(2,1)} %bitcast.6, bf16[1,768,512]{2,1,0:T(8,128)(2,1)} %stack_reshape.3), kind=kOutput, calls=%fused_computation.10 | convolution fusion | flops 608698368 | bytes 4521984 | tf_op jit(solution)/shard_map/dot_general | solution.py:133
  170.5 2.6 gather_fusion
  173.2 10.6 %collective-permute-done.3 = f32[768,192]{0,1:T(8,128)} collective-permute-done((f32[768,192]{0,1:T(8,128)}, f32[768,192]{0,1:T(8,128)}, u32[]{:S(2)}, u32[]{:S(2)}) %collective-permute-start.3) | collective-permute-done | bytes 589856 | tf_op jit(solution)/shard_map/ppermute | solution.py:136
  183.8 3.4 fusion
  188.0 4.6 %collective-permute-start.4 = (bf16[768,96]{0,1:T(8,128)(2,1)S(1)}, bf16[768,96]{0,1:T(8,128)(2,1)}, u32[]{:S(2)}, u32[]{:S(2)}) collective-permute-start(bf16[768,96]{0,1:T(8,128)(2,1)S(1)} %get-tuple-element.5), channel_id=1, source_target_pairs={{0,1},{1,2},{2,3},{3,4},{4,5},{5,6},{6,7},{7,0},{8,9},{9,10},{10,1... | collective-permute-start | bytes 442376 | tf_op jit(solution)/shard_map/ppermute | solution.py:72
  192.6 2.6 gather_fusion.2
  196.8 2.7 gather_fusion.3
  199.6 4.3 %collective-permute-start.5 = (bf16[768,96]{0,1:T(8,128)(2,1)S(1)}, bf16[768,96]{0,1:T(8,128)(2,1)S(1)}, u32[]{:S(2)}, u32[]{:S(2)}) collective-permute-start(bf16[768,96]{0,1:T(8,128)(2,1)S(1)} %get-tuple-element.5), channel_id=1, source_target_pairs={{0,2},{1,3},{2,4},{3,5},{4,6},{5,7},{6,0},{7,1},{8,10},{9,11},{10,... | collective-permute-start | bytes 442376 | tf_op jit(solution)/shard_map/ppermute | solution.py:72
  205.9 3.6 %collective-permute-start.7 = (bf16[768,96]{0,1:T(8,128)(2,1)S(1)}, bf16[768,96]{0,1:T(8,128)(2,1)S(1)}, u32[]{:S(2)}, u32[]{:S(2)}) collective-permute-start(bf16[768,96]{0,1:T(8,128)(2,1)S(1)} %get-tuple-element.5), channel_id=1, source_target_pairs={{0,4},{1,5},{2,6},{3,7},{4,0},{5,1},{6,2},{7,3},{8,12},{9,13},{10,... | collective-permute-start | bytes 442376 | tf_op jit(solution)/shard_map/ppermute | solution.py:72
  209.5 3.4 collective-permute-start.8
  212.9 3.9 %collective-permute-start.9 = (bf16[768,96]{0,1:T(8,128)(2,1)S(1)}, bf16[768,96]{0,1:T(8,128)(2,1)S(1)}, u32[]{:S(2)}, u32[]{:S(2)}) collective-permute-start(bf16[768,96]{0,1:T(8,128)(2,1)S(1)} %get-tuple-element.5), channel_id=1, source_target_pairs={{0,6},{1,7},{2,0},{3,1},{4,2},{5,3},{6,4},{7,5},{8,14},{9,15},{10,... | collective-permute-start | bytes 442376 | tf_op jit(solution)/shard_map/ppermute | solution.py:72
  218.4 3.1 collective-permute-start.10
  226.1 3.0 bitcast_convert_fusion
  232.7 14.0 %all-to-all-start.1 = ((bf16[64,192,128]{2,1,0:T(8,128)(2,1)}), bf16[64,192,128]{2,1,0:T(8,128)(2,1)S(1)}, u32[]{:S(2)}, u32[]{:S(2)}) async-start(bf16[64,192,128]{2,1,0:T(8,128)(2,1)} %pad_maximum_fusion.2), calls=%async_computation.1 | async-start | bytes 6291456 | tf_op jit(solution)/shard_map/all_to_all | solution.py:148
  247.3 89.5 %all-to-all-done.1 = bf16[64,192,128]{2,1,0:T(8,128)(2,1)S(1)} async-done(((bf16[64,192,128]{2,1,0:T(8,128)(2,1)}), bf16[64,192,128]{2,1,0:T(8,128)(2,1)S(1)}, u32[]{:S(2)}, u32[]{:S(2)}) %all-to-all-start.1) | async-done | bytes 3145760 | tf_op jit(solution)/shard_map/all_to_all | solution.py:148
  341.5 2.4 copy.64
  344.0 2.3 reshape_reshape.11
  346.3 2.3 copy.62
  (88 shorter events, 48.0 us)
Async XLA Ops:
  7.2 5.9 %copy-start = (bf16[48,512]{1,0:T(8,128)(2,1)S(1)}, bf16[48,512]{1,0:T(8,128)(2,1)}, u32[]{:S(2)}) copy-start(bf16[48,512]{1,0:T(8,128)(2,1)} %param.8) | copy-start | bytes 147460
  7.2 6.7 %copy-start.3 = (bf16[1,768,512]{2,1,0:T(8,128)(2,1)S(1)}, bf16[1,768,512]{2,1,0:T(8,128)(2,1)}, u32[]{:S(2)}) copy-start(bf16[1,768,512]{2,1,0:T(8,128)(2,1)} %param.15) | copy-start | bytes 2359300
  13.9 1.1 copy-start.1
  14.1 1.2 copy-start.2
  18.7 102.7 %all-to-all-start = ((bf16[64,192,128]{2,1,0:T(8,128)(2,1)}), bf16[64,192,128]{2,1,0:T(8,128)(2,1)S(1)}, u32[]{:S(2)}, u32[]{:S(2)}) async-start(bf16[64,192,128]{2,1,0:T(8,128)(2,1)} %pad_maximum_fusion), calls=%async_computation | async-start | bytes 6291456 | tf_op jit(solution)/shard_map/all_to_all | solution.py:115
  34.9 99.3 %all-gather.3.cloned.1.call-start = ((), (), s32[]{:S(2)}) async-start(), calls=%async_computation.2 | async-start | bytes 2359296 | tf_op jit(solution)/shard_map/all_gather | solution.py:107
  124.6 24.4 %collective-permute-start = (bf16[768,512]{1,0:T(8,128)(2,1)}, bf16[768,512]{1,0:T(8,128)(2,1)}, u32[]{:S(2)}, u32[]{:S(2)}) collective-permute-start(bf16[768,512]{1,0:T(8,128)(2,1)} %reshape.169), channel_id=1, source_target_pairs={{0,1},{1,2},{2,3},{3,0},{4,5},{5,6},{6,7},{7,4},{8,9},{9,10},{10,1... | collective-permute-start | bytes 2359304 | tf_op jit(solution)/shard_map/ppermute | solution.py:72
  126.5 34.3 %collective-permute-start.1 = (bf16[768,512]{1,0:T(8,128)(2,1)}, bf16[768,512]{1,0:T(8,128)(2,1)}, u32[]{:S(2)}, u32[]{:S(2)}) collective-permute-start(bf16[768,512]{1,0:T(8,128)(2,1)} %reshape.169), channel_id=1, source_target_pairs={{0,2},{1,3},{2,0},{3,1},{4,6},{5,7},{6,4},{7,5},{8,10},{9,11},{10,... | collective-permute-start | bytes 2359304 | tf_op jit(solution)/shard_map/ppermute | solution.py:72
  132.3 31.0 %collective-permute-start.2 = (bf16[768,512]{1,0:T(8,128)(2,1)}, bf16[768,512]{1,0:T(8,128)(2,1)}, u32[]{:S(2)}, u32[]{:S(2)}) collective-permute-start(bf16[768,512]{1,0:T(8,128)(2,1)} %reshape.169), channel_id=1, source_target_pairs={{0,3},{1,0},{2,1},{3,2},{4,7},{5,4},{6,5},{7,6},{8,11},{9,8},{10,9... | collective-permute-start | bytes 2359304 | tf_op jit(solution)/shard_map/ppermute | solution.py:72
  163.2 6.3 %copy-start.5 = (bf16[96,2048]{1,0:T(8,128)(2,1)S(1)}, bf16[96,2048]{1,0:T(8,128)(2,1)}, u32[]{:S(2)}) copy-start(bf16[96,2048]{1,0:T(8,128)(2,1)} %get-tuple-element.11) | copy-start | bytes 1179652
  163.2 6.3 %copy-start.4 = (bf16[96,2048]{1,0:T(8,128)(2,1)S(1)}, bf16[96,2048]{1,0:T(8,128)(2,1)}, u32[]{:S(2)}) copy-start(bf16[96,2048]{1,0:T(8,128)(2,1)} %get-tuple-element.14) | copy-start | bytes 1179652
  167.4 16.4 %collective-permute-start.3 = (f32[768,192]{0,1:T(8,128)}, f32[768,192]{0,1:T(8,128)}, u32[]{:S(2)}, u32[]{:S(2)}) collective-permute-start(f32[768,192]{0,1:T(8,128)} %convolution_bitcast_fusion), channel_id=1, source_target_pairs={{0,4},{4,0},{1,5},{5,1},{2,6},{6,2},{3,7},{7,3},{8,12},{12,8},{9,1... | collective-permute-start | bytes 1769480 | tf_op jit(solution)/shard_map/ppermute | solution.py:136
  187.2 8.0 %copy-start.8 = (s32[64]{0:T(128)S(1)}, s32[64]{0:T(128)}, u32[]{:S(2)}) copy-start(s32[64]{0:T(128)} %param.11) | copy-start | bytes 772
  188.0 24.9 %collective-permute-start.4 = (bf16[768,96]{0,1:T(8,128)(2,1)S(1)}, bf16[768,96]{0,1:T(8,128)(2,1)}, u32[]{:S(2)}, u32[]{:S(2)}) collective-permute-start(bf16[768,96]{0,1:T(8,128)(2,1)S(1)} %get-tuple-element.5), channel_id=1, source_target_pairs={{0,1},{1,2},{2,3},{3,4},{4,5},{5,6},{6,7},{7,0},{8,9},{9,10},{10,1... | collective-permute-start | bytes 442376 | tf_op jit(solution)/shard_map/ppermute | solution.py:72
  196.8 29.3 %copy-start.6 = (bf16[8,96,512]{2,1,0:T(8,128)(2,1)S(1)}, bf16[8,96,512]{2,1,0:T(8,128)(2,1)}, u32[]{:S(2)}) copy-start(bf16[8,96,512]{2,1,0:T(8,128)(2,1)} %gather_fusion.2) | copy-start | bytes 2359300
  199.6 18.8 %collective-permute-start.5 = (bf16[768,96]{0,1:T(8,128)(2,1)S(1)}, bf16[768,96]{0,1:T(8,128)(2,1)S(1)}, u32[]{:S(2)}, u32[]{:S(2)}) collective-permute-start(bf16[768,96]{0,1:T(8,128)(2,1)S(1)} %get-tuple-element.5), channel_id=1, source_target_pairs={{0,2},{1,3},{2,4},{3,5},{4,6},{5,7},{6,0},{7,1},{8,10},{9,11},{10,... | collective-permute-start | bytes 442376 | tf_op jit(solution)/shard_map/ppermute | solution.py:72
  203.9 18.3 %collective-permute-start.6 = (bf16[768,96]{0,1:T(8,128)(2,1)S(1)}, bf16[768,96]{0,1:T(8,128)(2,1)S(1)}, u32[]{:S(2)}, u32[]{:S(2)}) collective-permute-start(bf16[768,96]{0,1:T(8,128)(2,1)S(1)} %get-tuple-element.5), channel_id=1, source_target_pairs={{0,3},{1,4},{2,5},{3,6},{4,7},{5,0},{6,1},{7,2},{8,11},{9,12},{10,... | collective-permute-start | bytes 442376 | tf_op jit(solution)/shard_map/ppermute | solution.py:72
  205.9 17.0 %collective-permute-start.7 = (bf16[768,96]{0,1:T(8,128)(2,1)S(1)}, bf16[768,96]{0,1:T(8,128)(2,1)S(1)}, u32[]{:S(2)}, u32[]{:S(2)}) collective-permute-start(bf16[768,96]{0,1:T(8,128)(2,1)S(1)} %get-tuple-element.5), channel_id=1, source_target_pairs={{0,4},{1,5},{2,6},{3,7},{4,0},{5,1},{6,2},{7,3},{8,12},{9,13},{10,... | collective-permute-start | bytes 442376 | tf_op jit(solution)/shard_map/ppermute | solution.py:72
  209.5 14.1 %collective-permute-start.8 = (bf16[768,96]{0,1:T(8,128)(2,1)S(1)}, bf16[768,96]{0,1:T(8,128)(2,1)S(1)}, u32[]{:S(2)}, u32[]{:S(2)}) collective-permute-start(bf16[768,96]{0,1:T(8,128)(2,1)S(1)} %get-tuple-element.5), channel_id=1, source_target_pairs={{0,5},{1,6},{2,7},{3,0},{4,1},{5,2},{6,3},{7,4},{8,13},{9,14},{10,... | collective-permute-start | bytes 442376 | tf_op jit(solution)/shard_map/ppermute | solution.py:72
  212.9 11.3 %collective-permute-start.9 = (bf16[768,96]{0,1:T(8,128)(2,1)S(1)}, bf16[768,96]{0,1:T(8,128)(2,1)S(1)}, u32[]{:S(2)}, u32[]{:S(2)}) collective-permute-start(bf16[768,96]{0,1:T(8,128)(2,1)S(1)} %get-tuple-element.5), channel_id=1, source_target_pairs={{0,6},{1,7},{2,0},{3,1},{4,2},{5,3},{6,4},{7,5},{8,14},{9,15},{10,... | collective-permute-start | bytes 442376 | tf_op jit(solution)/shard_map/ppermute | solution.py:72
  218.4 7.0 %collective-permute-start.10 = (bf16[768,96]{0,1:T(8,128)(2,1)S(1)}, bf16[768,96]{0,1:T(8,128)(2,1)S(1)}, u32[]{:S(2)}, u32[]{:S(2)}) collective-permute-start(bf16[768,96]{0,1:T(8,128)(2,1)S(1)} %get-tuple-element.5), channel_id=1, source_target_pairs={{0,7},{1,0},{2,1},{3,2},{4,3},{5,4},{6,5},{7,6},{8,15},{9,8},{10,9... | collective-permute-start | bytes 442376 | tf_op jit(solution)/shard_map/ppermute | solution.py:72
  232.7 14.0 %copy-start.7 = (bf16[48,8]{0,1:T(8,128)(2,1)S(1)}, bf16[48,8]{0,1:T(8,128)(2,1)}, u32[]{:S(2)}) copy-start(bf16[48,8]{0,1:T(8,128)(2,1)} %param.10) | copy-start | bytes 2308
  232.7 104.0 %all-to-all-start.1 = ((bf16[64,192,128]{2,1,0:T(8,128)(2,1)}), bf16[64,192,128]{2,1,0:T(8,128)(2,1)S(1)}, u32[]{:S(2)}, u32[]{:S(2)}) async-start(bf16[64,192,128]{2,1,0:T(8,128)(2,1)} %pad_maximum_fusion.2), calls=%async_computation.1 | async-start | bytes 6291456 | tf_op jit(solution)/shard_map/all_to_all | solution.py:148
Sparse Core Ops, SparseCore 0:
  52.3 71.6 all-gather.2

commit v7 on v5

--- a/solution.py
+++ b/solution.py
@@ -104,8 +104,7 @@
         ],
         axis=0,
     )
-    both = lax.all_gather(give, "zlo", axis=0, tiled=False)
-    taken = lax.dynamic_index_in_dim(both, 1 - half, axis=0, keepdims=False)
+    taken = lax.ppermute(give, "zlo", pair)
 
     dispatch, combine, capacity = slot_layout(route_ids, route_weight, old_place, groups)
     outgoing = jnp.dot(dispatch, tokens, preferred_element_type=jnp.float32).astype(jnp.bfloat16)

time: 311 us -> 299 us (0.961)
  between operations: 14.5 us -> 1.14 us
  starting transfers between devices: 91.4 us -> 97.1 us
  local copies, waits for them, and re-layouts: 57.1 us -> 52.1 us
    ppermute x1, waiting for transfers between devices: 46 us -> 49.8 us  [body(): back = lax.ppermute(other_part, 'zlo', pair)]
    ppermute x0 -> x1, starting transfers between devices: none -> 3.38 us  [body(): taken = lax.ppermute(give, 'zlo', pair)]
  transfers between devices with their start and end apart: 15 -> 15, of which waited for: 3 -> 3; matrix products, arithmetic and copies ran while one was open for 21% -> 20% of each run, Pallas kernels for 0% -> 0%
where the time goes in v7:
time: 299 us; the launch traced here: 298 us
  waiting for transfers between devices  127 us (42%)
  starting transfers between devices  97.1 us (32%)
  local copies, waits for them, and re-layouts  52.1 us (17%)
  matrix products  11.1 us (4%)
  other arithmetic  9.64 us (3%)
    all_to_all x1, waiting for transfers between devices, body(): lax.all_to_all(jnp.concatenate([token_lanes, packed], axis=1), 'expert',...  54.1 us
    ppermute x1, waiting for transfers between devices, body(): back = lax.ppermute(other_part, 'zlo', pair)  49.8 us
    ppermute x10, starting transfers between devices, ring_gather(): lax.ppermute(value, axis, [(i, (i + shift) % size) for i in range(size)])  38.8 us
    all_to_all x1, waiting for transfers between devices, body(): lax.all_to_all(produced.reshape(groups, capacity, -1), 'expert', split_ax...  23 us
    all_to_all x1, starting transfers between devices, body(): lax.all_to_all(ordered, 'expert', split_axis=0, concat_axis=0, tiled=True)  22.1 us
    all_to_all x1, starting transfers between devices, body(): lax.all_to_all(jnp.concatenate([token_lanes, packed], axis=1), 'expert',...  16.5 us
    all_to_all x1, starting transfers between devices, body(): lax.all_to_all(produced.reshape(groups, capacity, -1), 'expert', split_ax...  14.3 us
    dynamic_slice x1, local copies, waits for them, and re-layouts, body(): lax.dynamic_index_in_dim(up_halves, half, axis=1, keepdims=False)  9.38 us
  transfers between devices with their start and end apart: 15, of which 3 were waited for; matrix products, arithmetic and copies ran while one was open for 20% of the time, Pallas kernels for 0%

profile of v7, /device:TPU:16, one launch (start us, length us, event | category | flops | bytes accessed | tf_op | source)
XLA Modules:
  0.0 298.1 jit_solution(938613712619898470)
XLA Ops:
  1.7 1.6 select_reduce_fusion
  10.1 2.1 pad_maximum_fusion
  12.1 16.5 %all-to-all-start = ((bf16[64,192,128]{2,1,0:T(8,128)(2,1)}), bf16[64,192,128]{2,1,0:T(8,128)(2,1)S(1)}, u32[]{:S(2)}, u32[]{:S(2)}) async-start(bf16[64,192,128]{2,1,0:T(8,128)(2,1)} %pad_maximum_fusion), calls=%async_computation | async-start | bytes 6291456 | tf_op jit(solution)/shard_map/all_to_all | solution.py:114
  28.6 3.3 %reshape_squeeze.21 = bf16[96,2,2048]{2,1,0:T(2,128)(2,1)} reshape(bf16[1,96,4096]{2,1,0:T(8,128)(2,1)} %param.13) | data formatting | bytes 1572864 | tf_op jit(solution)/shard_map/reshape;squeeze | solution.py:91
  31.9 3.2 %reshape_squeeze.22 = bf16[96,2,2048]{2,1,0:T(2,128)(2,1)} reshape(bf16[1,96,4096]{2,1,0:T(8,128)(2,1)} %param.14) | data formatting | bytes 1572864 | tf_op jit(solution)/shard_map/reshape;squeeze | solution.py:92
  35.1 9.4 %dynamic-slice_reduce_fusion = (bf16[96,2048]{1,0:T(8,128)(2,1)}, bf16[96,1,2048]{2,1,0:T(2,128)(2,1)S(1)}, bf16[96,1,2048]{2,1,0:T(2,128)(2,1)S(1)}, bf16[96,2048]{1,0:T(8,128)(2,1)}) fusion(bf16[96,2,2048]{2,1,0:T(2,128)(2,1)} %reshape_squeeze.22, s32[]{:T(128)S(6)} %select_n.41, s32[]{:T(128)S(6)} %select_n.43, bf16[96,2,2048]{2,1,0:T(2,128)(2,1)} %reshape_squeeze.21), kind=kLoop, calls=%fused_computation.24 | loop fusion | bytes 3145736 | tf_op jit(solution)/shard_map/jit(dynamic_index_in_dim)/dynamic_slice | solution.py:96
  45.9 3.4 %collective-permute-start.3 = (bf16[192,2048]{1,0:T(8,128)(2,1)}, bf16[192,2048]{1,0:T(8,128)(2,1)}, u32[]{:S(2)}, u32[]{:S(2)}) collective-permute-start(bf16[192,2048]{1,0:T(8,128)(2,1)} %pad_maximum_fusion.4), channel_id=1, source_target_pairs={{0,4},{4,0},{1,5},{5,1},{2,6},{6,2},{3,7},{7,3},{8,12},{12,8},{9,1... | collective-permute-start | bytes 2359304 | tf_op jit(solution)/shard_map/ppermute | solution.py:107
  49.3 54.1 %all-to-all-done = bf16[64,192,128]{2,1,0:T(8,128)(2,1)S(1)} async-done(((bf16[64,192,128]{2,1,0:T(8,128)(2,1)}), bf16[64,192,128]{2,1,0:T(8,128)(2,1)S(1)}, u32[]{:S(2)}, u32[]{:S(2)}) %all-to-all-start) | async-done | bytes 3145760 | tf_op jit(solution)/shard_map/all_to_all | solution.py:114
  104.4 2.3 reshape.168
  106.7 3.9 %collective-permute-start = (bf16[768,512]{1,0:T(8,128)(2,1)}, bf16[768,512]{1,0:T(8,128)(2,1)}, u32[]{:S(2)}, u32[]{:S(2)}) collective-permute-start(bf16[768,512]{1,0:T(8,128)(2,1)} %reshape.168), channel_id=1, source_target_pairs={{0,1},{1,2},{2,3},{3,0},{4,5},{5,6},{6,7},{7,4},{8,9},{9,10},{10,1... | collective-permute-start | bytes 2359304 | tf_op jit(solution)/shard_map/ppermute | solution.py:72
  110.6 5.1 %collective-permute-start.1 = (bf16[768,512]{1,0:T(8,128)(2,1)}, bf16[768,512]{1,0:T(8,128)(2,1)}, u32[]{:S(2)}, u32[]{:S(2)}) collective-permute-start(bf16[768,512]{1,0:T(8,128)(2,1)} %reshape.168), channel_id=1, source_target_pairs={{0,2},{1,3},{2,0},{3,1},{4,6},{5,7},{6,4},{7,5},{8,10},{9,11},{10,... | collective-permute-start | bytes 2359304 | tf_op jit(solution)/shard_map/ppermute | solution.py:72
  115.8 3.3 %collective-permute-start.2 = (bf16[768,512]{1,0:T(8,128)(2,1)}, bf16[768,512]{1,0:T(8,128)(2,1)}, u32[]{:S(2)}, u32[]{:S(2)}) collective-permute-start(bf16[768,512]{1,0:T(8,128)(2,1)} %reshape.168), channel_id=1, source_target_pairs={{0,3},{1,0},{2,1},{3,2},{4,7},{5,4},{6,5},{7,6},{8,11},{9,8},{10,9... | collective-permute-start | bytes 2359304 | tf_op jit(solution)/shard_map/ppermute | solution.py:72
  119.1 1.6 slice.48
  120.7 3.9 %gather_fusion.3 = bf16[64,144,128]{2,1,0:T(8,128)(2,1)} fusion(bf16[64,144,128]{2,1,0:T(8,128)(2,1)} %slice.48, s32[1024]{0:T(1024)S(1)} %pad_clamp_fusion), kind=kCustom, calls=%fused_computation.3 | custom fusion | bytes 4718848 | tf_op jit(solution)/shard_map/jit(_take)/gather | solution.py:123
  124.6 22.1 %all-to-all-start.1 = ((bf16[64,144,128]{2,1,0:T(8,128)(2,1)}), bf16[64,144,128]{2,1,0:T(8,128)(2,1)S(1)}, u32[]{:S(2)}, u32[]{:S(2)}) async-start(bf16[64,144,128]{2,1,0:T(8,128)(2,1)} %gather_fusion.3), calls=%async_computation.1 | async-start | bytes 4718592 | tf_op jit(solution)/shard_map/all_to_all | solution.py:124
  146.8 2.1 copy.79
  148.9 2.6 gather_fusion.1
  152.9 4.2 %convolution_bitcast_fusion = f32[768,192]{0,1:T(8,128)} fusion(bf16[4,192,512]{2,1,0:T(8,128)(2,1)} %gather_fusion.1, bf16[1,768,512]{2,1,0:T(8,128)(2,1)} %bitcast.8, bf16[1,768,512]{2,1,0:T(8,128)(2,1)} %bitcast.7, bf16[1,768,512]{2,1,0:T(8,128)(2,1)} %bitcast.6, bf16[1,768,512]{2,1,0:T(8,128)(2,1)} %stack_reshape.3), kind=kOutput, calls=%fused_computation.9 | convolution fusion | flops 608698368 | bytes 4521984 | tf_op jit(solution)/shard_map/dot_general | solution.py:134
  157.1 2.1 collective-permute-start.4
  160.8 49.8 %collective-permute-done.4 = f32[768,192]{0,1:T(8,128)} collective-permute-done((f32[768,192]{0,1:T(8,128)}, f32[768,192]{0,1:T(8,128)}, u32[]{:S(2)}, u32[]{:S(2)}) %collective-permute-start.4) | collective-permute-done | bytes 589856 | tf_op jit(solution)/shard_map/ppermute | solution.py:137
  210.6 3.4 %fusion = f32[768,192]{0,1:T(8,128)S(1)} fusion(f32[768,192]{0,1:T(8,128)} %collective-permute-done.4, bf16[4,192,512]{2,1,0:T(8,128)(2,1)} %gather_fusion, bf16[1,768,512]{2,1,0:T(8,128)(2,1)} %bitcast.8, bf16[1,768,512]{2,1,0:T(8,128)(2,1)} %bitcast.7, bf16[1,768,512]{2,1,0:T(8,128)(2,1)} %bitcast.6, bf16[1,768,512]{2,1,0:T(8,128)(2,1)} %stack_reshape.3), kind=kOutput, calls=%fused_computation.11 | convolution fusion | flops 608845824 | bytes 5111808 | tf_op jit(solution)/shard_map/dot_general | solution.py:131
  214.8 2.5 collective-permute-start.5
  218.9 3.5 %collective-permute-start.6 = (bf16[768,96]{0,1:T(8,128)(2,1)S(1)}, bf16[768,96]{0,1:T(8,128)(2,1)S(1)}, u32[]{:S(2)}, u32[]{:S(2)}) collective-permute-start(bf16[768,96]{0,1:T(8,128)(2,1)S(1)} %get-tuple-element.9), channel_id=1, source_target_pairs={{0,2},{1,3},{2,4},{3,5},{4,6},{5,7},{6,0},{7,1},{8,10},{9,11},{10,... | collective-permute-start | bytes 442376 | tf_op jit(solution)/shard_map/ppermute | solution.py:72
  222.4 5.8 %collective-permute-start.7 = (bf16[768,96]{0,1:T(8,128)(2,1)S(1)}, bf16[768,96]{0,1:T(8,128)(2,1)S(1)}, u32[]{:S(2)}, u32[]{:S(2)}) collective-permute-start(bf16[768,96]{0,1:T(8,128)(2,1)S(1)} %get-tuple-element.9), channel_id=1, source_target_pairs={{0,3},{1,4},{2,5},{3,6},{4,7},{5,0},{6,1},{7,2},{8,11},{9,12},{10,... | collective-permute-start | bytes 442376 | tf_op jit(solution)/shard_map/ppermute | solution.py:72
  228.2 1.9 collective-permute-start.8
  230.1 3.5 %collective-permute-start.9 = (bf16[768,96]{0,1:T(8,128)(2,1)S(1)}, bf16[768,96]{0,1:T(8,128)(2,1)S(1)}, u32[]{:S(2)}, u32[]{:S(2)}) collective-permute-start(bf16[768,96]{0,1:T(8,128)(2,1)S(1)} %get-tuple-element.9), channel_id=1, source_target_pairs={{0,5},{1,6},{2,7},{3,0},{4,1},{5,2},{6,3},{7,4},{8,13},{9,14},{10,... | collective-permute-start | bytes 442376 | tf_op jit(solution)/shard_map/ppermute | solution.py:72
  233.6 4.7 %collective-permute-start.10 = (bf16[768,96]{0,1:T(8,128)(2,1)S(1)}, bf16[768,96]{0,1:T(8,128)(2,1)S(1)}, u32[]{:S(2)}, u32[]{:S(2)}) collective-permute-start(bf16[768,96]{0,1:T(8,128)(2,1)S(1)} %get-tuple-element.9), channel_id=1, source_target_pairs={{0,6},{1,7},{2,0},{3,1},{4,2},{5,3},{6,4},{7,5},{8,14},{9,15},{10,... | collective-permute-start | bytes 442376 | tf_op jit(solution)/shard_map/ppermute | solution.py:72
  238.3 1.6 bitcast_dynamic-update-slice_fusion.6
  239.9 4.5 %collective-permute-start.11 = (bf16[768,96]{0,1:T(8,128)(2,1)S(1)}, bf16[768,96]{0,1:T(8,128)(2,1)S(1)}, u32[]{:S(2)}, u32[]{:S(2)}) collective-permute-start(bf16[768,96]{0,1:T(8,128)(2,1)S(1)} %get-tuple-element.9), channel_id=1, source_target_pairs={{0,7},{1,0},{2,1},{3,2},{4,3},{5,4},{6,5},{7,6},{8,15},{9,8},{10,9... | collective-permute-start | bytes 442376 | tf_op jit(solution)/shard_map/ppermute | solution.py:72
  248.4 2.3 bitcast_convert_fusion
  251.9 14.3 %all-to-all-start.2 = ((bf16[64,12,512]{2,1,0:T(8,128)(2,1)}), bf16[64,12,512]{2,1,0:T(8,128)(2,1)S(1)}, u32[]{:S(2)}, u32[]{:S(2)}) async-start(bf16[64,12,512]{2,1,0:T(8,128)(2,1)} %reshape.170), calls=%async_computation.2 | async-start | bytes 2097152 | tf_op jit(solution)/shard_map/all_to_all | solution.py:149
  274.0 23.0 %all-to-all-done.2 = bf16[64,12,512]{2,1,0:T(8,128)(2,1)S(1)} async-done(((bf16[64,12,512]{2,1,0:T(8,128)(2,1)}), bf16[64,12,512]{2,1,0:T(8,128)(2,1)S(1)}, u32[]{:S(2)}, u32[]{:S(2)}) %all-to-all-start.2) | async-done | bytes 786464 | tf_op jit(solution)/shard_map/all_to_all | solution.py:149
  (90 shorter events, 29.3 us)
Async XLA Ops:
  0.6 5.9 %copy-start = (bf16[48,512]{1,0:T(8,128)(2,1)S(1)}, bf16[48,512]{1,0:T(8,128)(2,1)}, u32[]{:S(2)}) copy-start(bf16[48,512]{1,0:T(8,128)(2,1)} %param.8) | copy-start | bytes 147460
  0.6 6.8 %copy-start.6 = (bf16[1,768,512]{2,1,0:T(8,128)(2,1)S(1)}, bf16[1,768,512]{2,1,0:T(8,128)(2,1)}, u32[]{:S(2)}) copy-start(bf16[1,768,512]{2,1,0:T(8,128)(2,1)} %param.15) | copy-start | bytes 2359300
  7.4 1.1 copy-start.4
  7.6 1.2 copy-start.5
  12.1 91.3 %all-to-all-start = ((bf16[64,192,128]{2,1,0:T(8,128)(2,1)}), bf16[64,192,128]{2,1,0:T(8,128)(2,1)S(1)}, u32[]{:S(2)}, u32[]{:S(2)}) async-start(bf16[64,192,128]{2,1,0:T(8,128)(2,1)} %pad_maximum_fusion), calls=%async_computation | async-start | bytes 6291456 | tf_op jit(solution)/shard_map/all_to_all | solution.py:114
  45.0 74.1 %copy-start.11 = (s32[64]{0:T(128)S(1)}, s32[64]{0:T(128)}, u32[]{:S(2)}) copy-start(s32[64]{0:T(128)} %param.11) | copy-start | bytes 772
  45.9 100.8 %collective-permute-start.3 = (bf16[192,2048]{1,0:T(8,128)(2,1)}, bf16[192,2048]{1,0:T(8,128)(2,1)}, u32[]{:S(2)}, u32[]{:S(2)}) collective-permute-start(bf16[192,2048]{1,0:T(8,128)(2,1)} %pad_maximum_fusion.4), channel_id=1, source_target_pairs={{0,4},{4,0},{1,5},{5,1},{2,6},{6,2},{3,7},{7,3},{8,12},{12,8},{9,1... | collective-permute-start | bytes 2359304 | tf_op jit(solution)/shard_map/ppermute | solution.py:107
  106.7 46.2 %collective-permute-start = (bf16[768,512]{1,0:T(8,128)(2,1)}, bf16[768,512]{1,0:T(8,128)(2,1)}, u32[]{:S(2)}, u32[]{:S(2)}) collective-permute-start(bf16[768,512]{1,0:T(8,128)(2,1)} %reshape.168), channel_id=1, source_target_pairs={{0,1},{1,2},{2,3},{3,0},{4,5},{5,6},{6,7},{7,4},{8,9},{9,10},{10,1... | collective-permute-start | bytes 2359304 | tf_op jit(solution)/shard_map/ppermute | solution.py:72
  110.6 42.2 %collective-permute-start.1 = (bf16[768,512]{1,0:T(8,128)(2,1)}, bf16[768,512]{1,0:T(8,128)(2,1)}, u32[]{:S(2)}, u32[]{:S(2)}) collective-permute-start(bf16[768,512]{1,0:T(8,128)(2,1)} %reshape.168), channel_id=1, source_target_pairs={{0,2},{1,3},{2,0},{3,1},{4,6},{5,7},{6,4},{7,5},{8,10},{9,11},{10,... | collective-permute-start | bytes 2359304 | tf_op jit(solution)/shard_map/ppermute | solution.py:72
  115.8 37.1 %collective-permute-start.2 = (bf16[768,512]{1,0:T(8,128)(2,1)}, bf16[768,512]{1,0:T(8,128)(2,1)}, u32[]{:S(2)}, u32[]{:S(2)}) collective-permute-start(bf16[768,512]{1,0:T(8,128)(2,1)} %reshape.168), channel_id=1, source_target_pairs={{0,3},{1,0},{2,1},{3,2},{4,7},{5,4},{6,5},{7,6},{8,11},{9,8},{10,9... | collective-permute-start | bytes 2359304 | tf_op jit(solution)/shard_map/ppermute | solution.py:72
  124.6 126.1 %all-to-all-start.1 = ((bf16[64,144,128]{2,1,0:T(8,128)(2,1)}), bf16[64,144,128]{2,1,0:T(8,128)(2,1)S(1)}, u32[]{:S(2)}, u32[]{:S(2)}) async-start(bf16[64,144,128]{2,1,0:T(8,128)(2,1)} %gather_fusion.3), calls=%async_computation.1 | async-start | bytes 4718592 | tf_op jit(solution)/shard_map/all_to_all | solution.py:124
  146.7 4.8 %copy-start.1 = (bf16[64,48,128]{2,1,0:T(8,128)(2,1)S(1)}, bf16[64,48,128]{2,1,0:T(8,128)(2,1)}, u32[]{:S(2)}) copy-start(bf16[64,48,128]{2,1,0:T(8,128)(2,1)} %slice.45) | copy-start | bytes 2359300
  152.9 6.3 %copy-start.9 = (bf16[96,2048]{1,0:T(8,128)(2,1)S(1)}, bf16[96,2048]{1,0:T(8,128)(2,1)}, u32[]{:S(2)}) copy-start(bf16[96,2048]{1,0:T(8,128)(2,1)} %get-tuple-element.15) | copy-start | bytes 1179652
  152.9 6.3 %copy-start.8 = (bf16[96,2048]{1,0:T(8,128)(2,1)S(1)}, bf16[96,2048]{1,0:T(8,128)(2,1)}, u32[]{:S(2)}) copy-start(bf16[96,2048]{1,0:T(8,128)(2,1)} %get-tuple-element.18) | copy-start | bytes 1179652
  157.1 53.6 %collective-permute-start.4 = (f32[768,192]{0,1:T(8,128)}, f32[768,192]{0,1:T(8,128)}, u32[]{:S(2)}, u32[]{:S(2)}) collective-permute-start(f32[768,192]{0,1:T(8,128)} %convolution_bitcast_fusion), channel_id=1, source_target_pairs={{0,4},{4,0},{1,5},{5,1},{2,6},{6,2},{3,7},{7,3},{8,12},{12,8},{9,1... | collective-permute-start | bytes 1769480 | tf_op jit(solution)/shard_map/ppermute | solution.py:137
  160.8 56.6 %copy-start.7 = (bf16[1,768,512]{2,1,0:T(8,128)(2,1)S(1)}, bf16[1,768,512]{2,1,0:T(8,128)(2,1)}, u32[]{:S(2)}) copy-start(bf16[1,768,512]{2,1,0:T(8,128)(2,1)} %param.15) | copy-start | bytes 2359300
  214.8 18.8 %collective-permute-start.5 = (bf16[768,96]{0,1:T(8,128)(2,1)S(1)}, bf16[768,96]{0,1:T(8,128)(2,1)}, u32[]{:S(2)}, u32[]{:S(2)}) collective-permute-start(bf16[768,96]{0,1:T(8,128)(2,1)S(1)} %get-tuple-element.9), channel_id=1, source_target_pairs={{0,1},{1,2},{2,3},{3,4},{4,5},{5,6},{6,7},{7,0},{8,9},{9,10},{10,1... | collective-permute-start | bytes 442376 | tf_op jit(solution)/shard_map/ppermute | solution.py:72
  218.9 21.0 %collective-permute-start.6 = (bf16[768,96]{0,1:T(8,128)(2,1)S(1)}, bf16[768,96]{0,1:T(8,128)(2,1)S(1)}, u32[]{:S(2)}, u32[]{:S(2)}) collective-permute-start(bf16[768,96]{0,1:T(8,128)(2,1)S(1)} %get-tuple-element.9), channel_id=1, source_target_pairs={{0,2},{1,3},{2,4},{3,5},{4,6},{5,7},{6,0},{7,1},{8,10},{9,11},{10,... | collective-permute-start | bytes 442376 | tf_op jit(solution)/shard_map/ppermute | solution.py:72
  222.4 22.6 %collective-permute-start.7 = (bf16[768,96]{0,1:T(8,128)(2,1)S(1)}, bf16[768,96]{0,1:T(8,128)(2,1)S(1)}, u32[]{:S(2)}, u32[]{:S(2)}) collective-permute-start(bf16[768,96]{0,1:T(8,128)(2,1)S(1)} %get-tuple-element.9), channel_id=1, source_target_pairs={{0,3},{1,4},{2,5},{3,6},{4,7},{5,0},{6,1},{7,2},{8,11},{9,12},{10,... | collective-permute-start | bytes 442376 | tf_op jit(solution)/shard_map/ppermute | solution.py:72
  228.2 17.5 %collective-permute-start.8 = (bf16[768,96]{0,1:T(8,128)(2,1)S(1)}, bf16[768,96]{0,1:T(8,128)(2,1)S(1)}, u32[]{:S(2)}, u32[]{:S(2)}) collective-permute-start(bf16[768,96]{0,1:T(8,128)(2,1)S(1)} %get-tuple-element.9), channel_id=1, source_target_pairs={{0,4},{1,5},{2,6},{3,7},{4,0},{5,1},{6,2},{7,3},{8,12},{9,13},{10,... | collective-permute-start | bytes 442376 | tf_op jit(solution)/shard_map/ppermute | solution.py:72
  230.1 16.3 %collective-permute-start.9 = (bf16[768,96]{0,1:T(8,128)(2,1)S(1)}, bf16[768,96]{0,1:T(8,128)(2,1)S(1)}, u32[]{:S(2)}, u32[]{:S(2)}) collective-permute-start(bf16[768,96]{0,1:T(8,128)(2,1)S(1)} %get-tuple-element.9), channel_id=1, source_target_pairs={{0,5},{1,6},{2,7},{3,0},{4,1},{5,2},{6,3},{7,4},{8,13},{9,14},{10,... | collective-permute-start | bytes 442376 | tf_op jit(solution)/shard_map/ppermute | solution.py:72
  233.6 13.5 %collective-permute-start.10 = (bf16[768,96]{0,1:T(8,128)(2,1)S(1)}, bf16[768,96]{0,1:T(8,128)(2,1)S(1)}, u32[]{:S(2)}, u32[]{:S(2)}) collective-permute-start(bf16[768,96]{0,1:T(8,128)(2,1)S(1)} %get-tuple-element.9), channel_id=1, source_target_pairs={{0,6},{1,7},{2,0},{3,1},{4,2},{5,3},{6,4},{7,5},{8,14},{9,15},{10,... | collective-permute-start | bytes 442376 | tf_op jit(solution)/shard_map/ppermute | solution.py:72
  239.9 7.9 %collective-permute-start.11 = (bf16[768,96]{0,1:T(8,128)(2,1)S(1)}, bf16[768,96]{0,1:T(8,128)(2,1)S(1)}, u32[]{:S(2)}, u32[]{:S(2)}) collective-permute-start(bf16[768,96]{0,1:T(8,128)(2,1)S(1)} %get-tuple-element.9), channel_id=1, source_target_pairs={{0,7},{1,0},{2,1},{3,2},{4,3},{5,4},{6,5},{7,6},{8,15},{9,8},{10,9... | collective-permute-start | bytes 442376 | tf_op jit(solution)/shard_map/ppermute | solution.py:72
  250.7 15.4 %copy-start.10 = (bf16[48,8]{0,1:T(8,128)(2,1)S(1)}, bf16[48,8]{0,1:T(8,128)(2,1)}, u32[]{:S(2)}) copy-start(bf16[48,8]{0,1:T(8,128)(2,1)} %param.10) | copy-start | bytes 2308
  251.9 45.1 %all-to-all-start.2 = ((bf16[64,12,512]{2,1,0:T(8,128)(2,1)}), bf16[64,12,512]{2,1,0:T(8,128)(2,1)S(1)}, u32[]{:S(2)}, u32[]{:S(2)}) async-start(bf16[64,12,512]{2,1,0:T(8,128)(2,1)} %reshape.170), calls=%async_computation.2 | async-start | bytes 2097152 | tf_op jit(solution)/shard_map/all_to_all | solution.py:149
  269.4 1.5 copy-start.3
  269.7 2.8 copy-start.2

commit v8 on v7

--- a/solution.py
+++ b/solution.py
@@ -134,8 +134,8 @@
     other_part = lax.dot_general(
         pieces, taken3, (((0, 2), (1, 2)), ((), ())), preferred_element_type=jnp.float32
     )
-    back = lax.ppermute(other_part, "zlo", pair)
-    sums = own_part + back
+    back = lax.ppermute(other_part.astype(jnp.bfloat16), "zlo", pair)
+    sums = own_part + back.astype(jnp.float32)
     gate_sum = sums[:, :rows]
     up_sum = sums[:, rows:]
     hidden = (jax.nn.silu(gate_sum) * up_sum).astype(jnp.bfloat16)

time: 299 us -> 301 us (level)
  waiting for transfers between devices: 127 us -> 138 us
  local copies, waits for them, and re-layouts: 52.1 us -> 46.2 us
    ppermute x1, waiting for transfers between devices: 0.01 us -> 50.4 us  [body(): taken = lax.ppermute(give, 'zlo', pair)]
    ppermute x1, waiting for transfers between devices: 49.8 us -> 6.18 us  [body(): back = lax.ppermute(other_part.astype(jnp.bfloat16), 'zlo', pair)]
    ppermute x10, starting transfers between devices: 38.8 us -> 35.1 us  [ring_gather(): lax.ppermute(value, axis, [(i, (i + shift) % size) for i in range(size)])]
    all_to_all x1, starting transfers between devices: 22.1 us -> 25.7 us  [body(): lax.all_to_all(ordered, 'expert', split_axis=0, concat_axis=0, tiled=True)]
    unnamed x36 -> x32, local copies, waits for them, and re-layouts: 7.9 us -> 7.94 us
  transfers between devices with their start and end apart: 15 -> 15, of which waited for: 3 -> 5; matrix products, arithmetic and copies ran while one was open for 20% -> 15% of each run, Pallas kernels for 0% -> 0%
where the time goes in v8:
time: 301 us; the launch traced here: 300 us
  waiting for transfers between devices  138 us (46%)
  starting transfers between devices  95.6 us (32%)
  local copies, waits for them, and re-layouts  46.2 us (15%)
  other arithmetic  10.1 us (3%)
  matrix products  8.91 us (3%)
    all_to_all x1, waiting for transfers between devices, body(): lax.all_to_all(jnp.concatenate([token_lanes, packed], axis=1), 'expert',...  57.1 us
    ppermute x1, waiting for transfers between devices, body(): taken = lax.ppermute(give, 'zlo', pair)  50.4 us
    ppermute x10, starting transfers between devices, ring_gather(): lax.ppermute(value, axis, [(i, (i + shift) % size) for i in range(size)])  35.1 us
    all_to_all x1, starting transfers between devices, body(): lax.all_to_all(ordered, 'expert', split_axis=0, concat_axis=0, tiled=True)  25.7 us
    all_to_all x1, waiting for transfers between devices, body(): lax.all_to_all(produced.reshape(groups, capacity, -1), 'expert', split_ax...  23.9 us
    all_to_all x1, starting transfers between devices, body(): lax.all_to_all(jnp.concatenate([token_lanes, packed], axis=1), 'expert',...  16.5 us
    all_to_all x1, starting transfers between devices, body(): lax.all_to_all(produced.reshape(groups, capacity, -1), 'expert', split_ax...  11.7 us
    dynamic_slice x1, local copies, waits for them, and re-layouts, body(): lax.dynamic_index_in_dim(up_halves, 1 - half, axis=1, keepdims=False)  9.23 us
  transfers between devices with their start and end apart: 15, of which 5 were waited for; matrix products, arithmetic and copies ran while one was open for 15% of the time, Pallas kernels for 0%

profile of v8, /device:TPU:16, one launch (start us, length us, event | category | flops | bytes accessed | tf_op | source)
XLA Modules:
  0.0 299.7 jit_solution(4001397174530558530)
XLA Ops:
  1.7 1.6 select_reduce_fusion
  10.1 2.1 pad_maximum_fusion
  12.1 16.5 %all-to-all-start = ((bf16[64,192,128]{2,1,0:T(8,128)(2,1)}), bf16[64,192,128]{2,1,0:T(8,128)(2,1)S(1)}, u32[]{:S(2)}, u32[]{:S(2)}) async-start(bf16[64,192,128]{2,1,0:T(8,128)(2,1)} %pad_maximum_fusion), calls=%async_computation | async-start | bytes 6291456 | tf_op jit(solution)/shard_map/all_to_all | solution.py:114
  28.6 3.3 %reshape_squeeze.21 = bf16[96,2,2048]{2,1,0:T(2,128)(2,1)} reshape(bf16[1,96,4096]{2,1,0:T(8,128)(2,1)} %param.13) | data formatting | bytes 1572864 | tf_op jit(solution)/shard_map/reshape;squeeze | solution.py:91
  31.9 3.2 %reshape_squeeze.22 = bf16[96,2,2048]{2,1,0:T(2,128)(2,1)} reshape(bf16[1,96,4096]{2,1,0:T(8,128)(2,1)} %param.14) | data formatting | bytes 1572864 | tf_op jit(solution)/shard_map/reshape;squeeze | solution.py:92
  35.1 9.2 %constant_dynamic-slice_fusion = (bf16[96,1,2048]{2,1,0:T(2,128)(2,1)S(1)}, bf16[96,2048]{1,0:T(8,128)(2,1)}, bf16[96,2048]{1,0:T(8,128)(2,1)}, bf16[96,1,2048]{2,1,0:T(2,128)(2,1)S(1)}) fusion(bf16[96,2,2048]{2,1,0:T(2,128)(2,1)} %reshape_squeeze.22, s32[]{:T(128)S(6)} %select_n.43, s32[]{:T(128)S(6)} %select_n.41, bf16[96,2,2048]{2,1,0:T(2,128)(2,1)} %reshape_squeeze.21), kind=kLoop, calls=%fused_computation.60 | loop fusion | bytes 3145736 | tf_op jit(solution)/shard_map/jit(dynamic_index_in_dim)/dynamic_slice | solution.py:103
  46.3 57.1 %all-to-all-done = bf16[64,192,128]{2,1,0:T(8,128)(2,1)S(1)} async-done(((bf16[64,192,128]{2,1,0:T(8,128)(2,1)}), bf16[64,192,128]{2,1,0:T(8,128)(2,1)S(1)}, u32[]{:S(2)}, u32[]{:S(2)}) %all-to-all-start) | async-done | bytes 3145760 | tf_op jit(solution)/shard_map/all_to_all | solution.py:114
  103.5 1.6 slice.48
  105.1 3.9 %gather_fusion.3 = bf16[64,144,128]{2,1,0:T(8,128)(2,1)} fusion(bf16[64,144,128]{2,1,0:T(8,128)(2,1)} %slice.48, s32[1024]{0:T(1024)S(1)} %pad_clamp_fusion), kind=kCustom, calls=%fused_computation.3 | custom fusion | bytes 4718848 | tf_op jit(solution)/shard_map/jit(_take)/gather | solution.py:123
  109.0 25.7 %all-to-all-start.1 = ((bf16[64,144,128]{2,1,0:T(8,128)(2,1)}), bf16[64,144,128]{2,1,0:T(8,128)(2,1)}, u32[]{:S(2)}, u32[]{:S(2)}) async-start(bf16[64,144,128]{2,1,0:T(8,128)(2,1)} %gather_fusion.3), calls=%async_computation.1 | async-start | bytes 4718592 | tf_op jit(solution)/shard_map/all_to_all | solution.py:124
  134.7 2.1 pad_maximum_fusion.4
  136.8 1.9 collective-permute-start.3
  139.6 1.6 reshape.168
  141.3 3.0 collective-permute-start
  144.3 1.9 collective-permute-start.1
  146.2 4.6 %collective-permute-start.2 = (bf16[768,512]{1,0:T(8,128)(2,1)S(1)}, bf16[768,512]{1,0:T(8,128)(2,1)}, u32[]{:S(2)}, u32[]{:S(2)}) collective-permute-start(bf16[768,512]{1,0:T(8,128)(2,1)S(1)} %reshape.168), channel_id=1, source_target_pairs={{0,3},{1,0},{2,1},{3,2},{4,7},{5,4},{6,5},{7,6},{8,11},{9,8},{10,9... | collective-permute-start | bytes 2359304 | tf_op jit(solution)/shard_map/ppermute | solution.py:72
  150.8 50.4 %collective-permute-done.3 = bf16[192,2048]{1,0:T(8,128)(2,1)} collective-permute-done((bf16[192,2048]{1,0:T(8,128)(2,1)}, bf16[192,2048]{1,0:T(8,128)(2,1)}, u32[]{:S(2)}, u32[]{:S(2)}) %collective-permute-start.3) | collective-permute-done | bytes 786464 | tf_op jit(solution)/shard_map/ppermute | solution.py:107
  203.5 2.9 fusion.1
  206.4 4.6 %collective-permute-start.4 = (bf16[768,192]{0,1:T(8,128)(2,1)S(1)}, bf16[768,192]{0,1:T(8,128)(2,1)S(1)}, u32[]{:S(2)}, u32[]{:S(2)}) collective-permute-start(bf16[768,192]{0,1:T(8,128)(2,1)S(1)} %fusion.1), channel_id=1, source_target_pairs={{0,4},{4,0},{1,5},{5,1},{2,6},{6,2},{3,7},{7,3},{8,12},{12,8},{9,1... | collective-permute-start | bytes 884744 | tf_op jit(solution)/shard_map/ppermute | solution.py:137
  211.8 6.2 %collective-permute-done.4 = bf16[768,192]{0,1:T(8,128)(2,1)S(1)} collective-permute-done((bf16[768,192]{0,1:T(8,128)(2,1)S(1)}, bf16[768,192]{0,1:T(8,128)(2,1)S(1)}, u32[]{:S(2)}, u32[]{:S(2)}) %collective-permute-start.4) | collective-permute-done | bytes 294944 | tf_op jit(solution)/shard_map/ppermute | solution.py:137
  218.0 2.7 fusion
  221.5 3.6 %collective-permute-start.5 = (bf16[768,96]{0,1:T(8,128)(2,1)S(1)}, bf16[768,96]{0,1:T(8,128)(2,1)S(1)}, u32[]{:S(2)}, u32[]{:S(2)}) collective-permute-start(bf16[768,96]{0,1:T(8,128)(2,1)S(1)} %get-tuple-element.9), channel_id=1, source_target_pairs={{0,1},{1,2},{2,3},{3,4},{4,5},{5,6},{6,7},{7,0},{8,9},{9,10},{10,1... | collective-permute-start | bytes 442376 | tf_op jit(solution)/shard_map/ppermute | solution.py:72
  225.7 1.9 collective-permute-start.6
  227.6 5.8 %collective-permute-start.7 = (bf16[768,96]{0,1:T(8,128)(2,1)S(1)}, bf16[768,96]{0,1:T(8,128)(2,1)S(1)}, u32[]{:S(2)}, u32[]{:S(2)}) collective-permute-start(bf16[768,96]{0,1:T(8,128)(2,1)S(1)} %get-tuple-element.9), channel_id=1, source_target_pairs={{0,3},{1,4},{2,5},{3,6},{4,7},{5,0},{6,1},{7,2},{8,11},{9,12},{10,... | collective-permute-start | bytes 442376 | tf_op jit(solution)/shard_map/ppermute | solution.py:72
  233.4 2.2 collective-permute-start.8
  235.6 2.8 collective-permute-start.9
  238.4 5.9 %collective-permute-start.10 = (bf16[768,96]{0,1:T(8,128)(2,1)S(1)}, bf16[768,96]{0,1:T(8,128)(2,1)S(1)}, u32[]{:S(2)}, u32[]{:S(2)}) collective-permute-start(bf16[768,96]{0,1:T(8,128)(2,1)S(1)} %get-tuple-element.9), channel_id=1, source_target_pairs={{0,6},{1,7},{2,0},{3,1},{4,2},{5,3},{6,4},{7,5},{8,14},{9,15},{10,... | collective-permute-start | bytes 442376 | tf_op jit(solution)/shard_map/ppermute | solution.py:72
  245.0 3.5 %collective-permute-start.11 = (bf16[768,96]{0,1:T(8,128)(2,1)S(1)}, bf16[768,96]{0,1:T(8,128)(2,1)S(1)}, u32[]{:S(2)}, u32[]{:S(2)}) collective-permute-start(bf16[768,96]{0,1:T(8,128)(2,1)S(1)} %get-tuple-element.9), channel_id=1, source_target_pairs={{0,7},{1,0},{2,1},{3,2},{4,3},{5,4},{6,5},{7,6},{8,15},{9,8},{10,9... | collective-permute-start | bytes 442376 | tf_op jit(solution)/shard_map/ppermute | solution.py:72
  252.8 2.1 bitcast_convert_fusion
  256.0 11.7 %all-to-all-start.2 = ((bf16[64,12,512]{2,1,0:T(8,128)(2,1)}), bf16[64,12,512]{2,1,0:T(8,128)(2,1)S(1)}, u32[]{:S(2)}, u32[]{:S(2)}) async-start(bf16[64,12,512]{2,1,0:T(8,128)(2,1)} %reshape.170), calls=%async_computation.2 | async-start | bytes 2097152 | tf_op jit(solution)/shard_map/all_to_all | solution.py:149
  268.3 1.8 fusion.17
  274.7 23.9 %all-to-all-done.2 = bf16[64,12,512]{2,1,0:T(8,128)(2,1)S(1)} async-done(((bf16[64,12,512]{2,1,0:T(8,128)(2,1)}), bf16[64,12,512]{2,1,0:T(8,128)(2,1)S(1)}, u32[]{:S(2)}, u32[]{:S(2)}) %all-to-all-start.2) | async-done | bytes 786464 | tf_op jit(solution)/shard_map/all_to_all | solution.py:149
  (86 shorter events, 27.3 us)
Async XLA Ops:
  0.6 5.9 %copy-start = (bf16[48,512]{1,0:T(8,128)(2,1)S(1)}, bf16[48,512]{1,0:T(8,128)(2,1)}, u32[]{:S(2)}) copy-start(bf16[48,512]{1,0:T(8,128)(2,1)} %param.8) | copy-start | bytes 147460
  0.6 6.8 %copy-start.4 = (bf16[1,768,512]{2,1,0:T(8,128)(2,1)S(1)}, bf16[1,768,512]{2,1,0:T(8,128)(2,1)}, u32[]{:S(2)}) copy-start(bf16[1,768,512]{2,1,0:T(8,128)(2,1)} %param.15) | copy-start | bytes 2359300
  7.4 1.1 copy-start.2
  7.6 1.2 copy-start.3
  12.1 91.3 %all-to-all-start = ((bf16[64,192,128]{2,1,0:T(8,128)(2,1)}), bf16[64,192,128]{2,1,0:T(8,128)(2,1)S(1)}, u32[]{:S(2)}, u32[]{:S(2)}) async-start(bf16[64,192,128]{2,1,0:T(8,128)(2,1)} %pad_maximum_fusion), calls=%async_computation | async-start | bytes 6291456 | tf_op jit(solution)/shard_map/all_to_all | solution.py:114
  44.4 2.0 copy-start.9
  109.0 145.9 %all-to-all-start.1 = ((bf16[64,144,128]{2,1,0:T(8,128)(2,1)}), bf16[64,144,128]{2,1,0:T(8,128)(2,1)}, u32[]{:S(2)}, u32[]{:S(2)}) async-start(bf16[64,144,128]{2,1,0:T(8,128)(2,1)} %gather_fusion.3), calls=%async_computation.1 | async-start | bytes 4718592 | tf_op jit(solution)/shard_map/all_to_all | solution.py:124
  136.8 64.4 %collective-permute-start.3 = (bf16[192,2048]{1,0:T(8,128)(2,1)}, bf16[192,2048]{1,0:T(8,128)(2,1)}, u32[]{:S(2)}, u32[]{:S(2)}) collective-permute-start(bf16[192,2048]{1,0:T(8,128)(2,1)} %pad_maximum_fusion.4), channel_id=1, source_target_pairs={{0,4},{4,0},{1,5},{5,1},{2,6},{6,2},{3,7},{7,3},{8,12},{12,8},{9,1... | collective-permute-start | bytes 2359304 | tf_op jit(solution)/shard_map/ppermute | solution.py:107
  139.6 63.4 %copy-start.1 = (bf16[64,48,128]{2,1,0:T(8,128)(2,1)S(1)}, bf16[64,48,128]{2,1,0:T(8,128)(2,1)}, u32[]{:S(2)}) copy-start(bf16[64,48,128]{2,1,0:T(8,128)(2,1)} %slice.45) | copy-start | bytes 2359300
  141.3 62.2 %collective-permute-start = (bf16[768,512]{1,0:T(8,128)(2,1)S(1)}, bf16[768,512]{1,0:T(8,128)(2,1)}, u32[]{:S(2)}, u32[]{:S(2)}) collective-permute-start(bf16[768,512]{1,0:T(8,128)(2,1)S(1)} %reshape.168), channel_id=1, source_target_pairs={{0,1},{1,2},{2,3},{3,0},{4,5},{5,6},{6,7},{7,4},{8,9},{9,10},{10,1... | collective-permute-start | bytes 2359304 | tf_op jit(solution)/shard_map/ppermute | solution.py:72
  144.3 59.2 %collective-permute-start.1 = (bf16[768,512]{1,0:T(8,128)(2,1)S(1)}, bf16[768,512]{1,0:T(8,128)(2,1)}, u32[]{:S(2)}, u32[]{:S(2)}) collective-permute-start(bf16[768,512]{1,0:T(8,128)(2,1)S(1)} %reshape.168), channel_id=1, source_target_pairs={{0,2},{1,3},{2,0},{3,1},{4,6},{5,7},{6,4},{7,5},{8,10},{9,11},{10,... | collective-permute-start | bytes 2359304 | tf_op jit(solution)/shard_map/ppermute | solution.py:72
  146.2 57.3 %collective-permute-start.2 = (bf16[768,512]{1,0:T(8,128)(2,1)S(1)}, bf16[768,512]{1,0:T(8,128)(2,1)}, u32[]{:S(2)}, u32[]{:S(2)}) collective-permute-start(bf16[768,512]{1,0:T(8,128)(2,1)S(1)} %reshape.168), channel_id=1, source_target_pairs={{0,3},{1,0},{2,1},{3,2},{4,7},{5,4},{6,5},{7,6},{8,11},{9,8},{10,9... | collective-permute-start | bytes 2359304 | tf_op jit(solution)/shard_map/ppermute | solution.py:72
  203.5 7.5 %copy-start.7 = (bf16[96,2048]{1,0:T(8,128)(2,1)S(1)}, bf16[96,2048]{1,0:T(8,128)(2,1)}, u32[]{:S(2)}) copy-start(bf16[96,2048]{1,0:T(8,128)(2,1)} %get-tuple-element.16) | copy-start | bytes 1179652
  203.5 7.5 %copy-start.6 = (bf16[96,2048]{1,0:T(8,128)(2,1)S(1)}, bf16[96,2048]{1,0:T(8,128)(2,1)}, u32[]{:S(2)}) copy-start(bf16[96,2048]{1,0:T(8,128)(2,1)} %get-tuple-element.17) | copy-start | bytes 1179652
  206.4 11.6 %collective-permute-start.4 = (bf16[768,192]{0,1:T(8,128)(2,1)S(1)}, bf16[768,192]{0,1:T(8,128)(2,1)S(1)}, u32[]{:S(2)}, u32[]{:S(2)}) collective-permute-start(bf16[768,192]{0,1:T(8,128)(2,1)S(1)} %fusion.1), channel_id=1, source_target_pairs={{0,4},{4,0},{1,5},{5,1},{2,6},{6,2},{3,7},{7,3},{8,12},{12,8},{9,1... | collective-permute-start | bytes 884744 | tf_op jit(solution)/shard_map/ppermute | solution.py:137
  211.8 13.3 %copy-start.5 = (bf16[1,768,512]{2,1,0:T(8,128)(2,1)S(1)}, bf16[1,768,512]{2,1,0:T(8,128)(2,1)}, u32[]{:S(2)}) copy-start(bf16[1,768,512]{2,1,0:T(8,128)(2,1)} %param.15) | copy-start | bytes 2359300
  221.5 17.0 %collective-permute-start.5 = (bf16[768,96]{0,1:T(8,128)(2,1)S(1)}, bf16[768,96]{0,1:T(8,128)(2,1)S(1)}, u32[]{:S(2)}, u32[]{:S(2)}) collective-permute-start(bf16[768,96]{0,1:T(8,128)(2,1)S(1)} %get-tuple-element.9), channel_id=1, source_target_pairs={{0,1},{1,2},{2,3},{3,4},{4,5},{5,6},{6,7},{7,0},{8,9},{9,10},{10,1... | collective-permute-start | bytes 442376 | tf_op jit(solution)/shard_map/ppermute | solution.py:72
  225.7 19.4 %collective-permute-start.6 = (bf16[768,96]{0,1:T(8,128)(2,1)S(1)}, bf16[768,96]{0,1:T(8,128)(2,1)S(1)}, u32[]{:S(2)}, u32[]{:S(2)}) collective-permute-start(bf16[768,96]{0,1:T(8,128)(2,1)S(1)} %get-tuple-element.9), channel_id=1, source_target_pairs={{0,2},{1,3},{2,4},{3,5},{4,6},{5,7},{6,0},{7,1},{8,10},{9,11},{10,... | collective-permute-start | bytes 442376 | tf_op jit(solution)/shard_map/ppermute | solution.py:72
  227.6 21.6 %collective-permute-start.7 = (bf16[768,96]{0,1:T(8,128)(2,1)S(1)}, bf16[768,96]{0,1:T(8,128)(2,1)S(1)}, u32[]{:S(2)}, u32[]{:S(2)}) collective-permute-start(bf16[768,96]{0,1:T(8,128)(2,1)S(1)} %get-tuple-element.9), channel_id=1, source_target_pairs={{0,3},{1,4},{2,5},{3,6},{4,7},{5,0},{6,1},{7,2},{8,11},{9,12},{10,... | collective-permute-start | bytes 442376 | tf_op jit(solution)/shard_map/ppermute | solution.py:72
  233.4 16.5 %collective-permute-start.8 = (bf16[768,96]{0,1:T(8,128)(2,1)S(1)}, bf16[768,96]{0,1:T(8,128)(2,1)S(1)}, u32[]{:S(2)}, u32[]{:S(2)}) collective-permute-start(bf16[768,96]{0,1:T(8,128)(2,1)S(1)} %get-tuple-element.9), channel_id=1, source_target_pairs={{0,4},{1,5},{2,6},{3,7},{4,0},{5,1},{6,2},{7,3},{8,12},{9,13},{10,... | collective-permute-start | bytes 442376 | tf_op jit(solution)/shard_map/ppermute | solution.py:72
  235.6 15.0 %collective-permute-start.9 = (bf16[768,96]{0,1:T(8,128)(2,1)S(1)}, bf16[768,96]{0,1:T(8,128)(2,1)S(1)}, u32[]{:S(2)}, u32[]{:S(2)}) collective-permute-start(bf16[768,96]{0,1:T(8,128)(2,1)S(1)} %get-tuple-element.9), channel_id=1, source_target_pairs={{0,5},{1,6},{2,7},{3,0},{4,1},{5,2},{6,3},{7,4},{8,13},{9,14},{10,... | collective-permute-start | bytes 442376 | tf_op jit(solution)/shard_map/ppermute | solution.py:72
  238.4 12.8 %collective-permute-start.10 = (bf16[768,96]{0,1:T(8,128)(2,1)S(1)}, bf16[768,96]{0,1:T(8,128)(2,1)S(1)}, u32[]{:S(2)}, u32[]{:S(2)}) collective-permute-start(bf16[768,96]{0,1:T(8,128)(2,1)S(1)} %get-tuple-element.9), channel_id=1, source_target_pairs={{0,6},{1,7},{2,0},{3,1},{4,2},{5,3},{6,4},{7,5},{8,14},{9,15},{10,... | collective-permute-start | bytes 442376 | tf_op jit(solution)/shard_map/ppermute | solution.py:72
  245.0 7.0 %collective-permute-start.11 = (bf16[768,96]{0,1:T(8,128)(2,1)S(1)}, bf16[768,96]{0,1:T(8,128)(2,1)S(1)}, u32[]{:S(2)}, u32[]{:S(2)}) collective-permute-start(bf16[768,96]{0,1:T(8,128)(2,1)S(1)} %get-tuple-element.9), channel_id=1, source_target_pairs={{0,7},{1,0},{2,1},{3,2},{4,3},{5,4},{6,5},{7,6},{8,15},{9,8},{10,9... | collective-permute-start | bytes 442376 | tf_op jit(solution)/shard_map/ppermute | solution.py:72
  254.8 12.9 %copy-start.8 = (bf16[48,8]{0,1:T(8,128)(2,1)S(1)}, bf16[48,8]{0,1:T(8,128)(2,1)}, u32[]{:S(2)}) copy-start(bf16[48,8]{0,1:T(8,128)(2,1)} %param.10) | copy-start | bytes 2308
  256.0 42.6 %all-to-all-start.2 = ((bf16[64,12,512]{2,1,0:T(8,128)(2,1)}), bf16[64,12,512]{2,1,0:T(8,128)(2,1)S(1)}, u32[]{:S(2)}, u32[]{:S(2)}) async-start(bf16[64,12,512]{2,1,0:T(8,128)(2,1)} %reshape.170), calls=%async_computation.2 | async-start | bytes 2097152 | tf_op jit(solution)/shard_map/all_to_all | solution.py:149

commit v9 on v7

--- a/solution.py
+++ b/solution.py
@@ -139,8 +139,13 @@
     gate_sum = sums[:, :rows]
     up_sum = sums[:, rows:]
     hidden = (jax.nn.silu(gate_sum) * up_sum).astype(jnp.bfloat16)
-    hidden_all, owners = ring_gather(hidden, ("zlo", "x"), narrow_count, narrow_index)
-    down3 = jnp.take(down_block.reshape(narrow_count, rows, narrow_width), owners, axis=0, mode="clip")
+    duo = jnp.stack([hidden, lax.ppermute(hidden, "zlo", pair)], axis=0)
+    quads, sources = ring_gather(duo, "x", columns, column)
+    hidden_all = quads.reshape(-1, hidden.shape[0], rows)
+    owners = ((half + jnp.arange(2, dtype=jnp.int32)[None, :]) % 2) * columns + sources[:, None]
+    down3 = jnp.take(
+        down_block.reshape(narrow_count, rows, narrow_width), owners.reshape(-1), axis=0, mode="clip"
+    )
     produced = lax.dot_general(
         hidden_all, down3, (((0, 2), (0, 1)), ((), ())), preferred_element_type=jnp.float32
     ).astype(jnp.bfloat16)

time: 299 us -> 302 us (1.010)
  the two profiles are of different devices: /device:TPU:16 before, /device:TPU:18 now
where the time goes in v9:
time: 302 us; the launch traced here: 301 us
  waiting for transfers between devices  160 us (53%)
  starting transfers between devices  83.1 us (28%)
  local copies, waits for them, and re-layouts  40 us (13%)
  other arithmetic  8.65 us (3%)
  matrix products  8.46 us (3%)
    all_to_all x1, waiting for transfers between devices, body(): lax.all_to_all(jnp.concatenate([token_lanes, packed], axis=1), 'expert',...  73.7 us
    ppermute x1, waiting for transfers between devices, body(): taken = lax.ppermute(give, 'zlo', pair)  37.5 us
    all_to_all x1, waiting for transfers between devices, body(): lax.all_to_all(produced.reshape(groups, capacity, -1), 'expert', split_ax...  23.9 us
    all_to_all x1, starting transfers between devices, body(): lax.all_to_all(ordered, 'expert', split_axis=0, concat_axis=0, tiled=True)  21.4 us
    ppermute x6, starting transfers between devices, ring_gather(): lax.ppermute(value, axis, [(i, (i + shift) % size) for i in range(size)])  20.8 us
    all_to_all x1, starting transfers between devices, body(): lax.all_to_all(jnp.concatenate([token_lanes, packed], axis=1), 'expert',...  16.6 us
    all_to_all x1, starting transfers between devices, body(): lax.all_to_all(produced.reshape(groups, capacity, -1), 'expert', split_ax...  14.2 us
    ppermute x1, waiting for transfers between devices, body(): back = lax.ppermute(other_part, 'zlo', pair)  12.8 us
  transfers between devices with their start and end apart: 12, of which 7 were waited for; matrix products, arithmetic and copies ran while one was open for 13% of the time, Pallas kernels for 0%

profile of v9, /device:TPU:18, one launch (start us, length us, event | category | flops | bytes accessed | tf_op | source)
XLA Modules:
  0.0 300.9 jit_solution(10120515436471264784)
XLA Ops:
  1.7 1.6 select_reduce_fusion
  10.1 2.1 pad_maximum_fusion
  12.1 16.6 %all-to-all-start = ((bf16[64,192,128]{2,1,0:T(8,128)(2,1)}), bf16[64,192,128]{2,1,0:T(8,128)(2,1)S(1)}, u32[]{:S(2)}, u32[]{:S(2)}) async-start(bf16[64,192,128]{2,1,0:T(8,128)(2,1)} %pad_maximum_fusion), calls=%async_computation | async-start | bytes 6291456 | tf_op jit(solution)/shard_map/all_to_all | solution.py:114
  28.8 73.7 %all-to-all-done = bf16[64,192,128]{2,1,0:T(8,128)(2,1)S(1)} async-done(((bf16[64,192,128]{2,1,0:T(8,128)(2,1)}), bf16[64,192,128]{2,1,0:T(8,128)(2,1)S(1)}, u32[]{:S(2)}, u32[]{:S(2)}) %all-to-all-start) | async-done | bytes 3145760 | tf_op jit(solution)/shard_map/all_to_all | solution.py:114
  102.4 1.6 slice.48
  104.0 3.9 %gather_fusion.3 = bf16[64,144,128]{2,1,0:T(8,128)(2,1)} fusion(bf16[64,144,128]{2,1,0:T(8,128)(2,1)} %slice.48, s32[1024]{0:T(1024)S(1)} %pad_clamp_fusion), kind=kCustom, calls=%fused_computation.3 | custom fusion | bytes 4718848 | tf_op jit(solution)/shard_map/jit(_take)/gather | solution.py:123
  107.9 21.4 %all-to-all-start.1 = ((bf16[64,144,128]{2,1,0:T(8,128)(2,1)}), bf16[64,144,128]{2,1,0:T(8,128)(2,1)}, u32[]{:S(2)}, u32[]{:S(2)}) async-start(bf16[64,144,128]{2,1,0:T(8,128)(2,1)} %gather_fusion.3), calls=%async_computation.1 | async-start | bytes 4718592 | tf_op jit(solution)/shard_map/all_to_all | solution.py:124
  129.3 3.3 %reshape_squeeze.21 = bf16[96,2,2048]{2,1,0:T(2,128)(2,1)} reshape(bf16[1,96,4096]{2,1,0:T(8,128)(2,1)} %param.13) | data formatting | bytes 1572864 | tf_op jit(solution)/shard_map/reshape;squeeze | solution.py:91
  132.6 3.2 %reshape_squeeze.22 = bf16[96,2,2048]{2,1,0:T(2,128)(2,1)} reshape(bf16[1,96,4096]{2,1,0:T(8,128)(2,1)} %param.14) | data formatting | bytes 1572864 | tf_op jit(solution)/shard_map/reshape;squeeze | solution.py:92
  135.8 9.2 %dynamic-slice_reduce_fusion = (bf16[96,2048]{1,0:T(8,128)(2,1)}, bf16[96,1,2048]{2,1,0:T(2,128)(2,1)S(1)}, bf16[96,1,2048]{2,1,0:T(2,128)(2,1)S(1)}, bf16[96,2048]{1,0:T(8,128)(2,1)}) fusion(bf16[96,2,2048]{2,1,0:T(2,128)(2,1)} %reshape_squeeze.22, s32[]{:T(128)S(6)} %select_n.44, s32[]{:T(128)S(6)} %select_n.46, bf16[96,2,2048]{2,1,0:T(2,128)(2,1)} %reshape_squeeze.21), kind=kLoop, calls=%fused_computation.25 | loop fusion | bytes 3145736 | tf_op jit(solution)/shard_map/jit(dynamic_index_in_dim)/dynamic_slice | solution.py:96
  146.4 1.9 collective-permute-start.3
  149.3 1.6 reshape.180
  150.9 3.0 %collective-permute-start = (bf16[768,512]{1,0:T(8,128)(2,1)S(1)}, bf16[768,512]{1,0:T(8,128)(2,1)}, u32[]{:S(2)}, u32[]{:S(2)}) collective-permute-start(bf16[768,512]{1,0:T(8,128)(2,1)S(1)} %reshape.180), channel_id=1, source_target_pairs={{0,1},{1,2},{2,3},{3,0},{4,5},{5,6},{6,7},{7,4},{8,9},{9,10},{10,1... | collective-permute-start | bytes 2359304 | tf_op jit(solution)/shard_map/ppermute | solution.py:72
  154.0 3.3 %collective-permute-start.1 = (bf16[768,512]{1,0:T(8,128)(2,1)S(1)}, bf16[768,512]{1,0:T(8,128)(2,1)}, u32[]{:S(2)}, u32[]{:S(2)}) collective-permute-start(bf16[768,512]{1,0:T(8,128)(2,1)S(1)} %reshape.180), channel_id=1, source_target_pairs={{0,2},{1,3},{2,0},{3,1},{4,6},{5,7},{6,4},{7,5},{8,10},{9,11},{10,... | collective-permute-start | bytes 2359304 | tf_op jit(solution)/shard_map/ppermute | solution.py:72
  157.3 3.7 %collective-permute-start.2 = (bf16[768,512]{1,0:T(8,128)(2,1)S(1)}, bf16[768,512]{1,0:T(8,128)(2,1)}, u32[]{:S(2)}, u32[]{:S(2)}) collective-permute-start(bf16[768,512]{1,0:T(8,128)(2,1)S(1)} %reshape.180), channel_id=1, source_target_pairs={{0,3},{1,0},{2,1},{3,2},{4,7},{5,4},{6,5},{7,6},{8,11},{9,8},{10,9... | collective-permute-start | bytes 2359304 | tf_op jit(solution)/shard_map/ppermute | solution.py:72
  161.1 37.5 %collective-permute-done.3 = bf16[192,2048]{1,0:T(8,128)(2,1)} collective-permute-done((bf16[192,2048]{1,0:T(8,128)(2,1)}, bf16[192,2048]{1,0:T(8,128)(2,1)}, u32[]{:S(2)}, u32[]{:S(2)}) %collective-permute-start.3) | collective-permute-done | bytes 786464 | tf_op jit(solution)/shard_map/ppermute | solution.py:107
  200.9 3.7 %convolution_bitcast_fusion = f32[768,192]{0,1:T(8,128)} fusion(bf16[4,192,512]{2,1,0:T(8,128)(2,1)S(1)} %gather_fusion.1, bf16[1,768,512]{2,1,0:T(8,128)(2,1)} %bitcast.8, bf16[1,768,512]{2,1,0:T(8,128)(2,1)} %bitcast.7, bf16[1,768,512]{2,1,0:T(8,128)(2,1)} %bitcast.6, bf16[1,768,512]{2,1,0:T(8,128)(2,1)S(1)} %stack_reshape.3), kind=kOutput, calls=%fused_computation.9 | convolution fusion | flops 608698368 | bytes 4521984 | tf_op jit(solution)/shard_map/dot_general | solution.py:134
  204.6 4.4 %collective-permute-start.4 = (f32[768,192]{0,1:T(8,128)}, f32[768,192]{0,1:T(8,128)S(1)}, u32[]{:S(2)}, u32[]{:S(2)}) collective-permute-start(f32[768,192]{0,1:T(8,128)} %convolution_bitcast_fusion), channel_id=1, source_target_pairs={{0,4},{4,0},{1,5},{5,1},{2,6},{6,2},{3,7},{7,3},{8,12},{12,8},{9,1... | collective-permute-start | bytes 1769480 | tf_op jit(solution)/shard_map/ppermute | solution.py:137
  209.8 12.8 %collective-permute-done.4 = f32[768,192]{0,1:T(8,128)S(1)} collective-permute-done((f32[768,192]{0,1:T(8,128)}, f32[768,192]{0,1:T(8,128)S(1)}, u32[]{:S(2)}, u32[]{:S(2)}) %collective-permute-start.4) | collective-permute-done | bytes 589856 | tf_op jit(solution)/shard_map/ppermute | solution.py:137
  222.6 2.7 fusion
  225.5 3.8 %collective-permute-start.5 = (bf16[768,96]{0,1:T(8,128)(2,1)S(1)}, bf16[768,96]{0,1:T(8,128)(2,1)S(1)}, u32[]{:S(2)}, u32[]{:S(2)}) collective-permute-start(bf16[768,96]{0,1:T(8,128)(2,1)S(1)} %fusion.5), channel_id=1, source_target_pairs={{0,4},{4,0},{1,5},{5,1},{2,6},{6,2},{3,7},{7,3},{8,12},{12,8},{9,1... | collective-permute-start | bytes 442376 | tf_op jit(solution)/shard_map/ppermute | solution.py:142
  229.3 3.3 %collective-permute-done.5 = bf16[768,96]{0,1:T(8,128)(2,1)S(1)} collective-permute-done((bf16[768,96]{0,1:T(8,128)(2,1)S(1)}, bf16[768,96]{0,1:T(8,128)(2,1)S(1)}, u32[]{:S(2)}, u32[]{:S(2)}) %collective-permute-start.5) | collective-permute-done | bytes 147488 | tf_op jit(solution)/shard_map/ppermute | solution.py:142
  232.7 3.4 %collective-permute-start.6 = (bf16[2,768,96]{1,2,0:T(8,128)(2,1)S(1)}, bf16[2,768,96]{1,2,0:T(8,128)(2,1)S(1)}, u32[]{:S(2)}, u32[]{:S(2)}) collective-permute-start(bf16[2,768,96]{1,2,0:T(8,128)(2,1)S(1)} %get-tuple-element.16), channel_id=1, source_target_pairs={{0,1},{1,2},{2,3},{3,0},{4,5},{5,6},{6,7},{7,4},{8,9},{9,10},{10,1... | collective-permute-start | bytes 884744 | tf_op jit(solution)/shard_map/ppermute | solution.py:72
  236.0 3.9 %collective-permute-start.7 = (bf16[2,768,96]{1,2,0:T(8,128)(2,1)S(1)}, bf16[2,768,96]{1,2,0:T(8,128)(2,1)S(1)}, u32[]{:S(2)}, u32[]{:S(2)}) collective-permute-start(bf16[2,768,96]{1,2,0:T(8,128)(2,1)S(1)} %get-tuple-element.16), channel_id=1, source_target_pairs={{0,2},{1,3},{2,0},{3,1},{4,6},{5,7},{6,4},{7,5},{8,10},{9,11},{10,... | collective-permute-start | bytes 884744 | tf_op jit(solution)/shard_map/ppermute | solution.py:72
  240.0 3.4 %collective-permute-start.8 = (bf16[2,768,96]{1,2,0:T(8,128)(2,1)S(1)}, bf16[2,768,96]{1,2,0:T(8,128)(2,1)S(1)}, u32[]{:S(2)}, u32[]{:S(2)}) collective-permute-start(bf16[2,768,96]{1,2,0:T(8,128)(2,1)S(1)} %get-tuple-element.16), channel_id=1, source_target_pairs={{0,3},{1,0},{2,1},{3,2},{4,7},{5,4},{6,5},{7,6},{8,11},{9,8},{10,9... | collective-permute-start | bytes 884744 | tf_op jit(solution)/shard_map/ppermute | solution.py:72
  244.1 5.2 %collective-permute-done.7 = bf16[2,768,96]{1,2,0:T(8,128)(2,1)S(1)} collective-permute-done((bf16[2,768,96]{1,2,0:T(8,128)(2,1)S(1)}, bf16[2,768,96]{1,2,0:T(8,128)(2,1)S(1)}, u32[]{:S(2)}, u32[]{:S(2)}) %collective-permute-start.7) | collective-permute-done | bytes 294944 | tf_op jit(solution)/shard_map/ppermute | solution.py:72
  249.4 3.2 %collective-permute-done.8 = bf16[2,768,96]{1,2,0:T(8,128)(2,1)S(1)} collective-permute-done((bf16[2,768,96]{1,2,0:T(8,128)(2,1)S(1)}, bf16[2,768,96]{1,2,0:T(8,128)(2,1)S(1)}, u32[]{:S(2)}, u32[]{:S(2)}) %collective-permute-start.8) | collective-permute-done | bytes 294944 | tf_op jit(solution)/shard_map/ppermute | solution.py:72
  254.7 14.2 %all-to-all-start.2 = ((bf16[64,12,512]{2,1,0:T(8,128)(2,1)}), bf16[64,12,512]{2,1,0:T(8,128)(2,1)S(1)}, u32[]{:S(2)}, u32[]{:S(2)}) async-start(bf16[64,12,512]{2,1,0:T(8,128)(2,1)} %reshape.183), calls=%async_computation.2 | async-start | bytes 2097152 | tf_op jit(solution)/shard_map/all_to_all | solution.py:154
  269.5 1.8 fusion.17
  271.7 1.2 reshape_reshape.10
  274.8 1.2 reshape_reshape.9
  276.0 23.9 %all-to-all-done.2 = bf16[64,12,512]{2,1,0:T(8,128)(2,1)S(1)} async-done(((bf16[64,12,512]{2,1,0:T(8,128)(2,1)}), bf16[64,12,512]{2,1,0:T(8,128)(2,1)S(1)}, u32[]{:S(2)}, u32[]{:S(2)}) %all-to-all-start.2) | async-done | bytes 786464 | tf_op jit(solution)/shard_map/all_to_all | solution.py:154
  (79 shorter events, 19.9 us)
Async XLA Ops:
  0.6 5.9 %copy-start = (bf16[48,512]{1,0:T(8,128)(2,1)S(1)}, bf16[48,512]{1,0:T(8,128)(2,1)}, u32[]{:S(2)}) copy-start(bf16[48,512]{1,0:T(8,128)(2,1)} %param.8) | copy-start | bytes 147460
  0.6 6.7 %copy-start.4 = (bf16[1,768,512]{2,1,0:T(8,128)(2,1)S(1)}, bf16[1,768,512]{2,1,0:T(8,128)(2,1)}, u32[]{:S(2)}) copy-start(bf16[1,768,512]{2,1,0:T(8,128)(2,1)} %param.15) | copy-start | bytes 2359300
  7.4 1.1 copy-start.2
  7.6 1.2 copy-start.3
  12.1 16.6 %copy-start.9 = (s32[64]{0:T(128)S(1)}, s32[64]{0:T(128)}, u32[]{:S(2)}) copy-start(s32[64]{0:T(128)} %param.11) | copy-start | bytes 772
  12.1 90.3 %all-to-all-start = ((bf16[64,192,128]{2,1,0:T(8,128)(2,1)}), bf16[64,192,128]{2,1,0:T(8,128)(2,1)S(1)}, u32[]{:S(2)}, u32[]{:S(2)}) async-start(bf16[64,192,128]{2,1,0:T(8,128)(2,1)} %pad_maximum_fusion), calls=%async_computation | async-start | bytes 6291456 | tf_op jit(solution)/shard_map/all_to_all | solution.py:114
  107.9 145.7 %all-to-all-start.1 = ((bf16[64,144,128]{2,1,0:T(8,128)(2,1)}), bf16[64,144,128]{2,1,0:T(8,128)(2,1)}, u32[]{:S(2)}, u32[]{:S(2)}) async-start(bf16[64,144,128]{2,1,0:T(8,128)(2,1)} %gather_fusion.3), calls=%async_computation.1 | async-start | bytes 4718592 | tf_op jit(solution)/shard_map/all_to_all | solution.py:124
  146.4 52.2 %collective-permute-start.3 = (bf16[192,2048]{1,0:T(8,128)(2,1)}, bf16[192,2048]{1,0:T(8,128)(2,1)}, u32[]{:S(2)}, u32[]{:S(2)}) collective-permute-start(bf16[192,2048]{1,0:T(8,128)(2,1)} %pad_maximum_fusion.5), channel_id=1, source_target_pairs={{0,4},{4,0},{1,5},{5,1},{2,6},{6,2},{3,7},{7,3},{8,12},{12,8},{9,1... | collective-permute-start | bytes 2359304 | tf_op jit(solution)/shard_map/ppermute | solution.py:107
  149.3 51.1 %copy-start.1 = (bf16[64,48,128]{2,1,0:T(8,128)(2,1)S(1)}, bf16[64,48,128]{2,1,0:T(8,128)(2,1)}, u32[]{:S(2)}) copy-start(bf16[64,48,128]{2,1,0:T(8,128)(2,1)} %slice.45) | copy-start | bytes 2359300
  150.9 50.0 %collective-permute-start = (bf16[768,512]{1,0:T(8,128)(2,1)S(1)}, bf16[768,512]{1,0:T(8,128)(2,1)}, u32[]{:S(2)}, u32[]{:S(2)}) collective-permute-start(bf16[768,512]{1,0:T(8,128)(2,1)S(1)} %reshape.180), channel_id=1, source_target_pairs={{0,1},{1,2},{2,3},{3,0},{4,5},{5,6},{6,7},{7,4},{8,9},{9,10},{10,1... | collective-permute-start | bytes 2359304 | tf_op jit(solution)/shard_map/ppermute | solution.py:72
  154.0 46.9 %collective-permute-start.1 = (bf16[768,512]{1,0:T(8,128)(2,1)S(1)}, bf16[768,512]{1,0:T(8,128)(2,1)}, u32[]{:S(2)}, u32[]{:S(2)}) collective-permute-start(bf16[768,512]{1,0:T(8,128)(2,1)S(1)} %reshape.180), channel_id=1, source_target_pairs={{0,2},{1,3},{2,0},{3,1},{4,6},{5,7},{6,4},{7,5},{8,10},{9,11},{10,... | collective-permute-start | bytes 2359304 | tf_op jit(solution)/shard_map/ppermute | solution.py:72
  157.3 43.6 %collective-permute-start.2 = (bf16[768,512]{1,0:T(8,128)(2,1)S(1)}, bf16[768,512]{1,0:T(8,128)(2,1)}, u32[]{:S(2)}, u32[]{:S(2)}) collective-permute-start(bf16[768,512]{1,0:T(8,128)(2,1)S(1)} %reshape.180), channel_id=1, source_target_pairs={{0,3},{1,0},{2,1},{3,2},{4,7},{5,4},{6,5},{7,6},{8,11},{9,8},{10,9... | collective-permute-start | bytes 2359304 | tf_op jit(solution)/shard_map/ppermute | solution.py:72
  200.9 8.1 %copy-start.7 = (bf16[96,2048]{1,0:T(8,128)(2,1)S(1)}, bf16[96,2048]{1,0:T(8,128)(2,1)}, u32[]{:S(2)}) copy-start(bf16[96,2048]{1,0:T(8,128)(2,1)} %get-tuple-element.13) | copy-start | bytes 1179652
  200.9 8.1 %copy-start.6 = (bf16[96,2048]{1,0:T(8,128)(2,1)S(1)}, bf16[96,2048]{1,0:T(8,128)(2,1)}, u32[]{:S(2)}) copy-start(bf16[96,2048]{1,0:T(8,128)(2,1)} %get-tuple-element.18) | copy-start | bytes 1179652
  204.6 18.0 %collective-permute-start.4 = (f32[768,192]{0,1:T(8,128)}, f32[768,192]{0,1:T(8,128)S(1)}, u32[]{:S(2)}, u32[]{:S(2)}) collective-permute-start(f32[768,192]{0,1:T(8,128)} %convolution_bitcast_fusion), channel_id=1, source_target_pairs={{0,4},{4,0},{1,5},{5,1},{2,6},{6,2},{3,7},{7,3},{8,12},{12,8},{9,1... | collective-permute-start | bytes 1769480 | tf_op jit(solution)/shard_map/ppermute | solution.py:137
  225.3 18.2 %copy-start.5 = (bf16[1,768,512]{2,1,0:T(8,128)(2,1)S(1)}, bf16[1,768,512]{2,1,0:T(8,128)(2,1)}, u32[]{:S(2)}) copy-start(bf16[1,768,512]{2,1,0:T(8,128)(2,1)} %param.15) | copy-start | bytes 2359300
  225.5 7.2 %collective-permute-start.5 = (bf16[768,96]{0,1:T(8,128)(2,1)S(1)}, bf16[768,96]{0,1:T(8,128)(2,1)S(1)}, u32[]{:S(2)}, u32[]{:S(2)}) collective-permute-start(bf16[768,96]{0,1:T(8,128)(2,1)S(1)} %fusion.5), channel_id=1, source_target_pairs={{0,4},{4,0},{1,5},{5,1},{2,6},{6,2},{3,7},{7,3},{8,12},{12,8},{9,1... | collective-permute-start | bytes 442376 | tf_op jit(solution)/shard_map/ppermute | solution.py:142
  232.7 11.5 %collective-permute-start.6 = (bf16[2,768,96]{1,2,0:T(8,128)(2,1)S(1)}, bf16[2,768,96]{1,2,0:T(8,128)(2,1)S(1)}, u32[]{:S(2)}, u32[]{:S(2)}) collective-permute-start(bf16[2,768,96]{1,2,0:T(8,128)(2,1)S(1)} %get-tuple-element.16), channel_id=1, source_target_pairs={{0,1},{1,2},{2,3},{3,0},{4,5},{5,6},{6,7},{7,4},{8,9},{9,10},{10,1... | collective-permute-start | bytes 884744 | tf_op jit(solution)/shard_map/ppermute | solution.py:72
  236.0 13.3 %collective-permute-start.7 = (bf16[2,768,96]{1,2,0:T(8,128)(2,1)S(1)}, bf16[2,768,96]{1,2,0:T(8,128)(2,1)S(1)}, u32[]{:S(2)}, u32[]{:S(2)}) collective-permute-start(bf16[2,768,96]{1,2,0:T(8,128)(2,1)S(1)} %get-tuple-element.16), channel_id=1, source_target_pairs={{0,2},{1,3},{2,0},{3,1},{4,6},{5,7},{6,4},{7,5},{8,10},{9,11},{10,... | collective-permute-start | bytes 884744 | tf_op jit(solution)/shard_map/ppermute | solution.py:72
  240.0 12.6 %collective-permute-start.8 = (bf16[2,768,96]{1,2,0:T(8,128)(2,1)S(1)}, bf16[2,768,96]{1,2,0:T(8,128)(2,1)S(1)}, u32[]{:S(2)}, u32[]{:S(2)}) collective-permute-start(bf16[2,768,96]{1,2,0:T(8,128)(2,1)S(1)} %get-tuple-element.16), channel_id=1, source_target_pairs={{0,3},{1,0},{2,1},{3,2},{4,7},{5,4},{6,5},{7,6},{8,11},{9,8},{10,9... | collective-permute-start | bytes 884744 | tf_op jit(solution)/shard_map/ppermute | solution.py:72
  253.6 15.4 %copy-start.8 = (bf16[48,8]{0,1:T(8,128)(2,1)S(1)}, bf16[48,8]{0,1:T(8,128)(2,1)}, u32[]{:S(2)}) copy-start(bf16[48,8]{0,1:T(8,128)(2,1)} %param.10) | copy-start | bytes 2308
  254.7 45.1 %all-to-all-start.2 = ((bf16[64,12,512]{2,1,0:T(8,128)(2,1)}), bf16[64,12,512]{2,1,0:T(8,128)(2,1)S(1)}, u32[]{:S(2)}, u32[]{:S(2)}) async-start(bf16[64,12,512]{2,1,0:T(8,128)(2,1)} %reshape.183), calls=%async_computation.2 | async-start | bytes 2097152 | tf_op jit(solution)/shard_map/all_to_all | solution.py:154

commit v10 on v8

--- a/solution.py
+++ b/solution.py
@@ -79,7 +79,8 @@
     half = lax.axis_index("zlo")
     column = lax.axis_index("x")
     columns = lax.axis_size("x")
-    narrow_count = lax.axis_size("zlo") * columns
+    halves = lax.axis_size("zlo")
+    narrow_count = halves * columns
     narrow_index = half * columns + column
     gate_block = gate_weight[0]
     up_block = up_weight[0]
@@ -87,27 +88,30 @@
     rows, width = gate_block.shape
     depth, narrow_width = down_block.shape
     pair = [(0, 1), (1, 0)]
+    offsets = jnp.arange(columns, dtype=jnp.int32)
 
-    gate_halves = gate_block.reshape(rows, 2, width // 2)
-    up_halves = up_block.reshape(rows, 2, width // 2)
-    keep = jnp.concatenate(
-        [
-            lax.dynamic_index_in_dim(gate_halves, half, axis=1, keepdims=False),
-            lax.dynamic_index_in_dim(up_halves, half, axis=1, keepdims=False),
-        ],
-        axis=0,
+    both_weights = jnp.concatenate([gate_block, up_block], axis=0).reshape(
+        2 * rows, narrow_count, narrow_width
     )
-    give = jnp.concatenate(
-        [
-            lax.dynamic_index_in_dim(gate_halves, 1 - half, axis=1, keepdims=False),
-            lax.dynamic_index_in_dim(up_halves, 1 - half, axis=1, keepdims=False),
-        ],
-        axis=0,
-    )
-    taken = lax.ppermute(give, "zlo", pair)
+    weight_pieces = []
+    for shift in range(columns):
+        target = (column + shift) % columns
+        wanted = jnp.stack([half * columns + target, (1 - half) * columns + target])
+        piece = jnp.take(both_weights, wanted, axis=1, mode="clip").reshape(2 * rows, -1)
+        if shift:
+            piece = lax.ppermute(
+                piece, "x", [(i, (i + shift) % columns) for i in range(columns)]
+            )
+        weight_pieces.append(piece)
+    weights_here = jnp.stack(weight_pieces, axis=0)
+
+    partner_tokens = lax.ppermute(tokens, "zlo", pair)
+    wide_tokens = jnp.concatenate([tokens, partner_tokens], axis=1)
 
     dispatch, combine, capacity = slot_layout(route_ids, route_weight, old_place, groups)
-    outgoing = jnp.dot(dispatch, tokens, preferred_element_type=jnp.float32).astype(jnp.bfloat16)
+    outgoing = jnp.dot(dispatch, wide_tokens, preferred_element_type=jnp.float32).astype(
+        jnp.bfloat16
+    )
     packed = pack_weights(gate_block, up_block, down_block, groups)
     token_lanes = to_lanes(outgoing, groups)
     split_at = token_lanes.shape[1]
@@ -118,24 +122,19 @@
         concat_axis=0,
         tiled=True,
     )
-    slice_rows = first[:, :split_at].reshape(groups * capacity, narrow_width)
+    wide_rows = first[:, :split_at].reshape(groups * capacity, wide_tokens.shape[1])
     spread = first[:, split_at:]
     ordered = jnp.take(spread, partner, axis=0, mode="clip")
     arrived = lax.all_to_all(ordered, "expert", split_axis=0, concat_axis=0, tiled=True)
 
-    pieces, sources = ring_gather(slice_rows, "x", columns, column)
-    keep3 = jnp.take(keep.reshape(keep.shape[0], columns, narrow_width), sources, axis=1, mode="clip")
-    taken3 = jnp.take(
-        taken.reshape(taken.shape[0], columns, narrow_width), sources, axis=1, mode="clip"
+    parts = lax.dot_general(
+        wide_rows, weights_here, (((1,), (2,)), ((), ())), preferred_element_type=jnp.float32
     )
-    own_part = lax.dot_general(
-        pieces, keep3, (((0, 2), (1, 2)), ((), ())), preferred_element_type=jnp.float32
-    )
-    other_part = lax.dot_general(
-        pieces, taken3, (((0, 2), (1, 2)), ((), ())), preferred_element_type=jnp.float32
-    )
-    back = lax.ppermute(other_part.astype(jnp.bfloat16), "zlo", pair)
-    sums = own_part + back.astype(jnp.float32)
+    sums = parts[:, 0]
+    for shift in range(1, columns):
+        sums = sums + lax.ppermute(
+            parts[:, shift], "x", [(i, (i - shift) % columns) for i in range(columns)]
+        )
     gate_sum = sums[:, :rows]
     up_sum = sums[:, rows:]
     hidden = (jax.nn.silu(gate_sum) * up_sum).astype(jnp.bfloat16)

time: 301 us -> 308 us (1.023)
  the two profiles are of different devices: /device:TPU:16 before, /device:TPU:22 now
where the time goes in v10:
time: 308 us; the launch traced here: 306 us
  waiting for transfers between devices  139 us (45%)
  starting transfers between devices  102 us (33%)
  local copies, waits for them, and re-layouts  44.9 us (15%)
  other arithmetic  11.5 us (4%)
  matrix products  7.79 us (3%)
    all_to_all x1, waiting for transfers between devices, body(): lax.all_to_all(jnp.concatenate([token_lanes, packed], axis=1), 'expert',...  84.9 us
    all_to_all x1, starting transfers between devices, body(): lax.all_to_all(ordered, 'expert', split_axis=0, concat_axis=0, tiled=True)  28.5 us
    all_to_all x1, waiting for transfers between devices, body(): lax.all_to_all(produced.reshape(groups, capacity, -1), 'expert', split_ax...  24.3 us
    ppermute x7, starting transfers between devices, ring_gather(): lax.ppermute(value, axis, [(i, (i + shift) % size) for i in range(size)])  24 us
    ppermute x3, waiting for transfers between devices, body(): lax.ppermute(parts[:, shift], 'x', [(i, (i - shift) % columns) for i in r...  23.6 us
    all_to_all x1, starting transfers between devices, body(): lax.all_to_all(jnp.concatenate([token_lanes, packed], axis=1), 'expert',...  15.7 us
    all_to_all x1, starting transfers between devices, body(): lax.all_to_all(produced.reshape(groups, capacity, -1), 'expert', split_ax...  12.7 us
    ppermute x3, starting transfers between devices, body(): lax.ppermute(parts[:, shift], 'x', [(i, (i - shift) % columns) for i in r...  9.55 us
  transfers between devices with their start and end apart: 17, of which 7 were waited for; matrix products, arithmetic and copies ran while one was open for 16% of the time, Pallas kernels for 0%

profile of v10, /device:TPU:22, one launch (start us, length us, event | category | flops | bytes accessed | tf_op | source)
XLA Modules:
  0.0 306.3 jit_solution(194958168642098868)
XLA Ops:
  0.6 4.3 %collective-permute-start = (bf16[48,512]{1,0:T(8,128)(2,1)}, bf16[48,512]{1,0:T(8,128)(2,1)S(1)}, u32[]{:S(2)}, u32[]{:S(2)}) collective-permute-start(bf16[48,512]{1,0:T(8,128)(2,1)} %param.8), channel_id=1, source_target_pairs={{0,4},{4,0},{1,5},{5,1},{2,6},{6,2},{3,7},{7,3},{8,12},{12,8},{9,1... | collective-permute-start | bytes 147464 | tf_op jit(solution)/shard_map/ppermute | solution.py:108
  17.3 3.7 %reshape.131 = bf16[64,96,128]{2,1,0:T(8,128)(2,1)} reshape(bf16[768,1024]{1,0:T(8,128)(2,1)} %convolution_convert_fusion) | data formatting | bytes 3145728 | tf_op jit(solution)/shard_map/reshape | solution.py:66
  21.0 3.5 %pad_maximum_fusion = bf16[64,240,128]{2,1,0:T(8,128)(2,1)} fusion(bf16[64,144,128]{2,1,0:T(8,128)(2,1)S(1)} %bitcast.106, bf16[64,96,128]{2,1,0:T(8,128)(2,1)} %reshape.131), kind=kLoop, calls=%fused_computation.6 | loop fusion | flops 7864320 | bytes 7864320 | tf_op jit(solution)/shard_map/concatenate | solution.py:119
  24.6 15.7 %all-to-all-start = ((bf16[64,240,128]{2,1,0:T(8,128)(2,1)}), bf16[64,240,128]{2,1,0:T(8,128)(2,1)}, u32[]{:S(2)}, u32[]{:S(2)}) async-start(bf16[64,240,128]{2,1,0:T(8,128)(2,1)} %pad_maximum_fusion), calls=%async_computation | async-start | bytes 7864320 | tf_op jit(solution)/shard_map/all_to_all | solution.py:118
  43.0 3.3 %collective-permute-start.2 = (bf16[192,1024]{1,0:T(8,128)(2,1)S(1)}, bf16[192,1024]{1,0:T(8,128)(2,1)}, u32[]{:S(2)}, u32[]{:S(2)}) collective-permute-start(bf16[192,1024]{1,0:T(8,128)(2,1)S(1)} %bitcast.123), channel_id=1, source_target_pairs={{0,2},{1,3},{2,0},{3,1},{4,6},{5,7},{6,4},{7,5},{8,10},{9,11},{10,... | collective-permute-start | bytes 1179656 | tf_op jit(solution)/shard_map/ppermute | solution.py:102
  47.7 1.9 collective-permute-start.3
  49.7 84.9 %all-to-all-done = bf16[64,240,128]{2,1,0:T(8,128)(2,1)} async-done(((bf16[64,240,128]{2,1,0:T(8,128)(2,1)}), bf16[64,240,128]{2,1,0:T(8,128)(2,1)}, u32[]{:S(2)}, u32[]{:S(2)}) %all-to-all-start) | async-done | bytes 3932192 | tf_op jit(solution)/shard_map/all_to_all | solution.py:118
  136.4 2.3 gather_fusion.5
  138.7 28.5 %all-to-all-start.1 = ((bf16[64,144,128]{2,1,0:T(8,128)(2,1)}), bf16[64,144,128]{2,1,0:T(8,128)(2,1)S(1)}, u32[]{:S(2)}, u32[]{:S(2)}) async-start(bf16[64,144,128]{2,1,0:T(8,128)(2,1)} %gather_fusion.5), calls=%async_computation.1 | async-start | bytes 4718592 | tf_op jit(solution)/shard_map/all_to_all | solution.py:128
  167.3 2.0 gather_fusion.1
  170.1 1.9 collective-permute-start.1
  172.0 2.0 gather_fusion
  174.7 2.7 slice.65
  177.4 3.7 %reshape.195 = bf16[768,1024,1]{1,0,2:T(8,128)(2,1)} reshape(bf16[64,96,128]{2,1,0:T(8,128)(2,1)} %slice.65) | data formatting | bytes 3145728 | tf_op jit(solution)/shard_map/reshape | solution.py:125
  181.1 2.4 collective-permute-done.1
  183.5 3.1 %fusion = f32[768,4,192]{0,2,1:T(8,128)S(1)} fusion(bf16[768,1024,1]{1,0,2:T(8,128)(2,1)} %reshape.195, bf16[1,192,1024]{2,1,0:T(8,128)(2,1)} %bitcast.20, bf16[1,192,1024]{2,1,0:T(8,128)(2,1)} %bitcast.16, bf16[1,192,1024]{2,1,0:T(8,128)(2,1)} %bitcast.12, bf16[1,192,1024]{2,1,0:T(8,128)(2,1)S(1)} %stack_reshape.3), kind=kOutput, calls=%fused_computation.9 | convolution fusion | flops 1214251008 | bytes 5505024 | tf_op jit(solution)/shard_map/dot_general | solution.py:130
  188.6 1.9 collective-permute-start.4
  190.5 4.9 %collective-permute-start.5 = (f32[768,192]{0,1:T(8,128)}, f32[768,192]{0,1:T(8,128)}, u32[]{:S(2)}, u32[]{:S(2)}) collective-permute-start(f32[768,192]{0,1:T(8,128)} %get-tuple-element.15), channel_id=1, source_target_pairs={{0,2},{1,3},{2,0},{3,1},{4,6},{5,7},{6,4},{7,5},{8,10},{9,11},{10,... | collective-permute-start | bytes 1769480 | tf_op jit(solution)/shard_map/ppermute | solution.py:135
  195.4 2.8 collective-permute-start.6
  198.2 9.7 %collective-permute-done.4 = f32[768,192]{0,1:T(8,128)} collective-permute-done((f32[768,192]{0,1:T(8,128)}, f32[768,192]{0,1:T(8,128)}, u32[]{:S(2)}, u32[]{:S(2)}) %collective-permute-start.4) | collective-permute-done | bytes 589856 | tf_op jit(solution)/shard_map/ppermute | solution.py:135
  207.9 11.4 %collective-permute-done.5 = f32[768,192]{0,1:T(8,128)} collective-permute-done((f32[768,192]{0,1:T(8,128)}, f32[768,192]{0,1:T(8,128)}, u32[]{:S(2)}, u32[]{:S(2)}) %collective-permute-start.5) | collective-permute-done | bytes 589856 | tf_op jit(solution)/shard_map/ppermute | solution.py:135
  219.2 2.5 collective-permute-done.6
  227.7 2.0 collective-permute-start.8
  229.7 6.3 %collective-permute-start.9 = (bf16[768,96]{0,1:T(8,128)(2,1)S(1)}, bf16[768,96]{0,1:T(8,128)(2,1)S(1)}, u32[]{:S(2)}, u32[]{:S(2)}) collective-permute-start(bf16[768,96]{0,1:T(8,128)(2,1)S(1)} %get-tuple-element.9), channel_id=1, source_target_pairs={{0,3},{1,4},{2,5},{3,6},{4,7},{5,0},{6,1},{7,2},{8,11},{9,12},{10,... | collective-permute-start | bytes 442376 | tf_op jit(solution)/shard_map/ppermute | solution.py:72
  236.0 1.9 collective-permute-start.10
  237.9 4.8 %collective-permute-start.11 = (bf16[768,96]{0,1:T(8,128)(2,1)S(1)}, bf16[768,96]{0,1:T(8,128)(2,1)S(1)}, u32[]{:S(2)}, u32[]{:S(2)}) collective-permute-start(bf16[768,96]{0,1:T(8,128)(2,1)S(1)} %get-tuple-element.9), channel_id=1, source_target_pairs={{0,5},{1,6},{2,7},{3,0},{4,1},{5,2},{6,3},{7,4},{8,13},{9,14},{10,... | collective-permute-start | bytes 442376 | tf_op jit(solution)/shard_map/ppermute | solution.py:72
  242.8 5.1 %collective-permute-start.12 = (bf16[768,96]{0,1:T(8,128)(2,1)S(1)}, bf16[768,96]{0,1:T(8,128)(2,1)S(1)}, u32[]{:S(2)}, u32[]{:S(2)}) collective-permute-start(bf16[768,96]{0,1:T(8,128)(2,1)S(1)} %get-tuple-element.9), channel_id=1, source_target_pairs={{0,6},{1,7},{2,0},{3,1},{4,2},{5,3},{6,4},{7,5},{8,14},{9,15},{10,... | collective-permute-start | bytes 442376 | tf_op jit(solution)/shard_map/ppermute | solution.py:72
  248.6 1.9 collective-permute-start.13
  253.9 3.8 %collective-permute-done.13 = bf16[768,96]{0,1:T(8,128)(2,1)S(1)} collective-permute-done((bf16[768,96]{0,1:T(8,128)(2,1)S(1)}, bf16[768,96]{0,1:T(8,128)(2,1)S(1)}, u32[]{:S(2)}, u32[]{:S(2)}) %collective-permute-start.13) | collective-permute-done | bytes 147488 | tf_op jit(solution)/shard_map/ppermute | solution.py:72
  258.4 2.1 bitcast_convert_fusion
  261.7 12.7 %all-to-all-start.2 = ((bf16[64,12,512]{2,1,0:T(8,128)(2,1)}), bf16[64,12,512]{2,1,0:T(8,128)(2,1)S(1)}, u32[]{:S(2)}, u32[]{:S(2)}) async-start(bf16[64,12,512]{2,1,0:T(8,128)(2,1)} %reshape.138), calls=%async_computation.2 | async-start | bytes 2097152 | tf_op jit(solution)/shard_map/all_to_all | solution.py:148
  280.9 24.3 %all-to-all-done.2 = bf16[64,12,512]{2,1,0:T(8,128)(2,1)S(1)} async-done(((bf16[64,12,512]{2,1,0:T(8,128)(2,1)}), bf16[64,12,512]{2,1,0:T(8,128)(2,1)S(1)}, u32[]{:S(2)}, u32[]{:S(2)}) %all-to-all-start.2) | async-done | bytes 786464 | tf_op jit(solution)/shard_map/all_to_all | solution.py:148
  (103 shorter events, 41.0 us)
Async XLA Ops:
  0.6 15.0 %collective-permute-start = (bf16[48,512]{1,0:T(8,128)(2,1)}, bf16[48,512]{1,0:T(8,128)(2,1)S(1)}, u32[]{:S(2)}, u32[]{:S(2)}) collective-permute-start(bf16[48,512]{1,0:T(8,128)(2,1)} %param.8), channel_id=1, source_target_pairs={{0,4},{4,0},{1,5},{5,1},{2,6},{6,2},{3,7},{7,3},{8,12},{12,8},{9,1... | collective-permute-start | bytes 147464 | tf_op jit(solution)/shard_map/ppermute | solution.py:108
  12.0 1.1 copy-start.3
  12.2 1.3 copy-start.4
  13.6 0.6 copy-start.9
  14.6 0.9 copy-start.11
  24.6 110.0 %all-to-all-start = ((bf16[64,240,128]{2,1,0:T(8,128)(2,1)}), bf16[64,240,128]{2,1,0:T(8,128)(2,1)}, u32[]{:S(2)}, u32[]{:S(2)}) async-start(bf16[64,240,128]{2,1,0:T(8,128)(2,1)} %pad_maximum_fusion), calls=%async_computation | async-start | bytes 7864320 | tf_op jit(solution)/shard_map/all_to_all | solution.py:118
  40.3 1.1 copy-start.5
  42.4 5.3 %copy-start = (bf16[192,8,512]{2,0,1:T(8,128)(2,1)}, bf16[192,8,512]{2,0,1:T(8,128)(2,1)S(1)}, u32[]{:S(2)}) copy-start(bf16[192,8,512]{2,0,1:T(8,128)(2,1)S(1)} %copy_dynamic-update-slice_fusion) | copy-start | bytes 4718596
  42.4 7.3 %copy-start.13 = (s32[64]{0:T(128)S(1)}, s32[64]{0:T(128)}, u32[]{:S(2)}) copy-start(s32[64]{0:T(128)} %param.11) | copy-start | bytes 772
  43.0 138.1 %collective-permute-start.2 = (bf16[192,1024]{1,0:T(8,128)(2,1)S(1)}, bf16[192,1024]{1,0:T(8,128)(2,1)}, u32[]{:S(2)}, u32[]{:S(2)}) collective-permute-start(bf16[192,1024]{1,0:T(8,128)(2,1)S(1)} %bitcast.123), channel_id=1, source_target_pairs={{0,2},{1,3},{2,0},{3,1},{4,6},{5,7},{6,4},{7,5},{8,10},{9,11},{10,... | collective-permute-start | bytes 1179656 | tf_op jit(solution)/shard_map/ppermute | solution.py:102
  47.7 133.4 %collective-permute-start.3 = (bf16[192,1024]{1,0:T(8,128)(2,1)}, bf16[192,1024]{1,0:T(8,128)(2,1)}, u32[]{:S(2)}, u32[]{:S(2)}) collective-permute-start(bf16[192,1024]{1,0:T(8,128)(2,1)} %bitcast.49), channel_id=1, source_target_pairs={{0,3},{1,0},{2,1},{3,2},{4,7},{5,4},{6,5},{7,6},{8,11},{9,8},{10,9... | collective-permute-start | bytes 1179656 | tf_op jit(solution)/shard_map/ppermute | solution.py:102
  138.7 121.8 %all-to-all-start.1 = ((bf16[64,144,128]{2,1,0:T(8,128)(2,1)}), bf16[64,144,128]{2,1,0:T(8,128)(2,1)S(1)}, u32[]{:S(2)}, u32[]{:S(2)}) async-start(bf16[64,144,128]{2,1,0:T(8,128)(2,1)} %gather_fusion.5), calls=%async_computation.1 | async-start | bytes 4718592 | tf_op jit(solution)/shard_map/all_to_all | solution.py:128
  170.1 13.4 %collective-permute-start.1 = (bf16[192,1024]{1,0:T(8,128)(2,1)}, bf16[192,1024]{1,0:T(8,128)(2,1)}, u32[]{:S(2)}, u32[]{:S(2)}) collective-permute-start(bf16[192,1024]{1,0:T(8,128)(2,1)} %bitcast.45), channel_id=1, source_target_pairs={{0,1},{1,2},{2,3},{3,0},{4,5},{5,6},{6,7},{7,4},{8,9},{9,10},{10,1... | collective-permute-start | bytes 1179656 | tf_op jit(solution)/shard_map/ppermute | solution.py:102
  186.6 2.0 copy-start.7
  188.6 19.3 %collective-permute-start.4 = (f32[768,192]{0,1:T(8,128)}, f32[768,192]{0,1:T(8,128)}, u32[]{:S(2)}, u32[]{:S(2)}) collective-permute-start(f32[768,192]{0,1:T(8,128)} %get-tuple-element.13), channel_id=1, source_target_pairs={{0,3},{1,0},{2,1},{3,2},{4,7},{5,4},{6,5},{7,6},{8,11},{9,8},{10,9... | collective-permute-start | bytes 1769480 | tf_op jit(solution)/shard_map/ppermute | solution.py:135
  190.5 28.7 %collective-permute-start.5 = (f32[768,192]{0,1:T(8,128)}, f32[768,192]{0,1:T(8,128)}, u32[]{:S(2)}, u32[]{:S(2)}) collective-permute-start(f32[768,192]{0,1:T(8,128)} %get-tuple-element.15), channel_id=1, source_target_pairs={{0,2},{1,3},{2,0},{3,1},{4,6},{5,7},{6,4},{7,5},{8,10},{9,11},{10,... | collective-permute-start | bytes 1769480 | tf_op jit(solution)/shard_map/ppermute | solution.py:135
  195.4 26.4 %collective-permute-start.6 = (f32[768,192]{0,1:T(8,128)}, f32[768,192]{0,1:T(8,128)}, u32[]{:S(2)}, u32[]{:S(2)}) collective-permute-start(f32[768,192]{0,1:T(8,128)} %get-tuple-element.14), channel_id=1, source_target_pairs={{0,1},{1,2},{2,3},{3,0},{4,5},{5,6},{6,7},{7,4},{8,9},{9,10},{10,1... | collective-permute-start | bytes 1769480 | tf_op jit(solution)/shard_map/ppermute | solution.py:135
  198.1 28.0 %copy-start.6 = (bf16[1,768,512]{2,1,0:T(8,128)(2,1)S(1)}, bf16[1,768,512]{2,1,0:T(8,128)(2,1)}, u32[]{:S(2)}) copy-start(bf16[1,768,512]{2,1,0:T(8,128)(2,1)} %param.15) | copy-start | bytes 2359300
  224.2 18.6 %collective-permute-start.7 = (bf16[768,96]{0,1:T(8,128)(2,1)S(1)}, bf16[768,96]{0,1:T(8,128)(2,1)S(1)}, u32[]{:S(2)}, u32[]{:S(2)}) collective-permute-start(bf16[768,96]{0,1:T(8,128)(2,1)S(1)} %get-tuple-element.9), channel_id=1, source_target_pairs={{0,1},{1,2},{2,3},{3,4},{4,5},{5,6},{6,7},{7,0},{8,9},{9,10},{10,1... | collective-permute-start | bytes 442376 | tf_op jit(solution)/shard_map/ppermute | solution.py:72
  227.6 30.7 %copy-start.8 = (bf16[8,96,512]{2,1,0:T(8,128)(2,1)S(1)}, bf16[8,96,512]{2,1,0:T(8,128)(2,1)}, u32[]{:S(2)}) copy-start(bf16[8,96,512]{2,1,0:T(8,128)(2,1)} %gather_fusion.4) | copy-start | bytes 2359300
  227.7 20.9 %collective-permute-start.8 = (bf16[768,96]{0,1:T(8,128)(2,1)S(1)}, bf16[768,96]{0,1:T(8,128)(2,1)S(1)}, u32[]{:S(2)}, u32[]{:S(2)}) collective-permute-start(bf16[768,96]{0,1:T(8,128)(2,1)S(1)} %get-tuple-element.9), channel_id=1, source_target_pairs={{0,2},{1,3},{2,4},{3,5},{4,6},{5,7},{6,0},{7,1},{8,10},{9,11},{10,... | collective-permute-start | bytes 442376 | tf_op jit(solution)/shard_map/ppermute | solution.py:72
  229.7 21.5 %collective-permute-start.9 = (bf16[768,96]{0,1:T(8,128)(2,1)S(1)}, bf16[768,96]{0,1:T(8,128)(2,1)S(1)}, u32[]{:S(2)}, u32[]{:S(2)}) collective-permute-start(bf16[768,96]{0,1:T(8,128)(2,1)S(1)} %get-tuple-element.9), channel_id=1, source_target_pairs={{0,3},{1,4},{2,5},{3,6},{4,7},{5,0},{6,1},{7,2},{8,11},{9,12},{10,... | collective-permute-start | bytes 442376 | tf_op jit(solution)/shard_map/ppermute | solution.py:72
  236.0 15.8 %collective-permute-start.10 = (bf16[768,96]{0,1:T(8,128)(2,1)S(1)}, bf16[768,96]{0,1:T(8,128)(2,1)S(1)}, u32[]{:S(2)}, u32[]{:S(2)}) collective-permute-start(bf16[768,96]{0,1:T(8,128)(2,1)S(1)} %get-tuple-element.9), channel_id=1, source_target_pairs={{0,4},{1,5},{2,6},{3,7},{4,0},{5,1},{6,2},{7,3},{8,12},{9,13},{10,... | collective-permute-start | bytes 442376 | tf_op jit(solution)/shard_map/ppermute | solution.py:72
  237.9 14.6 %collective-permute-start.11 = (bf16[768,96]{0,1:T(8,128)(2,1)S(1)}, bf16[768,96]{0,1:T(8,128)(2,1)S(1)}, u32[]{:S(2)}, u32[]{:S(2)}) collective-permute-start(bf16[768,96]{0,1:T(8,128)(2,1)S(1)} %get-tuple-element.9), channel_id=1, source_target_pairs={{0,5},{1,6},{2,7},{3,0},{4,1},{5,2},{6,3},{7,4},{8,13},{9,14},{10,... | collective-permute-start | bytes 442376 | tf_op jit(solution)/shard_map/ppermute | solution.py:72
  242.8 10.4 %collective-permute-start.12 = (bf16[768,96]{0,1:T(8,128)(2,1)S(1)}, bf16[768,96]{0,1:T(8,128)(2,1)S(1)}, u32[]{:S(2)}, u32[]{:S(2)}) collective-permute-start(bf16[768,96]{0,1:T(8,128)(2,1)S(1)} %get-tuple-element.9), channel_id=1, source_target_pairs={{0,6},{1,7},{2,0},{3,1},{4,2},{5,3},{6,4},{7,5},{8,14},{9,15},{10,... | collective-permute-start | bytes 442376 | tf_op jit(solution)/shard_map/ppermute | solution.py:72
  248.6 9.1 %collective-permute-start.13 = (bf16[768,96]{0,1:T(8,128)(2,1)S(1)}, bf16[768,96]{0,1:T(8,128)(2,1)S(1)}, u32[]{:S(2)}, u32[]{:S(2)}) collective-permute-start(bf16[768,96]{0,1:T(8,128)(2,1)S(1)} %get-tuple-element.9), channel_id=1, source_target_pairs={{0,7},{1,0},{2,1},{3,2},{4,3},{5,4},{6,5},{7,6},{8,15},{9,8},{10,9... | collective-permute-start | bytes 442376 | tf_op jit(solution)/shard_map/ppermute | solution.py:72
  260.5 13.9 %copy-start.12 = (bf16[48,8]{0,1:T(8,128)(2,1)S(1)}, bf16[48,8]{0,1:T(8,128)(2,1)}, u32[]{:S(2)}) copy-start(bf16[48,8]{0,1:T(8,128)(2,1)} %param.10) | copy-start | bytes 2308
  260.5 14.0 %copy-start.10 = (s32[48,8]{1,0:T(8,128)S(1)}, s32[48,8]{1,0:T(8,128)}, u32[]{:S(2)}) copy-start(s32[48,8]{1,0:T(8,128)} %copy-done.9) | copy-start | bytes 4612
  261.7 43.6 %all-to-all-start.2 = ((bf16[64,12,512]{2,1,0:T(8,128)(2,1)}), bf16[64,12,512]{2,1,0:T(8,128)(2,1)S(1)}, u32[]{:S(2)}, u32[]{:S(2)}) async-start(bf16[64,12,512]{2,1,0:T(8,128)(2,1)} %reshape.138), calls=%async_computation.2 | async-start | bytes 2097152 | tf_op jit(solution)/shard_map/all_to_all | solution.py:148
  276.3 1.5 copy-start.2
  277.8 1.6 copy-start.1

commit v11 on v7

--- a/solution.py
+++ b/solution.py
@@ -111,8 +111,11 @@
     packed = pack_weights(gate_block, up_block, down_block, groups)
     token_lanes = to_lanes(outgoing, groups)
     split_at = token_lanes.shape[1]
+    room = jnp.concatenate(
+        [jnp.zeros(token_lanes.shape, token_lanes.dtype), packed], axis=1
+    )
     first = lax.all_to_all(
-        jnp.concatenate([token_lanes, packed], axis=1),
+        lax.dynamic_update_slice_in_dim(room, token_lanes, 0, axis=1),
         "expert",
         split_axis=0,
         concat_axis=0,
@@ -123,11 +126,13 @@
     ordered = jnp.take(spread, partner, axis=0, mode="clip")
     arrived = lax.all_to_all(ordered, "expert", split_axis=0, concat_axis=0, tiled=True)
 
-    pieces, sources = ring_gather(slice_rows, "x", columns, column)
+    sources = (column - jnp.arange(columns, dtype=jnp.int32)) % columns
     keep3 = jnp.take(keep.reshape(keep.shape[0], columns, narrow_width), sources, axis=1, mode="clip")
     taken3 = jnp.take(
         taken.reshape(taken.shape[0], columns, narrow_width), sources, axis=1, mode="clip"
     )
+    keep3, taken3, slice_rows, spread = lax.optimization_barrier((keep3, taken3, slice_rows, spread))
+    pieces, sources = ring_gather(slice_rows, "x", columns, column)
     own_part = lax.dot_general(
         pieces, keep3, (((0, 2), (1, 2)), ((), ())), preferred_element_type=jnp.float32
     )

time: 299 us -> 313 us (1.047)
  waiting for transfers between devices: 127 us -> 150 us
  starting transfers between devices: 97.1 us -> 86.5 us
    ppermute x1, waiting for transfers between devices: 0.01 us -> 64.5 us  [body(): taken = lax.ppermute(give, 'zlo', pair)]
    all_to_all x1, waiting for transfers between devices: 54.1 us -> 0.01 us  [body(): lax.all_to_all(lax.dynamic_update_slice_in_dim(room, token_lanes, 0, axis...]
    ppermute x10, waiting for transfers between devices: 0.03 us -> 10.6 us  [ring_gather(): lax.ppermute(value, axis, [(i, (i + shift) % size) for i in range(size)])]
    all_to_all x1, starting transfers between devices: 22.1 us -> 16.7 us  [body(): lax.all_to_all(ordered, 'expert', split_axis=0, concat_axis=0, tiled=True)]
    ppermute x10, starting transfers between devices: 38.8 us -> 34.9 us  [ring_gather(): lax.ppermute(value, axis, [(i, (i + shift) % size) for i in range(size)])]
    unnamed x36 -> x32, local copies, waits for them, and re-layouts: 7.9 us -> 7.87 us
  transfers between devices with their start and end apart: 15 -> 15, of which waited for: 3 -> 5; matrix products, arithmetic and copies ran while one was open for 20% -> 18% of each run, Pallas kernels for 0% -> 0%
where the time goes in v11:
time: 313 us; the launch traced here: 312 us
  waiting for transfers between devices  150 us (48%)
  starting transfers between devices  86.5 us (28%)
  local copies, waits for them, and re-layouts  53.3 us (17%)
  matrix products  10.8 us (3%)
  other arithmetic  10.5 us (3%)
    ppermute x1, waiting for transfers between devices, body(): taken = lax.ppermute(give, 'zlo', pair)  64.5 us
    ppermute x1, waiting for transfers between devices, body(): back = lax.ppermute(other_part, 'zlo', pair)  51.6 us
    ppermute x10, starting transfers between devices, ring_gather(): lax.ppermute(value, axis, [(i, (i + shift) % size) for i in range(size)])  34.9 us
    all_to_all x1, waiting for transfers between devices, body(): lax.all_to_all(produced.reshape(groups, capacity, -1), 'expert', split_ax...  23 us
    all_to_all x1, starting transfers between devices, body(): lax.all_to_all(ordered, 'expert', split_axis=0, concat_axis=0, tiled=True)  16.7 us
    all_to_all x1, starting transfers between devices, body(): lax.all_to_all(lax.dynamic_update_slice_in_dim(room, token_lanes, 0, axis...  16.5 us
    all_to_all x1, starting transfers between devices, body(): lax.all_to_all(produced.reshape(groups, capacity, -1), 'expert', split_ax...  13 us
    ppermute x10, waiting for transfers between devices, ring_gather(): lax.ppermute(value, axis, [(i, (i + shift) % size) for i in range(size)])  10.6 us
  transfers between devices with their start and end apart: 15, of which 5 were waited for; matrix products, arithmetic and copies ran while one was open for 18% of the time, Pallas kernels for 0%

profile of v11, /device:TPU:16, one launch (start us, length us, event | category | flops | bytes accessed | tf_op | source)
XLA Modules:
  0.0 311.9 jit_solution(4276923445540216871)
XLA Ops:
  10.1 2.1 pad_maximum_fusion
  12.1 16.5 %all-to-all-start = ((bf16[64,192,128]{2,1,0:T(8,128)(2,1)}), bf16[64,192,128]{2,1,0:T(8,128)(2,1)S(1)}, u32[]{:S(2)}, u32[]{:S(2)}) async-start(bf16[64,192,128]{2,1,0:T(8,128)(2,1)} %pad_maximum_fusion), calls=%async_computation | async-start | bytes 6291456 | tf_op jit(solution)/shard_map/all_to_all | solution.py:117
  28.6 3.3 %reshape_squeeze.18 = bf16[96,2,2048]{2,1,0:T(2,128)(2,1)} reshape(bf16[1,96,4096]{2,1,0:T(8,128)(2,1)} %param.13) | data formatting | bytes 1572864 | tf_op jit(solution)/shard_map/reshape;squeeze | solution.py:91
  31.9 3.2 %reshape_squeeze.19 = bf16[96,2,2048]{2,1,0:T(2,128)(2,1)} reshape(bf16[1,96,4096]{2,1,0:T(8,128)(2,1)} %param.14) | data formatting | bytes 1572864 | tf_op jit(solution)/shard_map/reshape;squeeze | solution.py:92
  35.1 9.0 %constant_dynamic-slice_fusion = (bf16[96,1,2048]{2,1,0:T(2,128)(2,1)S(1)}, bf16[96,2048]{1,0:T(8,128)(2,1)}, bf16[96,2048]{1,0:T(8,128)(2,1)}, bf16[96,1,2048]{2,1,0:T(2,128)(2,1)S(1)}) fusion(bf16[96,2,2048]{2,1,0:T(2,128)(2,1)} %reshape_squeeze.19, s32[]{:T(128)S(6)} %select_n.43, s32[]{:T(128)S(6)} %select_n.41, bf16[96,2,2048]{2,1,0:T(2,128)(2,1)} %reshape_squeeze.18), kind=kLoop, calls=%fused_computation.57 | loop fusion | bytes 3145736 | tf_op jit(solution)/shard_map/jit(dynamic_index_in_dim)/dynamic_slice | solution.py:103
  45.5 3.4 %collective-permute-start = (bf16[192,2048]{1,0:T(8,128)(2,1)}, bf16[192,2048]{1,0:T(8,128)(2,1)}, u32[]{:S(2)}, u32[]{:S(2)}) collective-permute-start(bf16[192,2048]{1,0:T(8,128)(2,1)} %pad_maximum_fusion.4), channel_id=1, source_target_pairs={{0,4},{4,0},{1,5},{5,1},{2,6},{6,2},{3,7},{7,3},{8,12},{12,8},{9,1... | collective-permute-start | bytes 2359304 | tf_op jit(solution)/shard_map/ppermute | solution.py:107
  51.9 2.6 gather_fusion
  54.5 64.5 %collective-permute-done = bf16[192,2048]{1,0:T(8,128)(2,1)} collective-permute-done((bf16[192,2048]{1,0:T(8,128)(2,1)}, bf16[192,2048]{1,0:T(8,128)(2,1)}, u32[]{:S(2)}, u32[]{:S(2)}) %collective-permute-start) | collective-permute-done | bytes 786464 | tf_op jit(solution)/shard_map/ppermute | solution.py:107
  119.0 2.1 copy.79
  121.1 2.6 gather_fusion.1
  124.7 2.3 reshape.169
  128.5 2.5 collective-permute-start.1
  131.0 5.0 %collective-permute-start.2 = (bf16[768,512]{1,0:T(8,128)(2,1)}, bf16[768,512]{1,0:T(8,128)(2,1)}, u32[]{:S(2)}, u32[]{:S(2)}) collective-permute-start(bf16[768,512]{1,0:T(8,128)(2,1)} %reshape.169), channel_id=1, source_target_pairs={{0,2},{1,3},{2,0},{3,1},{4,6},{5,7},{6,4},{7,5},{8,10},{9,11},{10,... | collective-permute-start | bytes 2359304 | tf_op jit(solution)/shard_map/ppermute | solution.py:72
  136.1 3.3 %collective-permute-start.3 = (bf16[768,512]{1,0:T(8,128)(2,1)}, bf16[768,512]{1,0:T(8,128)(2,1)}, u32[]{:S(2)}, u32[]{:S(2)}) collective-permute-start(bf16[768,512]{1,0:T(8,128)(2,1)} %reshape.169), channel_id=1, source_target_pairs={{0,3},{1,0},{2,1},{3,2},{4,7},{5,4},{6,5},{7,6},{8,11},{9,8},{10,9... | collective-permute-start | bytes 2359304 | tf_op jit(solution)/shard_map/ppermute | solution.py:72
  139.5 3.9 %gather_fusion.3 = bf16[64,144,128]{2,1,0:T(8,128)(2,1)} fusion(bf16[64,144,128]{2,1,0:T(8,128)(2,1)} %slice.46, s32[1024]{0:T(1024)S(1)} %pad_clamp_fusion), kind=kCustom, calls=%fused_computation.3 | custom fusion | bytes 4718848 | tf_op jit(solution)/shard_map/jit(_take)/gather | solution.py:126
  143.4 16.7 %all-to-all-start.1 = ((bf16[64,144,128]{2,1,0:T(8,128)(2,1)}), bf16[64,144,128]{2,1,0:T(8,128)(2,1)S(1)}, u32[]{:S(2)}, u32[]{:S(2)}) async-start(bf16[64,144,128]{2,1,0:T(8,128)(2,1)} %gather_fusion.3), calls=%async_computation.1 | async-start | bytes 4718592 | tf_op jit(solution)/shard_map/all_to_all | solution.py:127
  160.1 8.6 %collective-permute-done.2 = bf16[768,512]{1,0:T(8,128)(2,1)} collective-permute-done((bf16[768,512]{1,0:T(8,128)(2,1)}, bf16[768,512]{1,0:T(8,128)(2,1)}, u32[]{:S(2)}, u32[]{:S(2)}) %collective-permute-start.2) | collective-permute-done | bytes 786464 | tf_op jit(solution)/shard_map/ppermute | solution.py:72
  168.6 2.0 collective-permute-done.3
  170.7 3.8 %convolution_bitcast_fusion = f32[768,192]{0,1:T(8,128)} fusion(bf16[192,4,512]{2,0,1:T(8,128)(2,1)S(1)} %bitcast.116, bf16[1,768,512]{2,1,0:T(8,128)(2,1)} %bitcast.12, bf16[1,768,512]{2,1,0:T(8,128)(2,1)} %bitcast.11, bf16[1,768,512]{2,1,0:T(8,128)(2,1)} %bitcast.10, bf16[1,768,512]{2,1,0:T(8,128)(2,1)} %bitcast.9), kind=kOutput, calls=%fused_computation.9 | convolution fusion | flops 608698368 | bytes 4521984 | tf_op jit(solution)/shard_map/dot_general | solution.py:139
  174.5 2.1 collective-permute-start.4
  176.7 51.6 %collective-permute-done.4 = f32[768,192]{0,1:T(8,128)} collective-permute-done((f32[768,192]{0,1:T(8,128)}, f32[768,192]{0,1:T(8,128)}, u32[]{:S(2)}, u32[]{:S(2)}) %collective-permute-start.4) | collective-permute-done | bytes 589856 | tf_op jit(solution)/shard_map/ppermute | solution.py:142
  228.3 3.4 %fusion = f32[768,192]{0,1:T(8,128)S(1)} fusion(f32[768,192]{0,1:T(8,128)} %collective-permute-done.4, bf16[192,4,512]{2,0,1:T(8,128)(2,1)} %bitcast.115, bf16[1,768,512]{2,1,0:T(8,128)(2,1)} %bitcast.12, bf16[1,768,512]{2,1,0:T(8,128)(2,1)} %bitcast.11, bf16[1,768,512]{2,1,0:T(8,128)(2,1)} %bitcast.10, bf16[1,768,512]{2,1,0:T(8,128)(2,1)} %bitcast.9), kind=kOutput, calls=%fused_computation.11 | convolution fusion | flops 608845824 | bytes 5111808 | tf_op jit(solution)/shard_map/dot_general | solution.py:136
  232.5 2.5 collective-permute-start.5
  236.5 2.8 collective-permute-start.6
  239.3 3.7 %collective-permute-start.7 = (bf16[768,96]{0,1:T(8,128)(2,1)S(1)}, bf16[768,96]{0,1:T(8,128)(2,1)S(1)}, u32[]{:S(2)}, u32[]{:S(2)}) collective-permute-start(bf16[768,96]{0,1:T(8,128)(2,1)S(1)} %get-tuple-element.15), channel_id=1, source_target_pairs={{0,3},{1,4},{2,5},{3,6},{4,7},{5,0},{6,1},{7,2},{8,11},{9,12},{10,... | collective-permute-start | bytes 442376 | tf_op jit(solution)/shard_map/ppermute | solution.py:72
  243.0 3.9 %collective-permute-start.8 = (bf16[768,96]{0,1:T(8,128)(2,1)S(1)}, bf16[768,96]{0,1:T(8,128)(2,1)S(1)}, u32[]{:S(2)}, u32[]{:S(2)}) collective-permute-start(bf16[768,96]{0,1:T(8,128)(2,1)S(1)} %get-tuple-element.15), channel_id=1, source_target_pairs={{0,4},{1,5},{2,6},{3,7},{4,0},{5,1},{6,2},{7,3},{8,12},{9,13},{10,... | collective-permute-start | bytes 442376 | tf_op jit(solution)/shard_map/ppermute | solution.py:72
  246.9 1.9 collective-permute-start.9
  248.8 5.1 %collective-permute-start.10 = (bf16[768,96]{0,1:T(8,128)(2,1)S(1)}, bf16[768,96]{0,1:T(8,128)(2,1)S(1)}, u32[]{:S(2)}, u32[]{:S(2)}) collective-permute-start(bf16[768,96]{0,1:T(8,128)(2,1)S(1)} %get-tuple-element.15), channel_id=1, source_target_pairs={{0,6},{1,7},{2,0},{3,1},{4,2},{5,3},{6,4},{7,5},{8,14},{9,15},{10,... | collective-permute-start | bytes 442376 | tf_op jit(solution)/shard_map/ppermute | solution.py:72
  255.6 4.0 %collective-permute-start.11 = (bf16[768,96]{0,1:T(8,128)(2,1)S(1)}, bf16[768,96]{0,1:T(8,128)(2,1)S(1)}, u32[]{:S(2)}, u32[]{:S(2)}) collective-permute-start(bf16[768,96]{0,1:T(8,128)(2,1)S(1)} %get-tuple-element.15), channel_id=1, source_target_pairs={{0,7},{1,0},{2,1},{3,2},{4,3},{5,4},{6,5},{7,6},{8,15},{9,8},{10,9... | collective-permute-start | bytes 442376 | tf_op jit(solution)/shard_map/ppermute | solution.py:72
  263.6 2.3 bitcast_convert_fusion
  267.0 13.0 %all-to-all-start.2 = ((bf16[64,12,512]{2,1,0:T(8,128)(2,1)}), bf16[64,12,512]{2,1,0:T(8,128)(2,1)S(1)}, u32[]{:S(2)}, u32[]{:S(2)}) async-start(bf16[64,12,512]{2,1,0:T(8,128)(2,1)} %reshape.170), calls=%async_computation.2 | async-start | bytes 2097152 | tf_op jit(solution)/shard_map/all_to_all | solution.py:154
  287.9 23.0 %all-to-all-done.2 = bf16[64,12,512]{2,1,0:T(8,128)(2,1)S(1)} async-done(((bf16[64,12,512]{2,1,0:T(8,128)(2,1)}), bf16[64,12,512]{2,1,0:T(8,128)(2,1)S(1)}, u32[]{:S(2)}, u32[]{:S(2)}) %all-to-all-start.2) | async-done | bytes 786464 | tf_op jit(solution)/shard_map/all_to_all | solution.py:154
  (85 shorter events, 34.1 us)
Async XLA Ops:
  0.6 5.9 %copy-start = (bf16[48,512]{1,0:T(8,128)(2,1)S(1)}, bf16[48,512]{1,0:T(8,128)(2,1)}, u32[]{:S(2)}) copy-start(bf16[48,512]{1,0:T(8,128)(2,1)} %param.8) | copy-start | bytes 147460
  0.6 6.8 %copy-start.5 = (bf16[1,768,512]{2,1,0:T(8,128)(2,1)S(1)}, bf16[1,768,512]{2,1,0:T(8,128)(2,1)}, u32[]{:S(2)}) copy-start(bf16[1,768,512]{2,1,0:T(8,128)(2,1)} %param.15) | copy-start | bytes 2359300
  7.4 1.1 copy-start.3
  7.6 1.2 copy-start.4
  12.1 111.6 %all-to-all-start = ((bf16[64,192,128]{2,1,0:T(8,128)(2,1)}), bf16[64,192,128]{2,1,0:T(8,128)(2,1)S(1)}, u32[]{:S(2)}, u32[]{:S(2)}) async-start(bf16[64,192,128]{2,1,0:T(8,128)(2,1)} %pad_maximum_fusion), calls=%async_computation | async-start | bytes 6291456 | tf_op jit(solution)/shard_map/all_to_all | solution.py:117
  45.5 73.5 %collective-permute-start = (bf16[192,2048]{1,0:T(8,128)(2,1)}, bf16[192,2048]{1,0:T(8,128)(2,1)}, u32[]{:S(2)}, u32[]{:S(2)}) collective-permute-start(bf16[192,2048]{1,0:T(8,128)(2,1)} %pad_maximum_fusion.4), channel_id=1, source_target_pairs={{0,4},{4,0},{1,5},{5,1},{2,6},{6,2},{3,7},{7,3},{8,12},{12,8},{9,1... | collective-permute-start | bytes 2359304 | tf_op jit(solution)/shard_map/ppermute | solution.py:107
  126.9 12.5 %copy-start.9 = (s32[64]{0:T(128)S(1)}, s32[64]{0:T(128)}, u32[]{:S(2)}) copy-start(s32[64]{0:T(128)} %param.11) | copy-start | bytes 772
  128.5 31.6 %collective-permute-start.1 = (bf16[768,512]{1,0:T(8,128)(2,1)}, bf16[768,512]{1,0:T(8,128)(2,1)}, u32[]{:S(2)}, u32[]{:S(2)}) collective-permute-start(bf16[768,512]{1,0:T(8,128)(2,1)} %reshape.169), channel_id=1, source_target_pairs={{0,1},{1,2},{2,3},{3,0},{4,5},{5,6},{6,7},{7,4},{8,9},{9,10},{10,1... | collective-permute-start | bytes 2359304 | tf_op jit(solution)/shard_map/ppermute | solution.py:72
  131.0 37.6 %collective-permute-start.2 = (bf16[768,512]{1,0:T(8,128)(2,1)}, bf16[768,512]{1,0:T(8,128)(2,1)}, u32[]{:S(2)}, u32[]{:S(2)}) collective-permute-start(bf16[768,512]{1,0:T(8,128)(2,1)} %reshape.169), channel_id=1, source_target_pairs={{0,2},{1,3},{2,0},{3,1},{4,6},{5,7},{6,4},{7,5},{8,10},{9,11},{10,... | collective-permute-start | bytes 2359304 | tf_op jit(solution)/shard_map/ppermute | solution.py:72
  136.1 34.6 %collective-permute-start.3 = (bf16[768,512]{1,0:T(8,128)(2,1)}, bf16[768,512]{1,0:T(8,128)(2,1)}, u32[]{:S(2)}, u32[]{:S(2)}) collective-permute-start(bf16[768,512]{1,0:T(8,128)(2,1)} %reshape.169), channel_id=1, source_target_pairs={{0,3},{1,0},{2,1},{3,2},{4,7},{5,4},{6,5},{7,6},{8,11},{9,8},{10,9... | collective-permute-start | bytes 2359304 | tf_op jit(solution)/shard_map/ppermute | solution.py:72
  143.4 27.3 %copy-start.7 = (bf16[4,192,512]{2,1,0:T(8,128)(2,1)S(1)}, bf16[4,192,512]{2,1,0:T(8,128)(2,1)}, u32[]{:S(2)}) copy-start(bf16[4,192,512]{2,1,0:T(8,128)(2,1)} %gather_fusion.1) | copy-start | bytes 2359300
  143.4 122.5 %all-to-all-start.1 = ((bf16[64,144,128]{2,1,0:T(8,128)(2,1)}), bf16[64,144,128]{2,1,0:T(8,128)(2,1)S(1)}, u32[]{:S(2)}, u32[]{:S(2)}) async-start(bf16[64,144,128]{2,1,0:T(8,128)(2,1)} %gather_fusion.3), calls=%async_computation.1 | async-start | bytes 4718592 | tf_op jit(solution)/shard_map/all_to_all | solution.py:127
  174.5 53.8 %collective-permute-start.4 = (f32[768,192]{0,1:T(8,128)}, f32[768,192]{0,1:T(8,128)}, u32[]{:S(2)}, u32[]{:S(2)}) collective-permute-start(f32[768,192]{0,1:T(8,128)} %convolution_bitcast_fusion), channel_id=1, source_target_pairs={{0,4},{4,0},{1,5},{5,1},{2,6},{6,2},{3,7},{7,3},{8,12},{12,8},{9,1... | collective-permute-start | bytes 1769480 | tf_op jit(solution)/shard_map/ppermute | solution.py:142
  176.6 58.3 %copy-start.6 = (bf16[1,768,512]{2,1,0:T(8,128)(2,1)S(1)}, bf16[1,768,512]{2,1,0:T(8,128)(2,1)}, u32[]{:S(2)}) copy-start(bf16[1,768,512]{2,1,0:T(8,128)(2,1)} %param.15) | copy-start | bytes 2359300
  232.5 16.4 %collective-permute-start.5 = (bf16[768,96]{0,1:T(8,128)(2,1)S(1)}, bf16[768,96]{0,1:T(8,128)(2,1)}, u32[]{:S(2)}, u32[]{:S(2)}) collective-permute-start(bf16[768,96]{0,1:T(8,128)(2,1)S(1)} %get-tuple-element.15), channel_id=1, source_target_pairs={{0,1},{1,2},{2,3},{3,4},{4,5},{5,6},{6,7},{7,0},{8,9},{9,10},{10,1... | collective-permute-start | bytes 442376 | tf_op jit(solution)/shard_map/ppermute | solution.py:72
  236.5 19.1 %collective-permute-start.6 = (bf16[768,96]{0,1:T(8,128)(2,1)S(1)}, bf16[768,96]{0,1:T(8,128)(2,1)S(1)}, u32[]{:S(2)}, u32[]{:S(2)}) collective-permute-start(bf16[768,96]{0,1:T(8,128)(2,1)S(1)} %get-tuple-element.15), channel_id=1, source_target_pairs={{0,2},{1,3},{2,4},{3,5},{4,6},{5,7},{6,0},{7,1},{8,10},{9,11},{10,... | collective-permute-start | bytes 442376 | tf_op jit(solution)/shard_map/ppermute | solution.py:72
  239.3 21.0 %collective-permute-start.7 = (bf16[768,96]{0,1:T(8,128)(2,1)S(1)}, bf16[768,96]{0,1:T(8,128)(2,1)S(1)}, u32[]{:S(2)}, u32[]{:S(2)}) collective-permute-start(bf16[768,96]{0,1:T(8,128)(2,1)S(1)} %get-tuple-element.15), channel_id=1, source_target_pairs={{0,3},{1,4},{2,5},{3,6},{4,7},{5,0},{6,1},{7,2},{8,11},{9,12},{10,... | collective-permute-start | bytes 442376 | tf_op jit(solution)/shard_map/ppermute | solution.py:72
  243.0 17.9 %collective-permute-start.8 = (bf16[768,96]{0,1:T(8,128)(2,1)S(1)}, bf16[768,96]{0,1:T(8,128)(2,1)S(1)}, u32[]{:S(2)}, u32[]{:S(2)}) collective-permute-start(bf16[768,96]{0,1:T(8,128)(2,1)S(1)} %get-tuple-element.15), channel_id=1, source_target_pairs={{0,4},{1,5},{2,6},{3,7},{4,0},{5,1},{6,2},{7,3},{8,12},{9,13},{10,... | collective-permute-start | bytes 442376 | tf_op jit(solution)/shard_map/ppermute | solution.py:72
  246.9 14.7 %collective-permute-start.9 = (bf16[768,96]{0,1:T(8,128)(2,1)S(1)}, bf16[768,96]{0,1:T(8,128)(2,1)S(1)}, u32[]{:S(2)}, u32[]{:S(2)}) collective-permute-start(bf16[768,96]{0,1:T(8,128)(2,1)S(1)} %get-tuple-element.15), channel_id=1, source_target_pairs={{0,5},{1,6},{2,7},{3,0},{4,1},{5,2},{6,3},{7,4},{8,13},{9,14},{10,... | collective-permute-start | bytes 442376 | tf_op jit(solution)/shard_map/ppermute | solution.py:72
  248.8 13.4 %collective-permute-start.10 = (bf16[768,96]{0,1:T(8,128)(2,1)S(1)}, bf16[768,96]{0,1:T(8,128)(2,1)S(1)}, u32[]{:S(2)}, u32[]{:S(2)}) collective-permute-start(bf16[768,96]{0,1:T(8,128)(2,1)S(1)} %get-tuple-element.15), channel_id=1, source_target_pairs={{0,6},{1,7},{2,0},{3,1},{4,2},{5,3},{6,4},{7,5},{8,14},{9,15},{10,... | collective-permute-start | bytes 442376 | tf_op jit(solution)/shard_map/ppermute | solution.py:72
  255.6 7.4 %collective-permute-start.11 = (bf16[768,96]{0,1:T(8,128)(2,1)S(1)}, bf16[768,96]{0,1:T(8,128)(2,1)S(1)}, u32[]{:S(2)}, u32[]{:S(2)}) collective-permute-start(bf16[768,96]{0,1:T(8,128)(2,1)S(1)} %get-tuple-element.15), channel_id=1, source_target_pairs={{0,7},{1,0},{2,1},{3,2},{4,3},{5,4},{6,5},{7,6},{8,15},{9,8},{10,9... | collective-permute-start | bytes 442376 | tf_op jit(solution)/shard_map/ppermute | solution.py:72
  265.9 14.2 %copy-start.8 = (bf16[48,8]{0,1:T(8,128)(2,1)S(1)}, bf16[48,8]{0,1:T(8,128)(2,1)}, u32[]{:S(2)}) copy-start(bf16[48,8]{0,1:T(8,128)(2,1)} %param.10) | copy-start | bytes 2308
  267.0 43.9 %all-to-all-start.2 = ((bf16[64,12,512]{2,1,0:T(8,128)(2,1)}), bf16[64,12,512]{2,1,0:T(8,128)(2,1)S(1)}, u32[]{:S(2)}, u32[]{:S(2)}) async-start(bf16[64,12,512]{2,1,0:T(8,128)(2,1)} %reshape.170), calls=%async_computation.2 | async-start | bytes 2097152 | tf_op jit(solution)/shard_map/all_to_all | solution.py:154
  283.2 1.5 copy-start.2
  283.5 2.8 copy-start.1

commit v12 on v7

--- a/solution.py
+++ b/solution.py
@@ -121,6 +121,7 @@
     slice_rows = first[:, :split_at].reshape(groups * capacity, narrow_width)
     spread = first[:, split_at:]
     ordered = jnp.take(spread, partner, axis=0, mode="clip")
+    ordered, slice_rows = lax.optimization_barrier((ordered, slice_rows))
     arrived = lax.all_to_all(ordered, "expert", split_axis=0, concat_axis=0, tiled=True)
 
     pieces, sources = ring_gather(slice_rows, "x", columns, column)

time: 299 us -> 300 us (level)
  the two profiles are of different devices: /device:TPU:16 before, /device:TPU:22 now
where the time goes in v12:
time: 300 us; the launch traced here: 299 us
  waiting for transfers between devices  141 us (47%)
  starting transfers between devices  87.4 us (29%)
  local copies, waits for them, and re-layouts  49.2 us (16%)
  matrix products  11.1 us (4%)
  other arithmetic  9.7 us (3%)
    all_to_all x1, waiting for transfers between devices, body(): lax.all_to_all(jnp.concatenate([token_lanes, packed], axis=1), 'expert',...  55.2 us
    ppermute x1, waiting for transfers between devices, body(): back = lax.ppermute(other_part, 'zlo', pair)  43.7 us
    ppermute x10, starting transfers between devices, ring_gather(): lax.ppermute(value, axis, [(i, (i + shift) % size) for i in range(size)])  33.8 us
    all_to_all x1, waiting for transfers between devices, body(): lax.all_to_all(produced.reshape(groups, capacity, -1), 'expert', split_ax...  23.1 us
    ppermute x10, waiting for transfers between devices, ring_gather(): lax.ppermute(value, axis, [(i, (i + shift) % size) for i in range(size)])  18.9 us
    all_to_all x1, starting transfers between devices, body(): lax.all_to_all(ordered, 'expert', split_axis=0, concat_axis=0, tiled=True)  17.8 us
    all_to_all x1, starting transfers between devices, body(): lax.all_to_all(jnp.concatenate([token_lanes, packed], axis=1), 'expert',...  16.5 us
    all_to_all x1, starting transfers between devices, body(): lax.all_to_all(produced.reshape(groups, capacity, -1), 'expert', split_ax...  13.8 us
  transfers between devices with their start and end apart: 15, of which 7 were waited for; matrix products, arithmetic and copies ran while one was open for 19% of the time, Pallas kernels for 0%

profile of v12, /device:TPU:22, one launch (start us, length us, event | category | flops | bytes accessed | tf_op | source)
XLA Modules:
  0.0 299.4 jit_solution(13987744122689083343)
XLA Ops:
  7.8 1.8 reshape_squeeze.20
  11.1 2.1 pad_maximum_fusion
  13.2 16.5 %all-to-all-start = ((bf16[64,192,128]{2,1,0:T(8,128)(2,1)}), bf16[64,192,128]{2,1,0:T(8,128)(2,1)S(1)}, u32[]{:S(2)}, u32[]{:S(2)}) async-start(bf16[64,192,128]{2,1,0:T(8,128)(2,1)} %pad_maximum_fusion), calls=%async_computation | async-start | bytes 6291456 | tf_op jit(solution)/shard_map/all_to_all | solution.py:114
  29.7 3.3 %reshape_squeeze.21 = bf16[96,2,2048]{2,1,0:T(2,128)(2,1)} reshape(bf16[1,96,4096]{2,1,0:T(8,128)(2,1)} %param.13) | data formatting | bytes 1572864 | tf_op jit(solution)/shard_map/reshape;squeeze | solution.py:91
  32.9 3.2 %reshape_squeeze.22 = bf16[96,2,2048]{2,1,0:T(2,128)(2,1)} reshape(bf16[1,96,4096]{2,1,0:T(8,128)(2,1)} %param.14) | data formatting | bytes 1572864 | tf_op jit(solution)/shard_map/reshape;squeeze | solution.py:92
  36.2 9.1 %dynamic-slice_reduce_fusion = (bf16[96,2048]{1,0:T(8,128)(2,1)}, bf16[96,1,2048]{2,1,0:T(2,128)(2,1)S(1)}, bf16[96,1,2048]{2,1,0:T(2,128)(2,1)S(1)}, bf16[96,2048]{1,0:T(8,128)(2,1)}) fusion(bf16[96,2,2048]{2,1,0:T(2,128)(2,1)} %reshape_squeeze.22, s32[]{:T(128)S(6)} %select_n.41, s32[]{:T(128)S(6)} %select_n.43, bf16[96,2,2048]{2,1,0:T(2,128)(2,1)} %reshape_squeeze.21), kind=kLoop, calls=%fused_computation.24 | loop fusion | bytes 3145736 | tf_op jit(solution)/shard_map/jit(dynamic_index_in_dim)/dynamic_slice | solution.py:96
  46.7 3.4 %collective-permute-start.3 = (bf16[192,2048]{1,0:T(8,128)(2,1)}, bf16[192,2048]{1,0:T(8,128)(2,1)}, u32[]{:S(2)}, u32[]{:S(2)}) collective-permute-start(bf16[192,2048]{1,0:T(8,128)(2,1)} %pad_maximum_fusion.4), channel_id=1, source_target_pairs={{0,4},{4,0},{1,5},{5,1},{2,6},{6,2},{3,7},{7,3},{8,12},{12,8},{9,1... | collective-permute-start | bytes 2359304 | tf_op jit(solution)/shard_map/ppermute | solution.py:107
  50.1 55.2 %all-to-all-done = bf16[64,192,128]{2,1,0:T(8,128)(2,1)S(1)} async-done(((bf16[64,192,128]{2,1,0:T(8,128)(2,1)}), bf16[64,192,128]{2,1,0:T(8,128)(2,1)S(1)}, u32[]{:S(2)}, u32[]{:S(2)}) %all-to-all-start) | async-done | bytes 3145760 | tf_op jit(solution)/shard_map/all_to_all | solution.py:114
  106.2 2.3 reshape.168
  110.0 3.9 %gather_fusion = bf16[64,144,128]{2,1,0:T(8,128)(2,1)} fusion(bf16[64,144,128]{2,1,0:T(8,128)(2,1)} %slice.45, s32[1024]{0:T(1024)S(1)} %pad_clamp_fusion.2), kind=kCustom, calls=%fused_computation | custom fusion | bytes 4718848 | tf_op jit(solution)/shard_map/jit(_take)/gather | solution.py:123
  114.0 2.2 collective-permute-start.2
  116.1 3.8 %collective-permute-start.1 = (bf16[768,512]{1,0:T(8,128)(2,1)}, bf16[768,512]{1,0:T(8,128)(2,1)}, u32[]{:S(2)}, u32[]{:S(2)}) collective-permute-start(bf16[768,512]{1,0:T(8,128)(2,1)} %reshape.168), channel_id=1, source_target_pairs={{0,2},{1,3},{2,0},{3,1},{4,6},{5,7},{6,4},{7,5},{8,10},{9,11},{10,... | collective-permute-start | bytes 2359304 | tf_op jit(solution)/shard_map/ppermute | solution.py:72
  120.0 3.9 %collective-permute-start = (bf16[768,512]{1,0:T(8,128)(2,1)}, bf16[768,512]{1,0:T(8,128)(2,1)}, u32[]{:S(2)}, u32[]{:S(2)}) collective-permute-start(bf16[768,512]{1,0:T(8,128)(2,1)} %reshape.168), channel_id=1, source_target_pairs={{0,1},{1,2},{2,3},{3,0},{4,5},{5,6},{6,7},{7,4},{8,9},{9,10},{10,1... | collective-permute-start | bytes 2359304 | tf_op jit(solution)/shard_map/ppermute | solution.py:72
  123.8 17.8 %all-to-all-start.1 = ((bf16[64,144,128]{2,1,0:T(8,128)(2,1)}), bf16[64,144,128]{2,1,0:T(8,128)(2,1)S(1)}, u32[]{:S(2)}, u32[]{:S(2)}) async-start(bf16[64,144,128]{2,1,0:T(8,128)(2,1)} %gather_fusion), calls=%async_computation.1 | async-start | bytes 4718592 | tf_op jit(solution)/shard_map/all_to_all | solution.py:125
  144.4 8.5 %collective-permute-done.2 = bf16[768,512]{1,0:T(8,128)(2,1)} collective-permute-done((bf16[768,512]{1,0:T(8,128)(2,1)}, bf16[768,512]{1,0:T(8,128)(2,1)}, u32[]{:S(2)}, u32[]{:S(2)}) %collective-permute-start.2) | collective-permute-done | bytes 786464 | tf_op jit(solution)/shard_map/ppermute | solution.py:72
  152.9 2.5 collective-permute-done
  155.4 4.1 %convolution_bitcast_fusion = f32[768,192]{0,1:T(8,128)} fusion(bf16[4,192,512]{2,1,0:T(8,128)(2,1)} %gather_fusion.2, bf16[1,768,512]{2,1,0:T(8,128)(2,1)} %bitcast.9, bf16[1,768,512]{2,1,0:T(8,128)(2,1)} %bitcast.8, bf16[1,768,512]{2,1,0:T(8,128)(2,1)} %bitcast.7, bf16[1,768,512]{2,1,0:T(8,128)(2,1)} %bitcast.6), kind=kOutput, calls=%fused_computation.9 | convolution fusion | flops 608698368 | bytes 4521984 | tf_op jit(solution)/shard_map/dot_general | solution.py:135
  159.5 2.1 collective-permute-start.4
  163.3 43.7 %collective-permute-done.4 = f32[768,192]{0,1:T(8,128)} collective-permute-done((f32[768,192]{0,1:T(8,128)}, f32[768,192]{0,1:T(8,128)}, u32[]{:S(2)}, u32[]{:S(2)}) %collective-permute-start.4) | collective-permute-done | bytes 589856 | tf_op jit(solution)/shard_map/ppermute | solution.py:138
  207.0 3.4 %fusion = f32[768,192]{0,1:T(8,128)S(1)} fusion(f32[768,192]{0,1:T(8,128)} %collective-permute-done.4, bf16[4,192,512]{2,1,0:T(8,128)(2,1)} %gather_fusion.1, bf16[1,768,512]{2,1,0:T(8,128)(2,1)} %bitcast.9, bf16[1,768,512]{2,1,0:T(8,128)(2,1)} %bitcast.8, bf16[1,768,512]{2,1,0:T(8,128)(2,1)} %bitcast.7, bf16[1,768,512]{2,1,0:T(8,128)(2,1)} %bitcast.6), kind=kOutput, calls=%fused_computation.11 | convolution fusion | flops 608845824 | bytes 5111808 | tf_op jit(solution)/shard_map/dot_general | solution.py:132
  211.2 5.1 %collective-permute-start.5 = (bf16[768,96]{0,1:T(8,128)(2,1)S(1)}, bf16[768,96]{0,1:T(8,128)(2,1)}, u32[]{:S(2)}, u32[]{:S(2)}) collective-permute-start(bf16[768,96]{0,1:T(8,128)(2,1)S(1)} %get-tuple-element.13), channel_id=1, source_target_pairs={{0,1},{1,2},{2,3},{3,4},{4,5},{5,6},{6,7},{7,0},{8,9},{9,10},{10,1... | collective-permute-start | bytes 442376 | tf_op jit(solution)/shard_map/ppermute | solution.py:72
  217.8 1.9 collective-permute-start.10
  219.7 5.3 %collective-permute-start.9 = (bf16[768,96]{0,1:T(8,128)(2,1)S(1)}, bf16[768,96]{0,1:T(8,128)(2,1)S(1)}, u32[]{:S(2)}, u32[]{:S(2)}) collective-permute-start(bf16[768,96]{0,1:T(8,128)(2,1)S(1)} %get-tuple-element.13), channel_id=1, source_target_pairs={{0,5},{1,6},{2,7},{3,0},{4,1},{5,2},{6,3},{7,4},{8,13},{9,14},{10,... | collective-permute-start | bytes 442376 | tf_op jit(solution)/shard_map/ppermute | solution.py:72
  225.0 1.9 collective-permute-start.8
  226.9 3.1 %collective-permute-start.7 = (bf16[768,96]{0,1:T(8,128)(2,1)S(1)}, bf16[768,96]{0,1:T(8,128)(2,1)S(1)}, u32[]{:S(2)}, u32[]{:S(2)}) collective-permute-start(bf16[768,96]{0,1:T(8,128)(2,1)S(1)} %get-tuple-element.13), channel_id=1, source_target_pairs={{0,3},{1,4},{2,5},{3,6},{4,7},{5,0},{6,1},{7,2},{8,11},{9,12},{10,... | collective-permute-start | bytes 442376 | tf_op jit(solution)/shard_map/ppermute | solution.py:72
  230.1 4.7 %collective-permute-start.6 = (bf16[768,96]{0,1:T(8,128)(2,1)S(1)}, bf16[768,96]{0,1:T(8,128)(2,1)S(1)}, u32[]{:S(2)}, u32[]{:S(2)}) collective-permute-start(bf16[768,96]{0,1:T(8,128)(2,1)S(1)} %get-tuple-element.13), channel_id=1, source_target_pairs={{0,2},{1,3},{2,4},{3,5},{4,6},{5,7},{6,0},{7,1},{8,10},{9,11},{10,... | collective-permute-start | bytes 442376 | tf_op jit(solution)/shard_map/ppermute | solution.py:72
  236.3 3.6 %collective-permute-done.6 = bf16[768,96]{0,1:T(8,128)(2,1)S(1)} collective-permute-done((bf16[768,96]{0,1:T(8,128)(2,1)S(1)}, bf16[768,96]{0,1:T(8,128)(2,1)S(1)}, u32[]{:S(2)}, u32[]{:S(2)}) %collective-permute-start.6) | collective-permute-done | bytes 147488 | tf_op jit(solution)/shard_map/ppermute | solution.py:72
  240.0 1.9 collective-permute-start.11
  245.2 4.3 %collective-permute-done.11 = bf16[768,96]{0,1:T(8,128)(2,1)S(1)} collective-permute-done((bf16[768,96]{0,1:T(8,128)(2,1)S(1)}, bf16[768,96]{0,1:T(8,128)(2,1)S(1)}, u32[]{:S(2)}, u32[]{:S(2)}) %collective-permute-start.11) | collective-permute-done | bytes 147488 | tf_op jit(solution)/shard_map/ppermute | solution.py:72
  250.2 2.3 bitcast_convert_fusion
  253.6 13.8 %all-to-all-start.2 = ((bf16[64,12,512]{2,1,0:T(8,128)(2,1)}), bf16[64,12,512]{2,1,0:T(8,128)(2,1)S(1)}, u32[]{:S(2)}, u32[]{:S(2)}) async-start(bf16[64,12,512]{2,1,0:T(8,128)(2,1)} %reshape.170), calls=%async_computation.2 | async-start | bytes 2097152 | tf_op jit(solution)/shard_map/all_to_all | solution.py:150
  275.3 23.1 %all-to-all-done.2 = bf16[64,12,512]{2,1,0:T(8,128)(2,1)S(1)} async-done(((bf16[64,12,512]{2,1,0:T(8,128)(2,1)}), bf16[64,12,512]{2,1,0:T(8,128)(2,1)S(1)}, u32[]{:S(2)}, u32[]{:S(2)}) %all-to-all-start.2) | async-done | bytes 786464 | tf_op jit(solution)/shard_map/all_to_all | solution.py:150
  (85 shorter events, 34.6 us)
Async XLA Ops:
  0.6 6.0 %copy-start = (bf16[48,512]{1,0:T(8,128)(2,1)S(1)}, bf16[48,512]{1,0:T(8,128)(2,1)}, u32[]{:S(2)}) copy-start(bf16[48,512]{1,0:T(8,128)(2,1)} %param.8) | copy-start | bytes 147460
  0.6 6.8 %copy-start.4 = (bf16[1,96,4096]{2,1,0:T(8,128)(2,1)S(1)}, bf16[1,96,4096]{2,1,0:T(8,128)(2,1)}, u32[]{:S(2)}) copy-start(bf16[1,96,4096]{2,1,0:T(8,128)(2,1)} %param.14) | copy-start | bytes 2359300
  3.3 4.4 %copy-start.3 = (bf16[1,96,4096]{2,1,0:T(8,128)(2,1)S(1)}, bf16[1,96,4096]{2,1,0:T(8,128)(2,1)}, u32[]{:S(2)}) copy-start(bf16[1,96,4096]{2,1,0:T(8,128)(2,1)} %param.13) | copy-start | bytes 2359300
  13.2 92.1 %all-to-all-start = ((bf16[64,192,128]{2,1,0:T(8,128)(2,1)}), bf16[64,192,128]{2,1,0:T(8,128)(2,1)S(1)}, u32[]{:S(2)}, u32[]{:S(2)}) async-start(bf16[64,192,128]{2,1,0:T(8,128)(2,1)} %pad_maximum_fusion), calls=%async_computation | async-start | bytes 6291456 | tf_op jit(solution)/shard_map/all_to_all | solution.py:114
  45.3 4.8 %copy-start.9 = (s32[64]{0:T(128)S(1)}, s32[64]{0:T(128)}, u32[]{:S(2)}) copy-start(s32[64]{0:T(128)} %param.11) | copy-start | bytes 772
  46.7 95.0 %collective-permute-start.3 = (bf16[192,2048]{1,0:T(8,128)(2,1)}, bf16[192,2048]{1,0:T(8,128)(2,1)}, u32[]{:S(2)}, u32[]{:S(2)}) collective-permute-start(bf16[192,2048]{1,0:T(8,128)(2,1)} %pad_maximum_fusion.4), channel_id=1, source_target_pairs={{0,4},{4,0},{1,5},{5,1},{2,6},{6,2},{3,7},{7,3},{8,12},{12,8},{9,1... | collective-permute-start | bytes 2359304 | tf_op jit(solution)/shard_map/ppermute | solution.py:107
  114.0 38.9 %collective-permute-start.2 = (bf16[768,512]{1,0:T(8,128)(2,1)}, bf16[768,512]{1,0:T(8,128)(2,1)}, u32[]{:S(2)}, u32[]{:S(2)}) collective-permute-start(bf16[768,512]{1,0:T(8,128)(2,1)} %reshape.168), channel_id=1, source_target_pairs={{0,3},{1,0},{2,1},{3,2},{4,7},{5,4},{6,5},{7,6},{8,11},{9,8},{10,9... | collective-permute-start | bytes 2359304 | tf_op jit(solution)/shard_map/ppermute | solution.py:72
  116.1 36.7 %collective-permute-start.1 = (bf16[768,512]{1,0:T(8,128)(2,1)}, bf16[768,512]{1,0:T(8,128)(2,1)}, u32[]{:S(2)}, u32[]{:S(2)}) collective-permute-start(bf16[768,512]{1,0:T(8,128)(2,1)} %reshape.168), channel_id=1, source_target_pairs={{0,2},{1,3},{2,0},{3,1},{4,6},{5,7},{6,4},{7,5},{8,10},{9,11},{10,... | collective-permute-start | bytes 2359304 | tf_op jit(solution)/shard_map/ppermute | solution.py:72
  120.0 35.4 %collective-permute-start = (bf16[768,512]{1,0:T(8,128)(2,1)}, bf16[768,512]{1,0:T(8,128)(2,1)}, u32[]{:S(2)}, u32[]{:S(2)}) collective-permute-start(bf16[768,512]{1,0:T(8,128)(2,1)} %reshape.168), channel_id=1, source_target_pairs={{0,1},{1,2},{2,3},{3,0},{4,5},{5,6},{6,7},{7,4},{8,9},{9,10},{10,1... | collective-permute-start | bytes 2359304 | tf_op jit(solution)/shard_map/ppermute | solution.py:72
  123.8 128.7 %all-to-all-start.1 = ((bf16[64,144,128]{2,1,0:T(8,128)(2,1)}), bf16[64,144,128]{2,1,0:T(8,128)(2,1)S(1)}, u32[]{:S(2)}, u32[]{:S(2)}) async-start(bf16[64,144,128]{2,1,0:T(8,128)(2,1)} %gather_fusion), calls=%async_computation.1 | async-start | bytes 4718592 | tf_op jit(solution)/shard_map/all_to_all | solution.py:125
  155.4 6.3 %copy-start.7 = (bf16[96,2048]{1,0:T(8,128)(2,1)S(1)}, bf16[96,2048]{1,0:T(8,128)(2,1)}, u32[]{:S(2)}) copy-start(bf16[96,2048]{1,0:T(8,128)(2,1)} %get-tuple-element.19) | copy-start | bytes 1179652
  155.4 6.3 %copy-start.6 = (bf16[96,2048]{1,0:T(8,128)(2,1)S(1)}, bf16[96,2048]{1,0:T(8,128)(2,1)}, u32[]{:S(2)}) copy-start(bf16[96,2048]{1,0:T(8,128)(2,1)} %get-tuple-element.22) | copy-start | bytes 1179652
  159.5 47.4 %collective-permute-start.4 = (f32[768,192]{0,1:T(8,128)}, f32[768,192]{0,1:T(8,128)}, u32[]{:S(2)}, u32[]{:S(2)}) collective-permute-start(f32[768,192]{0,1:T(8,128)} %convolution_bitcast_fusion), channel_id=1, source_target_pairs={{0,4},{4,0},{1,5},{5,1},{2,6},{6,2},{3,7},{7,3},{8,12},{12,8},{9,1... | collective-permute-start | bytes 1769480 | tf_op jit(solution)/shard_map/ppermute | solution.py:138
  163.3 53.0 %copy-start.5 = (bf16[1,768,512]{2,1,0:T(8,128)(2,1)S(1)}, bf16[1,768,512]{2,1,0:T(8,128)(2,1)}, u32[]{:S(2)}) copy-start(bf16[1,768,512]{2,1,0:T(8,128)(2,1)} %param.15) | copy-start | bytes 2359300
  211.2 18.9 %collective-permute-start.5 = (bf16[768,96]{0,1:T(8,128)(2,1)S(1)}, bf16[768,96]{0,1:T(8,128)(2,1)}, u32[]{:S(2)}, u32[]{:S(2)}) collective-permute-start(bf16[768,96]{0,1:T(8,128)(2,1)S(1)} %get-tuple-element.13), channel_id=1, source_target_pairs={{0,1},{1,2},{2,3},{3,4},{4,5},{5,6},{6,7},{7,0},{8,9},{9,10},{10,1... | collective-permute-start | bytes 442376 | tf_op jit(solution)/shard_map/ppermute | solution.py:72
  217.8 26.8 %collective-permute-start.10 = (bf16[768,96]{0,1:T(8,128)(2,1)S(1)}, bf16[768,96]{0,1:T(8,128)(2,1)S(1)}, u32[]{:S(2)}, u32[]{:S(2)}) collective-permute-start(bf16[768,96]{0,1:T(8,128)(2,1)S(1)} %get-tuple-element.13), channel_id=1, source_target_pairs={{0,6},{1,7},{2,0},{3,1},{4,2},{5,3},{6,4},{7,5},{8,14},{9,15},{10,... | collective-permute-start | bytes 442376 | tf_op jit(solution)/shard_map/ppermute | solution.py:72
  219.7 24.2 %collective-permute-start.9 = (bf16[768,96]{0,1:T(8,128)(2,1)S(1)}, bf16[768,96]{0,1:T(8,128)(2,1)S(1)}, u32[]{:S(2)}, u32[]{:S(2)}) collective-permute-start(bf16[768,96]{0,1:T(8,128)(2,1)S(1)} %get-tuple-element.13), channel_id=1, source_target_pairs={{0,5},{1,6},{2,7},{3,0},{4,1},{5,2},{6,3},{7,4},{8,13},{9,14},{10,... | collective-permute-start | bytes 442376 | tf_op jit(solution)/shard_map/ppermute | solution.py:72
  225.0 18.2 %collective-permute-start.8 = (bf16[768,96]{0,1:T(8,128)(2,1)S(1)}, bf16[768,96]{0,1:T(8,128)(2,1)S(1)}, u32[]{:S(2)}, u32[]{:S(2)}) collective-permute-start(bf16[768,96]{0,1:T(8,128)(2,1)S(1)} %get-tuple-element.13), channel_id=1, source_target_pairs={{0,4},{1,5},{2,6},{3,7},{4,0},{5,1},{6,2},{7,3},{8,12},{9,13},{10,... | collective-permute-start | bytes 442376 | tf_op jit(solution)/shard_map/ppermute | solution.py:72
  226.9 15.6 %collective-permute-start.7 = (bf16[768,96]{0,1:T(8,128)(2,1)S(1)}, bf16[768,96]{0,1:T(8,128)(2,1)S(1)}, u32[]{:S(2)}, u32[]{:S(2)}) collective-permute-start(bf16[768,96]{0,1:T(8,128)(2,1)S(1)} %get-tuple-element.13), channel_id=1, source_target_pairs={{0,3},{1,4},{2,5},{3,6},{4,7},{5,0},{6,1},{7,2},{8,11},{9,12},{10,... | collective-permute-start | bytes 442376 | tf_op jit(solution)/shard_map/ppermute | solution.py:72
  230.1 9.9 %collective-permute-start.6 = (bf16[768,96]{0,1:T(8,128)(2,1)S(1)}, bf16[768,96]{0,1:T(8,128)(2,1)S(1)}, u32[]{:S(2)}, u32[]{:S(2)}) collective-permute-start(bf16[768,96]{0,1:T(8,128)(2,1)S(1)} %get-tuple-element.13), channel_id=1, source_target_pairs={{0,2},{1,3},{2,4},{3,5},{4,6},{5,7},{6,0},{7,1},{8,10},{9,11},{10,... | collective-permute-start | bytes 442376 | tf_op jit(solution)/shard_map/ppermute | solution.py:72
  240.0 9.5 %collective-permute-start.11 = (bf16[768,96]{0,1:T(8,128)(2,1)S(1)}, bf16[768,96]{0,1:T(8,128)(2,1)S(1)}, u32[]{:S(2)}, u32[]{:S(2)}) collective-permute-start(bf16[768,96]{0,1:T(8,128)(2,1)S(1)} %get-tuple-element.13), channel_id=1, source_target_pairs={{0,7},{1,0},{2,1},{3,2},{4,3},{5,4},{6,5},{7,6},{8,15},{9,8},{10,9... | collective-permute-start | bytes 442376 | tf_op jit(solution)/shard_map/ppermute | solution.py:72
  252.5 15.0 %copy-start.8 = (bf16[48,8]{0,1:T(8,128)(2,1)S(1)}, bf16[48,8]{0,1:T(8,128)(2,1)}, u32[]{:S(2)}) copy-start(bf16[48,8]{0,1:T(8,128)(2,1)} %param.10) | copy-start | bytes 2308
  253.6 44.7 %all-to-all-start.2 = ((bf16[64,12,512]{2,1,0:T(8,128)(2,1)}), bf16[64,12,512]{2,1,0:T(8,128)(2,1)S(1)}, u32[]{:S(2)}, u32[]{:S(2)}) async-start(bf16[64,12,512]{2,1,0:T(8,128)(2,1)} %reshape.170), calls=%async_computation.2 | async-start | bytes 2097152 | tf_op jit(solution)/shard_map/all_to_all | solution.py:150
  270.6 1.6 copy-start.2
  271.0 2.7 copy-start.1

commit v13 on v6

--- a/solution.py
+++ b/solution.py
@@ -42,20 +42,19 @@
         .transpose(0, 2, 1, 3)
         .reshape(-1, rows, LANES)
     )
-    stacked = jnp.concatenate([gate_c, up_c, down_c], axis=0)
-    return stacked.reshape(groups, -1, LANES)
+    pair_c = jnp.concatenate([gate_c, up_c], axis=0)
+    return pair_c.reshape(groups, -1, LANES), down_c.reshape(groups, -1, LANES)
 
 
-def unpack_weights(packed, gate_shape, down_shape):
+def unpack_weights(pair_packed, down_packed, gate_shape, down_shape):
     rows, width = gate_shape
     depth, narrow_width = down_shape
-    chunks = packed.reshape(-1, rows, LANES)
+    chunks = pair_packed.reshape(-1, rows, LANES)
     n_gate = width // LANES
     gate = chunks[:n_gate].transpose(1, 0, 2).reshape(rows, width)
-    up = chunks[n_gate : 2 * n_gate].transpose(1, 0, 2).reshape(rows, width)
+    up = chunks[n_gate:].transpose(1, 0, 2).reshape(rows, width)
     down = (
-        chunks[2 * n_gate :]
-        .reshape(depth // rows, narrow_width // LANES, rows, LANES)
+        down_packed.reshape(depth // rows, narrow_width // LANES, rows, LANES)
         .transpose(0, 2, 1, 3)
         .reshape(depth, narrow_width)
     )
@@ -104,23 +103,26 @@
         ],
         axis=0,
     )
-    both = lax.all_gather(give, "zlo", axis=0, tiled=False)
-    taken = lax.dynamic_index_in_dim(both, 1 - half, axis=0, keepdims=False)
+    taken = lax.ppermute(give, "zlo", pair)
 
     dispatch, combine, capacity = slot_layout(route_ids, route_weight, old_place, groups)
     outgoing = jnp.dot(dispatch, tokens, preferred_element_type=jnp.float32).astype(jnp.bfloat16)
-    packed = pack_weights(gate_block, up_block, down_block, groups)
+    pair_packed, down_packed = pack_weights(gate_block, up_block, down_block, groups)
     token_lanes = to_lanes(outgoing, groups)
     split_at = token_lanes.shape[1]
+    pair_at = split_at + pair_packed.shape[1]
     first = lax.all_to_all(
-        jnp.concatenate([token_lanes, packed], axis=1),
+        jnp.concatenate([token_lanes, pair_packed, down_packed], axis=1),
         "expert",
         split_axis=0,
         concat_axis=0,
         tiled=True,
     )
     slice_rows = first[:, :split_at].reshape(groups * capacity, narrow_width)
-    spread = first[:, split_at:]
+    pair_spread = first[:, split_at:pair_at]
+    down_spread = first[:, pair_at:]
+    pair_ordered = jnp.take(pair_spread, partner, axis=0, mode="clip")
+    arrived = lax.all_to_all(pair_ordered, "expert", split_axis=0, concat_axis=0, tiled=True)
 
     pieces, sources = ring_gather(slice_rows, "x", columns, column)
     keep3 = jnp.take(keep.reshape(keep.shape[0], columns, narrow_width), sources, axis=1, mode="clip")
@@ -144,16 +146,19 @@
         hidden_all, down3, (((0, 2), (0, 1)), ((), ())), preferred_element_type=jnp.float32
     ).astype(jnp.bfloat16)
 
-    ordered = jnp.take(spread, partner, axis=0, mode="clip")
+    produced, arrived = lax.optimization_barrier((produced, arrived))
+    down_ordered = jnp.take(down_spread, partner, axis=0, mode="clip")
     second = lax.all_to_all(
-        jnp.concatenate([to_lanes(produced, groups), ordered], axis=1),
+        jnp.concatenate([to_lanes(produced, groups), down_ordered], axis=1),
         "expert",
         split_axis=0,
         concat_axis=0,
         tiled=True,
     )
     returned = second[:, :split_at].reshape(groups * capacity, narrow_width)
-    new_gate, new_up, new_down = unpack_weights(second[:, split_at:], gate_block.shape, down_block.shape)
+    new_gate, new_up, new_down = unpack_weights(
+        arrived, second[:, split_at:], gate_block.shape, down_block.shape
+    )
     layer_out = jnp.dot(combine, returned, preferred_element_type=jnp.float32).astype(jnp.bfloat16)
     return (
         layer_out,

time: 362 us -> 315 us (0.87)
  the two profiles are of different devices: /device:TPU:40 before, /device:TPU:16 now
where the time goes in v13:
time: 315 us; the launch traced here: 314 us
  waiting for transfers between devices  141 us (45%)
  starting transfers between devices  91.2 us (29%)
  local copies, waits for them, and re-layouts  54.2 us (17%)
  other arithmetic  15.6 us (5%)
  matrix products  11.6 us (4%)
    all_to_all x1, waiting for transfers between devices, body(): lax.all_to_all(jnp.concatenate([token_lanes, pair_packed, down_packed], a...  55.2 us
    ppermute x10, waiting for transfers between devices, ring_gather(): lax.ppermute(value, axis, [(i, (i + shift) % size) for i in range(size)])  46.9 us
    all_to_all x1, waiting for transfers between devices, body(): lax.all_to_all(jnp.concatenate([to_lanes(produced, groups), down_ordered]...  37.3 us
    ppermute x10, starting transfers between devices, ring_gather(): lax.ppermute(value, axis, [(i, (i + shift) % size) for i in range(size)])  30.3 us
    all_to_all x1, starting transfers between devices, body(): lax.all_to_all(pair_ordered, 'expert', split_axis=0, concat_axis=0, tiled...  25.7 us
    all_to_all x1, starting transfers between devices, body(): lax.all_to_all(jnp.concatenate([token_lanes, pair_packed, down_packed], a...  16.5 us
    all_to_all x1, starting transfers between devices, body(): lax.all_to_all(jnp.concatenate([to_lanes(produced, groups), down_ordered]...  11.1 us
    unnamed x42, local copies, waits for them, and re-layouts  9.51 us
  transfers between devices with their start and end apart: 15, of which 8 were waited for; matrix products, arithmetic and copies ran while one was open for 17% of the time, Pallas kernels for 0%

profile of v13, /device:TPU:16, one launch (start us, length us, event | category | flops | bytes accessed | tf_op | source)
XLA Modules:
  0.0 314.3 jit_solution(12332627086932055873)
XLA Ops:
  11.5 7.5 %pad_maximum_fusion = bf16[64,192,128]{2,1,0:T(8,128)(2,1)} fusion(bf16[64,48,128]{2,1,0:T(8,128)(2,1)S(1)} %bitcast.98, bf16[32,96,128]{2,1,0:T(8,128)(2,1)S(1)} %get-tuple-element.20, bf16[32,96,128]{2,1,0:T(8,128)(2,1)S(1)} %get-tuple-element.21, bf16[64,48,128]{2,1,0:T(8,128)(2,1)S(1)} %reshape.156), kind=kLoop, calls=%fused_computation.5 | loop fusion | flops 12582912 | bytes 6291456 | tf_op jit(solution)/shard_map/concatenate | solution.py:115
  19.1 16.5 %all-to-all-start = ((bf16[64,192,128]{2,1,0:T(8,128)(2,1)}), bf16[64,192,128]{2,1,0:T(8,128)(2,1)S(1)}, u32[]{:S(2)}, u32[]{:S(2)}) async-start(bf16[64,192,128]{2,1,0:T(8,128)(2,1)} %pad_maximum_fusion), calls=%async_computation | async-start | bytes 6291456 | tf_op jit(solution)/shard_map/all_to_all | solution.py:114
  35.6 3.3 %reshape_squeeze.21 = bf16[96,2,2048]{2,1,0:T(2,128)(2,1)} reshape(bf16[1,96,4096]{2,1,0:T(8,128)(2,1)} %param.13) | data formatting | bytes 1572864 | tf_op jit(solution)/shard_map/reshape;squeeze | solution.py:90
  38.8 3.2 %reshape_squeeze.22 = bf16[96,2,2048]{2,1,0:T(2,128)(2,1)} reshape(bf16[1,96,4096]{2,1,0:T(8,128)(2,1)} %param.14) | data formatting | bytes 1572864 | tf_op jit(solution)/shard_map/reshape;squeeze | solution.py:91
  42.1 9.2 %dynamic-slice_reduce_fusion = (bf16[96,2048]{1,0:T(8,128)(2,1)}, bf16[96,1,2048]{2,1,0:T(2,128)(2,1)S(1)}, bf16[96,1,2048]{2,1,0:T(2,128)(2,1)S(1)}, bf16[96,2048]{1,0:T(8,128)(2,1)}) fusion(bf16[96,2,2048]{2,1,0:T(2,128)(2,1)} %reshape_squeeze.22, s32[]{:T(128)S(6)} %select_n.41, s32[]{:T(128)S(6)} %select_n.43, bf16[96,2,2048]{2,1,0:T(2,128)(2,1)} %reshape_squeeze.21), kind=kLoop, calls=%fused_computation.28 | loop fusion | bytes 3145736 | tf_op jit(solution)/shard_map/jit(dynamic_index_in_dim)/dynamic_slice | solution.py:95
  52.7 3.4 %collective-permute-start.3 = (bf16[192,2048]{1,0:T(8,128)(2,1)}, bf16[192,2048]{1,0:T(8,128)(2,1)}, u32[]{:S(2)}, u32[]{:S(2)}) collective-permute-start(bf16[192,2048]{1,0:T(8,128)(2,1)} %pad_maximum_fusion.4), channel_id=1, source_target_pairs={{0,4},{4,0},{1,5},{5,1},{2,6},{6,2},{3,7},{7,3},{8,12},{12,8},{9,1... | collective-permute-start | bytes 2359304 | tf_op jit(solution)/shard_map/ppermute | solution.py:106
  56.1 55.2 %all-to-all-done = bf16[64,192,128]{2,1,0:T(8,128)(2,1)S(1)} async-done(((bf16[64,192,128]{2,1,0:T(8,128)(2,1)}), bf16[64,192,128]{2,1,0:T(8,128)(2,1)S(1)}, u32[]{:S(2)}, u32[]{:S(2)}) %all-to-all-start) | async-done | bytes 3145760 | tf_op jit(solution)/shard_map/all_to_all | solution.py:114
  112.5 2.2 reshape.157
  114.7 3.8 %collective-permute-start.2 = (bf16[768,512]{1,0:T(8,128)(2,1)}, bf16[768,512]{1,0:T(8,128)(2,1)}, u32[]{:S(2)}, u32[]{:S(2)}) collective-permute-start(bf16[768,512]{1,0:T(8,128)(2,1)} %reshape.157), channel_id=1, source_target_pairs={{0,3},{1,0},{2,1},{3,2},{4,7},{5,4},{6,5},{7,6},{8,11},{9,8},{10,9... | collective-permute-start | bytes 2359304 | tf_op jit(solution)/shard_map/ppermute | solution.py:71
  118.5 3.0 collective-permute-start.1
  121.5 3.3 %collective-permute-start = (bf16[768,512]{1,0:T(8,128)(2,1)}, bf16[768,512]{1,0:T(8,128)(2,1)}, u32[]{:S(2)}, u32[]{:S(2)}) collective-permute-start(bf16[768,512]{1,0:T(8,128)(2,1)} %reshape.157), channel_id=1, source_target_pairs={{0,1},{1,2},{2,3},{3,0},{4,5},{5,6},{6,7},{7,4},{8,9},{9,10},{10,1... | collective-permute-start | bytes 2359304 | tf_op jit(solution)/shard_map/ppermute | solution.py:71
  126.1 2.1 copy.78
  128.2 2.6 gather_fusion.1
  130.8 2.3 stack_reshape.3
  133.1 17.2 %collective-permute-done.2 = bf16[768,512]{1,0:T(8,128)(2,1)} collective-permute-done((bf16[768,512]{1,0:T(8,128)(2,1)}, bf16[768,512]{1,0:T(8,128)(2,1)}, u32[]{:S(2)}, u32[]{:S(2)}) %collective-permute-start.2) | collective-permute-done | bytes 786464 | tf_op jit(solution)/shard_map/ppermute | solution.py:71
  150.3 5.6 %collective-permute-done = bf16[768,512]{1,0:T(8,128)(2,1)} collective-permute-done((bf16[768,512]{1,0:T(8,128)(2,1)}, bf16[768,512]{1,0:T(8,128)(2,1)}, u32[]{:S(2)}, u32[]{:S(2)}) %collective-permute-start) | collective-permute-done | bytes 786464 | tf_op jit(solution)/shard_map/ppermute | solution.py:71
  155.9 4.1 %convolution_bitcast_fusion = f32[768,192]{0,1:T(8,128)} fusion(bf16[4,192,512]{2,1,0:T(8,128)(2,1)} %gather_fusion.1, bf16[1,768,512]{2,1,0:T(8,128)(2,1)} %bitcast.7, bf16[1,768,512]{2,1,0:T(8,128)(2,1)} %bitcast.6, bf16[1,768,512]{2,1,0:T(8,128)(2,1)} %bitcast.5, bf16[1,768,512]{2,1,0:T(8,128)(2,1)} %stack_reshape.3), kind=kOutput, calls=%fused_computation.10 | convolution fusion | flops 608698368 | bytes 4521984 | tf_op jit(solution)/shard_map/dot_general | solution.py:135
  160.0 4.1 %collective-permute-start.4 = (f32[768,192]{0,1:T(8,128)}, f32[768,192]{0,1:T(8,128)}, u32[]{:S(2)}, u32[]{:S(2)}) collective-permute-start(f32[768,192]{0,1:T(8,128)} %convolution_bitcast_fusion), channel_id=1, source_target_pairs={{0,4},{4,0},{1,5},{5,1},{2,6},{6,2},{3,7},{7,3},{8,12},{12,8},{9,1... | collective-permute-start | bytes 1769480 | tf_op jit(solution)/shard_map/ppermute | solution.py:138
  165.4 3.3 %gather_fusion.3 = bf16[64,96,128]{2,1,0:T(8,128)(2,1)} fusion(bf16[64,96,128]{2,1,0:T(8,128)(2,1)} %slice.58, s32[1024]{0:T(1024)S(1)} %pad_clamp_fusion), kind=kCustom, calls=%fused_computation.3 | custom fusion | bytes 3145984 | tf_op jit(solution)/shard_map/jit(_take)/gather | solution.py:124
  168.8 25.7 %all-to-all-start.1 = ((bf16[64,96,128]{2,1,0:T(8,128)(2,1)}), bf16[64,96,128]{2,1,0:T(8,128)(2,1)S(1)}, u32[]{:S(2)}, u32[]{:S(2)}) async-start(bf16[64,96,128]{2,1,0:T(8,128)(2,1)} %gather_fusion.3), calls=%async_computation.1 | async-start | bytes 3145728 | tf_op jit(solution)/shard_map/all_to_all | solution.py:125
  196.2 3.3 %fusion = f32[768,192]{0,1:T(8,128)S(1)} fusion(f32[768,192]{0,1:T(8,128)} %collective-permute-done.4, bf16[4,192,512]{2,1,0:T(8,128)(2,1)} %gather_fusion, bf16[1,768,512]{2,1,0:T(8,128)(2,1)} %bitcast.7, bf16[1,768,512]{2,1,0:T(8,128)(2,1)} %bitcast.6, bf16[1,768,512]{2,1,0:T(8,128)(2,1)} %bitcast.5, bf16[1,768,512]{2,1,0:T(8,128)(2,1)S(1)} %copy-done.12), kind=kOutput, calls=%fused_computation.12 | convolution fusion | flops 608845824 | bytes 5111808 | tf_op jit(solution)/shard_map/dot_general | solution.py:132
  200.2 1.9 collective-permute-start.5
  204.3 5.5 %collective-permute-start.10 = (bf16[768,96]{0,1:T(8,128)(2,1)S(1)}, bf16[768,96]{0,1:T(8,128)(2,1)S(1)}, u32[]{:S(2)}, u32[]{:S(2)}) collective-permute-start(bf16[768,96]{0,1:T(8,128)(2,1)S(1)} %get-tuple-element.9), channel_id=1, source_target_pairs={{0,6},{1,7},{2,0},{3,1},{4,2},{5,3},{6,4},{7,5},{8,14},{9,15},{10,... | collective-permute-start | bytes 442376 | tf_op jit(solution)/shard_map/ppermute | solution.py:71
  209.9 4.8 %collective-permute-start.9 = (bf16[768,96]{0,1:T(8,128)(2,1)S(1)}, bf16[768,96]{0,1:T(8,128)(2,1)S(1)}, u32[]{:S(2)}, u32[]{:S(2)}) collective-permute-start(bf16[768,96]{0,1:T(8,128)(2,1)S(1)} %get-tuple-element.9), channel_id=1, source_target_pairs={{0,5},{1,6},{2,7},{3,0},{4,1},{5,2},{6,3},{7,4},{8,13},{9,14},{10,... | collective-permute-start | bytes 442376 | tf_op jit(solution)/shard_map/ppermute | solution.py:71
  214.7 1.9 collective-permute-start.8
  216.7 2.2 collective-permute-start.7
  218.9 15.8 %collective-permute-done.5 = bf16[768,96]{0,1:T(8,128)(2,1)} collective-permute-done((bf16[768,96]{0,1:T(8,128)(2,1)S(1)}, bf16[768,96]{0,1:T(8,128)(2,1)}, u32[]{:S(2)}, u32[]{:S(2)}) %collective-permute-start.5) | collective-permute-done | bytes 147488 | tf_op jit(solution)/shard_map/ppermute | solution.py:71
  238.2 6.6 %collective-permute-done.6 = bf16[768,96]{0,1:T(8,128)(2,1)S(1)} collective-permute-done((bf16[768,96]{0,1:T(8,128)(2,1)S(1)}, bf16[768,96]{0,1:T(8,128)(2,1)S(1)}, u32[]{:S(2)}, u32[]{:S(2)}) %collective-permute-start.6) | collective-permute-done | bytes 147488 | tf_op jit(solution)/shard_map/ppermute | solution.py:71
  244.8 1.9 collective-permute-start.11
  252.4 3.0 bitcast_convert_fusion
  258.3 11.1 %all-to-all-start.2 = ((bf16[64,96,128]{2,1,0:T(8,128)(2,1)}), bf16[64,96,128]{2,1,0:T(8,128)(2,1)S(1)}, u32[]{:S(2)}, u32[]{:S(2)}) async-start(bf16[64,96,128]{2,1,0:T(8,128)(2,1)} %pad_maximum_fusion.2), calls=%async_computation.2 | async-start | bytes 3145728 | tf_op jit(solution)/shard_map/all_to_all | solution.py:151
  274.0 37.3 %all-to-all-done.2 = bf16[64,96,128]{2,1,0:T(8,128)(2,1)S(1)} async-done(((bf16[64,96,128]{2,1,0:T(8,128)(2,1)}), bf16[64,96,128]{2,1,0:T(8,128)(2,1)S(1)}, u32[]{:S(2)}, u32[]{:S(2)}) %all-to-all-start.2) | async-done | bytes 1572896 | tf_op jit(solution)/shard_map/all_to_all | solution.py:151
  (97 shorter events, 40.2 us)
Async XLA Ops:
  0.6 5.9 %copy-start = (bf16[48,512]{1,0:T(8,128)(2,1)S(1)}, bf16[48,512]{1,0:T(8,128)(2,1)}, u32[]{:S(2)}) copy-start(bf16[48,512]{1,0:T(8,128)(2,1)} %param.8) | copy-start | bytes 147460
  3.2 4.2 %copy-start.2 = (bf16[1,96,4096]{2,1,0:T(8,128)(2,1)S(1)}, bf16[1,96,4096]{2,1,0:T(8,128)(2,1)}, u32[]{:S(2)}) copy-start(bf16[1,96,4096]{2,1,0:T(8,128)(2,1)} %param.14) | copy-start | bytes 2359300
  6.9 1.5 copy-start.1
  7.4 2.1 copy-start.3
  9.5 1.1 copy-start.6
  9.7 1.2 copy-start.7
  19.1 92.2 %all-to-all-start = ((bf16[64,192,128]{2,1,0:T(8,128)(2,1)}), bf16[64,192,128]{2,1,0:T(8,128)(2,1)S(1)}, u32[]{:S(2)}, u32[]{:S(2)}) async-start(bf16[64,192,128]{2,1,0:T(8,128)(2,1)} %pad_maximum_fusion), calls=%async_computation | async-start | bytes 6291456 | tf_op jit(solution)/shard_map/all_to_all | solution.py:114
  52.7 73.4 %collective-permute-start.3 = (bf16[192,2048]{1,0:T(8,128)(2,1)}, bf16[192,2048]{1,0:T(8,128)(2,1)}, u32[]{:S(2)}, u32[]{:S(2)}) collective-permute-start(bf16[192,2048]{1,0:T(8,128)(2,1)} %pad_maximum_fusion.4), channel_id=1, source_target_pairs={{0,4},{4,0},{1,5},{5,1},{2,6},{6,2},{3,7},{7,3},{8,12},{12,8},{9,1... | collective-permute-start | bytes 2359304 | tf_op jit(solution)/shard_map/ppermute | solution.py:106
  114.7 35.5 %collective-permute-start.2 = (bf16[768,512]{1,0:T(8,128)(2,1)}, bf16[768,512]{1,0:T(8,128)(2,1)}, u32[]{:S(2)}, u32[]{:S(2)}) collective-permute-start(bf16[768,512]{1,0:T(8,128)(2,1)} %reshape.157), channel_id=1, source_target_pairs={{0,3},{1,0},{2,1},{3,2},{4,7},{5,4},{6,5},{7,6},{8,11},{9,8},{10,9... | collective-permute-start | bytes 2359304 | tf_op jit(solution)/shard_map/ppermute | solution.py:71
  118.5 31.8 %collective-permute-start.1 = (bf16[768,512]{1,0:T(8,128)(2,1)}, bf16[768,512]{1,0:T(8,128)(2,1)}, u32[]{:S(2)}, u32[]{:S(2)}) collective-permute-start(bf16[768,512]{1,0:T(8,128)(2,1)} %reshape.157), channel_id=1, source_target_pairs={{0,2},{1,3},{2,0},{3,1},{4,6},{5,7},{6,4},{7,5},{8,10},{9,11},{10,... | collective-permute-start | bytes 2359304 | tf_op jit(solution)/shard_map/ppermute | solution.py:71
  121.5 34.4 %collective-permute-start = (bf16[768,512]{1,0:T(8,128)(2,1)}, bf16[768,512]{1,0:T(8,128)(2,1)}, u32[]{:S(2)}, u32[]{:S(2)}) collective-permute-start(bf16[768,512]{1,0:T(8,128)(2,1)} %reshape.157), channel_id=1, source_target_pairs={{0,1},{1,2},{2,3},{3,0},{4,5},{5,6},{6,7},{7,4},{8,9},{9,10},{10,1... | collective-permute-start | bytes 2359304 | tf_op jit(solution)/shard_map/ppermute | solution.py:71
  155.9 8.3 %copy-start.14 = (s32[64]{0:T(128)S(1)}, s32[64]{0:T(128)}, u32[]{:S(2)}) copy-start(s32[64]{0:T(128)} %param.11) | copy-start | bytes 772
  160.0 36.1 %collective-permute-start.4 = (f32[768,192]{0,1:T(8,128)}, f32[768,192]{0,1:T(8,128)}, u32[]{:S(2)}, u32[]{:S(2)}) collective-permute-start(f32[768,192]{0,1:T(8,128)} %convolution_bitcast_fusion), channel_id=1, source_target_pairs={{0,4},{4,0},{1,5},{5,1},{2,6},{6,2},{3,7},{7,3},{8,12},{12,8},{9,1... | collective-permute-start | bytes 1769480 | tf_op jit(solution)/shard_map/ppermute | solution.py:138
  168.8 25.8 %copy-start.10 = (bf16[96,2048]{1,0:T(8,128)(2,1)S(1)}, bf16[96,2048]{1,0:T(8,128)(2,1)}, u32[]{:S(2)}) copy-start(bf16[96,2048]{1,0:T(8,128)(2,1)} %get-tuple-element.18) | copy-start | bytes 1179652
  168.8 25.8 %copy-start.9 = (bf16[96,2048]{1,0:T(8,128)(2,1)S(1)}, bf16[96,2048]{1,0:T(8,128)(2,1)}, u32[]{:S(2)}) copy-start(bf16[96,2048]{1,0:T(8,128)(2,1)} %get-tuple-element.23) | copy-start | bytes 1179652
  168.8 86.6 %all-to-all-start.1 = ((bf16[64,96,128]{2,1,0:T(8,128)(2,1)}), bf16[64,96,128]{2,1,0:T(8,128)(2,1)S(1)}, u32[]{:S(2)}, u32[]{:S(2)}) async-start(bf16[64,96,128]{2,1,0:T(8,128)(2,1)} %gather_fusion.3), calls=%async_computation.1 | async-start | bytes 3145728 | tf_op jit(solution)/shard_map/all_to_all | solution.py:125
  194.6 1.6 copy-start.12
  196.2 6.0 %copy-start.4 = (bf16[1,768,512]{2,1,0:T(8,128)(2,1)S(1)}, bf16[1,768,512]{2,1,0:T(8,128)(2,1)}, u32[]{:S(2)}) copy-start(bf16[1,768,512]{2,1,0:T(8,128)(2,1)} %param.15) | copy-start | bytes 2359300
  199.4 4.2 %copy-start.5 = (bf16[64,48,128]{2,1,0:T(8,128)(2,1)S(1)}, bf16[64,48,128]{2,1,0:T(8,128)(2,1)}, u32[]{:S(2)}) copy-start(bf16[64,48,128]{2,1,0:T(8,128)(2,1)} %get-tuple-element.11) | copy-start | bytes 2359300
  200.2 34.5 %collective-permute-start.5 = (bf16[768,96]{0,1:T(8,128)(2,1)S(1)}, bf16[768,96]{0,1:T(8,128)(2,1)}, u32[]{:S(2)}, u32[]{:S(2)}) collective-permute-start(bf16[768,96]{0,1:T(8,128)(2,1)S(1)} %get-tuple-element.9), channel_id=1, source_target_pairs={{0,1},{1,2},{2,3},{3,4},{4,5},{5,6},{6,7},{7,0},{8,9},{9,10},{10,1... | collective-permute-start | bytes 442376 | tf_op jit(solution)/shard_map/ppermute | solution.py:71
  204.3 48.1 %copy-start.11 = (bf16[8,96,512]{2,1,0:T(8,128)(2,1)S(1)}, bf16[8,96,512]{2,1,0:T(8,128)(2,1)}, u32[]{:S(2)}) copy-start(bf16[8,96,512]{2,1,0:T(8,128)(2,1)} %gather_fusion.2) | copy-start | bytes 2359300
  204.3 45.0 %collective-permute-start.10 = (bf16[768,96]{0,1:T(8,128)(2,1)S(1)}, bf16[768,96]{0,1:T(8,128)(2,1)S(1)}, u32[]{:S(2)}, u32[]{:S(2)}) collective-permute-start(bf16[768,96]{0,1:T(8,128)(2,1)S(1)} %get-tuple-element.9), channel_id=1, source_target_pairs={{0,6},{1,7},{2,0},{3,1},{4,2},{5,3},{6,4},{7,5},{8,14},{9,15},{10,... | collective-permute-start | bytes 442376 | tf_op jit(solution)/shard_map/ppermute | solution.py:71
  209.9 38.8 %collective-permute-start.9 = (bf16[768,96]{0,1:T(8,128)(2,1)S(1)}, bf16[768,96]{0,1:T(8,128)(2,1)S(1)}, u32[]{:S(2)}, u32[]{:S(2)}) collective-permute-start(bf16[768,96]{0,1:T(8,128)(2,1)S(1)} %get-tuple-element.9), channel_id=1, source_target_pairs={{0,5},{1,6},{2,7},{3,0},{4,1},{5,2},{6,3},{7,4},{8,13},{9,14},{10,... | collective-permute-start | bytes 442376 | tf_op jit(solution)/shard_map/ppermute | solution.py:71
  214.7 33.3 %collective-permute-start.8 = (bf16[768,96]{0,1:T(8,128)(2,1)S(1)}, bf16[768,96]{0,1:T(8,128)(2,1)S(1)}, u32[]{:S(2)}, u32[]{:S(2)}) collective-permute-start(bf16[768,96]{0,1:T(8,128)(2,1)S(1)} %get-tuple-element.9), channel_id=1, source_target_pairs={{0,4},{1,5},{2,6},{3,7},{4,0},{5,1},{6,2},{7,3},{8,12},{9,13},{10,... | collective-permute-start | bytes 442376 | tf_op jit(solution)/shard_map/ppermute | solution.py:71
  216.7 30.7 %collective-permute-start.7 = (bf16[768,96]{0,1:T(8,128)(2,1)S(1)}, bf16[768,96]{0,1:T(8,128)(2,1)S(1)}, u32[]{:S(2)}, u32[]{:S(2)}) collective-permute-start(bf16[768,96]{0,1:T(8,128)(2,1)S(1)} %get-tuple-element.9), channel_id=1, source_target_pairs={{0,3},{1,4},{2,5},{3,6},{4,7},{5,0},{6,1},{7,2},{8,11},{9,12},{10,... | collective-permute-start | bytes 442376 | tf_op jit(solution)/shard_map/ppermute | solution.py:71
  234.7 10.1 %collective-permute-start.6 = (bf16[768,96]{0,1:T(8,128)(2,1)S(1)}, bf16[768,96]{0,1:T(8,128)(2,1)S(1)}, u32[]{:S(2)}, u32[]{:S(2)}) collective-permute-start(bf16[768,96]{0,1:T(8,128)(2,1)S(1)} %get-tuple-element.9), channel_id=1, source_target_pairs={{0,2},{1,3},{2,4},{3,5},{4,6},{5,7},{6,0},{7,1},{8,10},{9,11},{10,... | collective-permute-start | bytes 442376 | tf_op jit(solution)/shard_map/ppermute | solution.py:71
  244.8 7.0 %collective-permute-start.11 = (bf16[768,96]{0,1:T(8,128)(2,1)S(1)}, bf16[768,96]{0,1:T(8,128)(2,1)S(1)}, u32[]{:S(2)}, u32[]{:S(2)}) collective-permute-start(bf16[768,96]{0,1:T(8,128)(2,1)S(1)} %get-tuple-element.9), channel_id=1, source_target_pairs={{0,7},{1,0},{2,1},{3,2},{4,3},{5,4},{6,5},{7,6},{8,15},{9,8},{10,9... | collective-permute-start | bytes 442376 | tf_op jit(solution)/shard_map/ppermute | solution.py:71
  258.3 11.1 %copy-start.13 = (bf16[48,8]{0,1:T(8,128)(2,1)S(1)}, bf16[48,8]{0,1:T(8,128)(2,1)}, u32[]{:S(2)}) copy-start(bf16[48,8]{0,1:T(8,128)(2,1)} %param.10) | copy-start | bytes 2308
  258.3 53.0 %all-to-all-start.2 = ((bf16[64,96,128]{2,1,0:T(8,128)(2,1)}), bf16[64,96,128]{2,1,0:T(8,128)(2,1)S(1)}, u32[]{:S(2)}, u32[]{:S(2)}) async-start(bf16[64,96,128]{2,1,0:T(8,128)(2,1)} %pad_maximum_fusion.2), calls=%async_computation.2 | async-start | bytes 3145728 | tf_op jit(solution)/shard_map/all_to_all | solution.py:151
  270.9 1.5 copy-start.8

commit v14 on v7

--- a/solution.py
+++ b/solution.py
@@ -128,13 +128,14 @@
     taken3 = jnp.take(
         taken.reshape(taken.shape[0], columns, narrow_width), sources, axis=1, mode="clip"
     )
-    own_part = lax.dot_general(
-        pieces, keep3, (((0, 2), (1, 2)), ((), ())), preferred_element_type=jnp.float32
-    )
     other_part = lax.dot_general(
         pieces, taken3, (((0, 2), (1, 2)), ((), ())), preferred_element_type=jnp.float32
     )
     back = lax.ppermute(other_part, "zlo", pair)
+    pieces, keep3, other_part = lax.optimization_barrier((pieces, keep3, other_part))
+    own_part = lax.dot_general(
+        pieces, keep3, (((0, 2), (1, 2)), ((), ())), preferred_element_type=jnp.float32
+    )
     sums = own_part + back
     gate_sum = sums[:, :rows]
     up_sum = sums[:, rows:]

time: 299 us -> 311 us (1.040)
  waiting for transfers between devices: 127 us -> 144 us
  starting transfers between devices: 97.1 us -> 93 us
    ppermute x1, waiting for transfers between devices: 0.01 us -> 43.1 us  [body(): taken = lax.ppermute(give, 'zlo', pair)]
    ppermute x1, waiting for transfers between devices: 49.8 us -> 7.5 us  [body(): back = lax.ppermute(other_part, 'zlo', pair)]
    all_to_all x1, waiting for transfers between devices: 54.1 us -> 68.2 us  [body(): lax.all_to_all(jnp.concatenate([token_lanes, packed], axis=1), 'expert',...]
  transfers between devices with their start and end apart: 15 -> 15, of which waited for: 3 -> 5; matrix products, arithmetic and copies ran while one was open for 20% -> 16% of each run, Pallas kernels for 0% -> 0%
where the time goes in v14:
time: 311 us; the launch traced here: 310 us
  waiting for transfers between devices  144 us (46%)
  starting transfers between devices  93 us (30%)
  local copies, waits for them, and re-layouts  51.1 us (16%)
  other arithmetic  12.4 us (4%)
  matrix products  8.48 us (3%)
    all_to_all x1, waiting for transfers between devices, body(): lax.all_to_all(jnp.concatenate([token_lanes, packed], axis=1), 'expert',...  68.2 us
    ppermute x1, waiting for transfers between devices, body(): taken = lax.ppermute(give, 'zlo', pair)  43.1 us
    ppermute x10, starting transfers between devices, ring_gather(): lax.ppermute(value, axis, [(i, (i + shift) % size) for i in range(size)])  35.9 us
    all_to_all x1, waiting for transfers between devices, body(): lax.all_to_all(produced.reshape(groups, capacity, -1), 'expert', split_ax...  23.9 us
    all_to_all x1, starting transfers between devices, body(): lax.all_to_all(ordered, 'expert', split_axis=0, concat_axis=0, tiled=True)  20.1 us
    all_to_all x1, starting transfers between devices, body(): lax.all_to_all(jnp.concatenate([token_lanes, packed], axis=1), 'expert',...  16.5 us
    all_to_all x1, starting transfers between devices, body(): lax.all_to_all(produced.reshape(groups, capacity, -1), 'expert', split_ax...  14.3 us
    dynamic_slice x1, local copies, waits for them, and re-layouts, body(): lax.dynamic_index_in_dim(up_halves, 1 - half, axis=1, keepdims=False)  9.36 us
  transfers between devices with their start and end apart: 15, of which 5 were waited for; matrix products, arithmetic and copies ran while one was open for 16% of the time, Pallas kernels for 0%

profile of v14, /device:TPU:16, one launch (start us, length us, event | category | flops | bytes accessed | tf_op | source)
XLA Modules:
  0.0 309.9 jit_solution(15303067126628796753)
XLA Ops:
  1.6 1.6 select_reduce_fusion
  6.0 1.8 reshape_squeeze.20
  13.5 2.1 pad_maximum_fusion
  15.6 16.5 %all-to-all-start = ((bf16[64,192,128]{2,1,0:T(8,128)(2,1)}), bf16[64,192,128]{2,1,0:T(8,128)(2,1)S(1)}, u32[]{:S(2)}, u32[]{:S(2)}) async-start(bf16[64,192,128]{2,1,0:T(8,128)(2,1)} %pad_maximum_fusion), calls=%async_computation | async-start | bytes 6291456 | tf_op jit(solution)/shard_map/all_to_all | solution.py:114
  32.1 3.3 %reshape_squeeze.22 = bf16[96,2,2048]{2,1,0:T(2,128)(2,1)} reshape(bf16[1,96,4096]{2,1,0:T(8,128)(2,1)} %param.14) | data formatting | bytes 1572864 | tf_op jit(solution)/shard_map/reshape;squeeze | solution.py:92
  35.3 3.2 %reshape_squeeze.21 = bf16[96,2,2048]{2,1,0:T(2,128)(2,1)} reshape(bf16[1,96,4096]{2,1,0:T(8,128)(2,1)} %param.13) | data formatting | bytes 1572864 | tf_op jit(solution)/shard_map/reshape;squeeze | solution.py:91
  38.6 68.2 %all-to-all-done = bf16[64,192,128]{2,1,0:T(8,128)(2,1)S(1)} async-done(((bf16[64,192,128]{2,1,0:T(8,128)(2,1)}), bf16[64,192,128]{2,1,0:T(8,128)(2,1)S(1)}, u32[]{:S(2)}, u32[]{:S(2)}) %all-to-all-start) | async-done | bytes 3145760 | tf_op jit(solution)/shard_map/all_to_all | solution.py:114
  108.4 3.9 %gather_fusion.3 = bf16[64,144,128]{2,1,0:T(8,128)(2,1)} fusion(bf16[64,144,128]{2,1,0:T(8,128)(2,1)} %slice.48, s32[1024]{0:T(1024)S(1)} %pad_clamp_fusion), kind=kCustom, calls=%fused_computation.3 | custom fusion | bytes 4718848 | tf_op jit(solution)/shard_map/jit(_take)/gather | solution.py:123
  112.3 20.1 %all-to-all-start.1 = ((bf16[64,144,128]{2,1,0:T(8,128)(2,1)}), bf16[64,144,128]{2,1,0:T(8,128)(2,1)}, u32[]{:S(2)}, u32[]{:S(2)}) async-start(bf16[64,144,128]{2,1,0:T(8,128)(2,1)} %gather_fusion.3), calls=%async_computation.1 | async-start | bytes 4718592 | tf_op jit(solution)/shard_map/all_to_all | solution.py:124
  132.4 9.4 %constant_dynamic-slice_fusion = (bf16[96,1,2048]{2,1,0:T(2,128)(2,1)S(1)}, bf16[96,2048]{1,0:T(8,128)(2,1)}, bf16[96,2048]{1,0:T(8,128)(2,1)}, bf16[96,1,2048]{2,1,0:T(2,128)(2,1)S(1)}) fusion(bf16[96,2,2048]{2,1,0:T(2,128)(2,1)} %reshape_squeeze.22, s32[]{:T(128)S(6)} %select_n.43, s32[]{:T(128)S(6)} %select_n.41, bf16[96,2,2048]{2,1,0:T(2,128)(2,1)} %reshape_squeeze.21), kind=kLoop, calls=%fused_computation.57 | loop fusion | bytes 3145736 | tf_op jit(solution)/shard_map/jit(dynamic_index_in_dim)/dynamic_slice | solution.py:103
  143.2 1.9 collective-permute-start.3
  146.0 2.3 reshape.168
  148.4 5.2 %collective-permute-start.2 = (bf16[768,512]{1,0:T(8,128)(2,1)}, bf16[768,512]{1,0:T(8,128)(2,1)S(1)}, u32[]{:S(2)}, u32[]{:S(2)}) collective-permute-start(bf16[768,512]{1,0:T(8,128)(2,1)} %reshape.168), channel_id=1, source_target_pairs={{0,3},{1,0},{2,1},{3,2},{4,7},{5,4},{6,5},{7,6},{8,11},{9,8},{10,9... | collective-permute-start | bytes 2359304 | tf_op jit(solution)/shard_map/ppermute | solution.py:72
  153.6 2.9 collective-permute-start.1
  156.5 2.2 collective-permute-start
  158.7 43.1 %collective-permute-done.3 = bf16[192,2048]{1,0:T(8,128)(2,1)} collective-permute-done((bf16[192,2048]{1,0:T(8,128)(2,1)}, bf16[192,2048]{1,0:T(8,128)(2,1)}, u32[]{:S(2)}, u32[]{:S(2)}) %collective-permute-start.3) | collective-permute-done | bytes 786464 | tf_op jit(solution)/shard_map/ppermute | solution.py:107
  206.5 2.0 convolution_bitcast_fusion.1
  208.5 4.4 %collective-permute-start.4 = (f32[768,192]{0,1:T(8,128)}, f32[768,192]{0,1:T(8,128)}, u32[]{:S(2)}, u32[]{:S(2)}) collective-permute-start(f32[768,192]{0,1:T(8,128)} %convolution_bitcast_fusion.1), channel_id=1, source_target_pairs={{0,4},{4,0},{1,5},{5,1},{2,6},{6,2},{3,7},{7,3},{8,12},{12,8},{9,1... | collective-permute-start | bytes 1769480 | tf_op jit(solution)/shard_map/ppermute | solution.py:134
  214.0 2.9 gather_fusion
  216.8 2.3 convolution_bitcast_fusion
  219.1 7.5 %collective-permute-done.4 = f32[768,192]{0,1:T(8,128)} collective-permute-done((f32[768,192]{0,1:T(8,128)}, f32[768,192]{0,1:T(8,128)}, u32[]{:S(2)}, u32[]{:S(2)}) %collective-permute-start.4) | collective-permute-done | bytes 589856 | tf_op jit(solution)/shard_map/ppermute | solution.py:134
  228.5 4.2 %collective-permute-start.5 = (bf16[768,96]{0,1:T(8,128)(2,1)S(1)}, bf16[768,96]{0,1:T(8,128)(2,1)S(1)}, u32[]{:S(2)}, u32[]{:S(2)}) collective-permute-start(bf16[768,96]{0,1:T(8,128)(2,1)S(1)} %get-tuple-element.13), channel_id=1, source_target_pairs={{0,1},{1,2},{2,3},{3,4},{4,5},{5,6},{6,7},{7,0},{8,9},{9,10},{10,1... | collective-permute-start | bytes 442376 | tf_op jit(solution)/shard_map/ppermute | solution.py:72
  233.4 4.4 %collective-permute-start.6 = (bf16[768,96]{0,1:T(8,128)(2,1)S(1)}, bf16[768,96]{0,1:T(8,128)(2,1)S(1)}, u32[]{:S(2)}, u32[]{:S(2)}) collective-permute-start(bf16[768,96]{0,1:T(8,128)(2,1)S(1)} %get-tuple-element.13), channel_id=1, source_target_pairs={{0,2},{1,3},{2,4},{3,5},{4,6},{5,7},{6,0},{7,1},{8,10},{9,11},{10,... | collective-permute-start | bytes 442376 | tf_op jit(solution)/shard_map/ppermute | solution.py:72
  237.8 4.4 %collective-permute-start.7 = (bf16[768,96]{0,1:T(8,128)(2,1)S(1)}, bf16[768,96]{0,1:T(8,128)(2,1)S(1)}, u32[]{:S(2)}, u32[]{:S(2)}) collective-permute-start(bf16[768,96]{0,1:T(8,128)(2,1)S(1)} %get-tuple-element.13), channel_id=1, source_target_pairs={{0,3},{1,4},{2,5},{3,6},{4,7},{5,0},{6,1},{7,2},{8,11},{9,12},{10,... | collective-permute-start | bytes 442376 | tf_op jit(solution)/shard_map/ppermute | solution.py:72
  242.2 2.2 collective-permute-start.8
  244.4 3.0 collective-permute-start.9
  247.5 4.6 %collective-permute-start.10 = (bf16[768,96]{0,1:T(8,128)(2,1)S(1)}, bf16[768,96]{0,1:T(8,128)(2,1)S(1)}, u32[]{:S(2)}, u32[]{:S(2)}) collective-permute-start(bf16[768,96]{0,1:T(8,128)(2,1)S(1)} %get-tuple-element.13), channel_id=1, source_target_pairs={{0,6},{1,7},{2,0},{3,1},{4,2},{5,3},{6,4},{7,5},{8,14},{9,15},{10,... | collective-permute-start | bytes 442376 | tf_op jit(solution)/shard_map/ppermute | solution.py:72
  252.8 2.8 collective-permute-start.11
  260.5 2.1 bitcast_convert_fusion
  263.7 14.3 %all-to-all-start.2 = ((bf16[64,12,512]{2,1,0:T(8,128)(2,1)}), bf16[64,12,512]{2,1,0:T(8,128)(2,1)S(1)}, u32[]{:S(2)}, u32[]{:S(2)}) async-start(bf16[64,12,512]{2,1,0:T(8,128)(2,1)} %reshape.170), calls=%async_computation.2 | async-start | bytes 2097152 | tf_op jit(solution)/shard_map/all_to_all | solution.py:150
  278.5 1.8 fusion.12
  284.9 23.9 %all-to-all-done.2 = bf16[64,12,512]{2,1,0:T(8,128)(2,1)S(1)} async-done(((bf16[64,12,512]{2,1,0:T(8,128)(2,1)}), bf16[64,12,512]{2,1,0:T(8,128)(2,1)S(1)}, u32[]{:S(2)}, u32[]{:S(2)}) %all-to-all-start.2) | async-done | bytes 786464 | tf_op jit(solution)/shard_map/all_to_all | solution.py:150
  (92 shorter events, 34.3 us)
Async XLA Ops:
  0.6 10.0 %copy-start = (bf16[48,512]{1,0:T(8,128)(2,1)S(1)}, bf16[48,512]{1,0:T(8,128)(2,1)}, u32[]{:S(2)}) copy-start(bf16[48,512]{1,0:T(8,128)(2,1)} %param.8) | copy-start | bytes 147460
  6.0 2.3 copy-start.4
  7.8 1.1 copy-start.5
  15.6 91.2 %all-to-all-start = ((bf16[64,192,128]{2,1,0:T(8,128)(2,1)}), bf16[64,192,128]{2,1,0:T(8,128)(2,1)S(1)}, u32[]{:S(2)}, u32[]{:S(2)}) async-start(bf16[64,192,128]{2,1,0:T(8,128)(2,1)} %pad_maximum_fusion), calls=%async_computation | async-start | bytes 6291456 | tf_op jit(solution)/shard_map/all_to_all | solution.py:114
  32.1 6.5 %copy-start.11 = (s32[64]{0:T(128)S(1)}, s32[64]{0:T(128)}, u32[]{:S(2)}) copy-start(s32[64]{0:T(128)} %param.11) | copy-start | bytes 772
  112.3 150.2 %all-to-all-start.1 = ((bf16[64,144,128]{2,1,0:T(8,128)(2,1)}), bf16[64,144,128]{2,1,0:T(8,128)(2,1)}, u32[]{:S(2)}, u32[]{:S(2)}) async-start(bf16[64,144,128]{2,1,0:T(8,128)(2,1)} %gather_fusion.3), calls=%async_computation.1 | async-start | bytes 4718592 | tf_op jit(solution)/shard_map/all_to_all | solution.py:124
  143.2 58.6 %collective-permute-start.3 = (bf16[192,2048]{1,0:T(8,128)(2,1)}, bf16[192,2048]{1,0:T(8,128)(2,1)}, u32[]{:S(2)}, u32[]{:S(2)}) collective-permute-start(bf16[192,2048]{1,0:T(8,128)(2,1)} %pad_maximum_fusion.4), channel_id=1, source_target_pairs={{0,4},{4,0},{1,5},{5,1},{2,6},{6,2},{3,7},{7,3},{8,12},{12,8},{9,1... | collective-permute-start | bytes 2359304 | tf_op jit(solution)/shard_map/ppermute | solution.py:107
  146.0 58.4 %copy-start.1 = (bf16[64,48,128]{2,1,0:T(8,128)(2,1)S(1)}, bf16[64,48,128]{2,1,0:T(8,128)(2,1)}, u32[]{:S(2)}) copy-start(bf16[64,48,128]{2,1,0:T(8,128)(2,1)} %slice.45) | copy-start | bytes 2359300
  148.4 56.6 %collective-permute-start.2 = (bf16[768,512]{1,0:T(8,128)(2,1)}, bf16[768,512]{1,0:T(8,128)(2,1)S(1)}, u32[]{:S(2)}, u32[]{:S(2)}) collective-permute-start(bf16[768,512]{1,0:T(8,128)(2,1)} %reshape.168), channel_id=1, source_target_pairs={{0,3},{1,0},{2,1},{3,2},{4,7},{5,4},{6,5},{7,6},{8,11},{9,8},{10,9... | collective-permute-start | bytes 2359304 | tf_op jit(solution)/shard_map/ppermute | solution.py:72
  153.6 51.4 %collective-permute-start.1 = (bf16[768,512]{1,0:T(8,128)(2,1)}, bf16[768,512]{1,0:T(8,128)(2,1)S(1)}, u32[]{:S(2)}, u32[]{:S(2)}) collective-permute-start(bf16[768,512]{1,0:T(8,128)(2,1)} %reshape.168), channel_id=1, source_target_pairs={{0,2},{1,3},{2,0},{3,1},{4,6},{5,7},{6,4},{7,5},{8,10},{9,11},{10,... | collective-permute-start | bytes 2359304 | tf_op jit(solution)/shard_map/ppermute | solution.py:72
  156.5 48.5 %collective-permute-start = (bf16[768,512]{1,0:T(8,128)(2,1)}, bf16[768,512]{1,0:T(8,128)(2,1)}, u32[]{:S(2)}, u32[]{:S(2)}) collective-permute-start(bf16[768,512]{1,0:T(8,128)(2,1)} %reshape.168), channel_id=1, source_target_pairs={{0,1},{1,2},{2,3},{3,0},{4,5},{5,6},{6,7},{7,4},{8,9},{9,10},{10,1... | collective-permute-start | bytes 2359304 | tf_op jit(solution)/shard_map/ppermute | solution.py:72
  205.0 1.5 copy-start.9
  206.5 6.5 %copy-start.2 = (bf16[4,768,512]{2,1,0:T(8,128)(2,1)}, bf16[4,768,512]{2,1,0:T(8,128)(2,1)S(1)}, u32[]{:S(2)}) copy-start(bf16[4,768,512]{2,1,0:T(8,128)(2,1)S(1)} %pad_maximum_fusion.1) | copy-start | bytes 9437188
  206.5 6.4 %copy-start.8 = (bf16[96,2048]{1,0:T(8,128)(2,1)S(1)}, bf16[96,2048]{1,0:T(8,128)(2,1)}, u32[]{:S(2)}) copy-start(bf16[96,2048]{1,0:T(8,128)(2,1)} %get-tuple-element.20) | copy-start | bytes 1179652
  206.5 6.5 %copy-start.7 = (bf16[96,2048]{1,0:T(8,128)(2,1)S(1)}, bf16[96,2048]{1,0:T(8,128)(2,1)}, u32[]{:S(2)}) copy-start(bf16[96,2048]{1,0:T(8,128)(2,1)} %get-tuple-element.21) | copy-start | bytes 1179652
  208.5 18.1 %collective-permute-start.4 = (f32[768,192]{0,1:T(8,128)}, f32[768,192]{0,1:T(8,128)}, u32[]{:S(2)}, u32[]{:S(2)}) collective-permute-start(f32[768,192]{0,1:T(8,128)} %convolution_bitcast_fusion.1), channel_id=1, source_target_pairs={{0,4},{4,0},{1,5},{5,1},{2,6},{6,2},{3,7},{7,3},{8,12},{12,8},{9,1... | collective-permute-start | bytes 1769480 | tf_op jit(solution)/shard_map/ppermute | solution.py:134
  213.0 3.8 %copy-start.3 = (bf16[4,768,512]{2,1,0:T(8,128)(2,1)S(1)}, bf16[4,768,512]{2,1,0:T(8,128)(2,1)}, u32[]{:S(2)}) copy-start(bf16[4,768,512]{2,1,0:T(8,128)(2,1)} %copy-done.2) | copy-start | bytes 9437188
  219.1 13.7 %copy-start.6 = (bf16[1,768,512]{2,1,0:T(8,128)(2,1)S(1)}, bf16[1,768,512]{2,1,0:T(8,128)(2,1)}, u32[]{:S(2)}) copy-start(bf16[1,768,512]{2,1,0:T(8,128)(2,1)} %param.15) | copy-start | bytes 2359300
  228.5 18.9 %collective-permute-start.5 = (bf16[768,96]{0,1:T(8,128)(2,1)S(1)}, bf16[768,96]{0,1:T(8,128)(2,1)S(1)}, u32[]{:S(2)}, u32[]{:S(2)}) collective-permute-start(bf16[768,96]{0,1:T(8,128)(2,1)S(1)} %get-tuple-element.13), channel_id=1, source_target_pairs={{0,1},{1,2},{2,3},{3,4},{4,5},{5,6},{6,7},{7,0},{8,9},{9,10},{10,1... | collective-permute-start | bytes 442376 | tf_op jit(solution)/shard_map/ppermute | solution.py:72
  233.4 19.4 %collective-permute-start.6 = (bf16[768,96]{0,1:T(8,128)(2,1)S(1)}, bf16[768,96]{0,1:T(8,128)(2,1)S(1)}, u32[]{:S(2)}, u32[]{:S(2)}) collective-permute-start(bf16[768,96]{0,1:T(8,128)(2,1)S(1)} %get-tuple-element.13), channel_id=1, source_target_pairs={{0,2},{1,3},{2,4},{3,5},{4,6},{5,7},{6,0},{7,1},{8,10},{9,11},{10,... | collective-permute-start | bytes 442376 | tf_op jit(solution)/shard_map/ppermute | solution.py:72
  237.8 18.4 %collective-permute-start.7 = (bf16[768,96]{0,1:T(8,128)(2,1)S(1)}, bf16[768,96]{0,1:T(8,128)(2,1)S(1)}, u32[]{:S(2)}, u32[]{:S(2)}) collective-permute-start(bf16[768,96]{0,1:T(8,128)(2,1)S(1)} %get-tuple-element.13), channel_id=1, source_target_pairs={{0,3},{1,4},{2,5},{3,6},{4,7},{5,0},{6,1},{7,2},{8,11},{9,12},{10,... | collective-permute-start | bytes 442376 | tf_op jit(solution)/shard_map/ppermute | solution.py:72
  242.2 14.7 %collective-permute-start.8 = (bf16[768,96]{0,1:T(8,128)(2,1)S(1)}, bf16[768,96]{0,1:T(8,128)(2,1)S(1)}, u32[]{:S(2)}, u32[]{:S(2)}) collective-permute-start(bf16[768,96]{0,1:T(8,128)(2,1)S(1)} %get-tuple-element.13), channel_id=1, source_target_pairs={{0,4},{1,5},{2,6},{3,7},{4,0},{5,1},{6,2},{7,3},{8,12},{9,13},{10,... | collective-permute-start | bytes 442376 | tf_op jit(solution)/shard_map/ppermute | solution.py:72
  244.4 13.1 %collective-permute-start.9 = (bf16[768,96]{0,1:T(8,128)(2,1)S(1)}, bf16[768,96]{0,1:T(8,128)(2,1)S(1)}, u32[]{:S(2)}, u32[]{:S(2)}) collective-permute-start(bf16[768,96]{0,1:T(8,128)(2,1)S(1)} %get-tuple-element.13), channel_id=1, source_target_pairs={{0,5},{1,6},{2,7},{3,0},{4,1},{5,2},{6,3},{7,4},{8,13},{9,14},{10,... | collective-permute-start | bytes 442376 | tf_op jit(solution)/shard_map/ppermute | solution.py:72
  247.5 10.8 %collective-permute-start.10 = (bf16[768,96]{0,1:T(8,128)(2,1)S(1)}, bf16[768,96]{0,1:T(8,128)(2,1)S(1)}, u32[]{:S(2)}, u32[]{:S(2)}) collective-permute-start(bf16[768,96]{0,1:T(8,128)(2,1)S(1)} %get-tuple-element.13), channel_id=1, source_target_pairs={{0,6},{1,7},{2,0},{3,1},{4,2},{5,3},{6,4},{7,5},{8,14},{9,15},{10,... | collective-permute-start | bytes 442376 | tf_op jit(solution)/shard_map/ppermute | solution.py:72
  252.8 7.0 %collective-permute-start.11 = (bf16[768,96]{0,1:T(8,128)(2,1)S(1)}, bf16[768,96]{0,1:T(8,128)(2,1)S(1)}, u32[]{:S(2)}, u32[]{:S(2)}) collective-permute-start(bf16[768,96]{0,1:T(8,128)(2,1)S(1)} %get-tuple-element.13), channel_id=1, source_target_pairs={{0,7},{1,0},{2,1},{3,2},{4,3},{5,4},{6,5},{7,6},{8,15},{9,8},{10,9... | collective-permute-start | bytes 442376 | tf_op jit(solution)/shard_map/ppermute | solution.py:72
  262.5 15.4 %copy-start.10 = (bf16[48,8]{0,1:T(8,128)(2,1)S(1)}, bf16[48,8]{0,1:T(8,128)(2,1)}, u32[]{:S(2)}) copy-start(bf16[48,8]{0,1:T(8,128)(2,1)} %param.10) | copy-start | bytes 2308
  263.7 45.1 %all-to-all-start.2 = ((bf16[64,12,512]{2,1,0:T(8,128)(2,1)}), bf16[64,12,512]{2,1,0:T(8,128)(2,1)S(1)}, u32[]{:S(2)}, u32[]{:S(2)}) async-start(bf16[64,12,512]{2,1,0:T(8,128)(2,1)} %reshape.170), calls=%async_computation.2 | async-start | bytes 2097152 | tf_op jit(solution)/shard_map/all_to_all | solution.py:150
